TPU v7x, 256 devices: a whole 4x4x8 slice. The times are simulated.
256 devices in a mesh: seq: 16 (over y, z_hi, core), head: 16 (over x, z_lo).
Axes of the slice: x: 4, y: 4, z: 8 (z_hi: 2, z_lo: 4; z = z_hi * 4 + z_lo), core: 2. Of those that a mesh axis runs over, the one named last changes fastest.
Arguments:
- x_in: bfloat16 [8192, 8192], P('seq', 'head'), may hold values from -6 to 6
- z_in: bfloat16 [8192, 8192], P('seq', 'head'), may hold values from -12 to 12
- bc: bfloat16 [2, 8192, 128], P(None, 'seq'), may hold values from -1.796875 to 1.796875
- dt_raw: float32 [128, 8192], P('head', 'seq'), may hold values from -3 to 3
- dt_bias: float32 [128], P('head'), may hold values from -8 to 0
- decay_rate: float32 [128], P('head'), may hold values from 0.001 to 0.4
- d_skip: float32 [128], P('head'), may hold values from 0.5 to 1.5
- norm_gain: float32 [8192], P('head'), may hold values from 0.1 to 1.9
- out_weight: bfloat16 [8192, 4096], P('head', 'seq'), may hold values from -0.0625 to 0.0625
- resid: bfloat16 [8192, 4096], P(('seq', 'head')), may hold values from -6 to 6
- mlp_gain: float32 [4096], replicated, may hold values from 0.1 to 1.9
- gate_weight: bfloat16 [4096, 8192], P(None, 'head'), may hold values from -0.09375 to 0.09375
- up_weight: bfloat16 [4096, 8192], P(None, 'head'), may hold values from -0.09375 to 0.09375
- down_weight: bfloat16 [8192, 4096], P('head', 'seq'), may hold values from -0.0625 to 0.0625
Outputs:
- layer_out: bfloat16 [8192, 4096], P(('seq', 'head'))
All inputs are finite; a program needn't handle non-finite values.
Results may differ from a plain program's by a relative error of at most 0.0075.
Values may be sent and summed in bfloat16 or wider, within the bound.
No kernel may reach another device: no remote copies, remote signals or barrier semaphores. Data moves between devices by JAX's collectives and lax.ppermute only.
A program may use at most 128 MiB of HBM per device.

v0:
```python
import jax
import jax.numpy as jnp
from jax import lax
from jax.sharding import PartitionSpec as P

BLOCK = 256
INNER = 8192


epsilon = 1e-05


def passed_along(value, axis, steps):
    count = lax.axis_size(axis)
    initial, last = (max(0, -steps), min(count, count - steps))
    return lax.ppermute(value, axis, [(source, source + steps) for source in range(initial, last)])


def block_scan(x_heads, b_rows, c_rows, step_size, log_decay, block_len, start_state):
    length, head_count, head_width = x_heads.shape
    state_size = b_rows.shape[1]
    block_count = length // block_len
    x_blocks = x_heads.reshape(block_count, block_len, head_count, head_width)
    b_blocks = b_rows.reshape(block_count, block_len, state_size)
    c_blocks = c_rows.reshape(block_count, block_len, state_size)
    d_blocks = step_size.reshape(head_count, block_count, block_len).transpose(1, 0, 2)
    a_blocks = log_decay.reshape(head_count, block_count, block_len).transpose(1, 0, 2)
    lower_mask = jnp.tril(jnp.ones((block_len, block_len), dtype=bool))

    def advance(carry_state, inputs):
        x_block, b_block, c_block, d_block, a_block = inputs
        cumulative = jnp.cumsum(a_block, axis=1)
        gap_values = jnp.where(
            lower_mask[None], cumulative[:, :, None] - cumulative[:, None, :], -jnp.inf
        )
        scores = jnp.dot(c_block, b_block.T, preferred_element_type=jnp.float32)
        mixing = (jnp.exp(gap_values) * scores[None] * d_block[:, None, :]).astype(jnp.bfloat16)
        within = jnp.einsum("hij,jhp->ihp", mixing, x_block, preferred_element_type=jnp.float32)
        carried = jnp.einsum(
            "in,hpn->ihp", c_block.astype(jnp.float32), carry_state, precision=lax.Precision.HIGHEST
        )
        carried = carried * jnp.exp(cumulative).T[:, :, None]
        last_cum = cumulative[:, -1:]
        inject = (
            (jnp.exp(last_cum - cumulative) * d_block)[:, :, None]
            * b_block.astype(jnp.float32)[None]
        ).astype(jnp.bfloat16)
        added = jnp.einsum("jhp,hjn->hpn", x_block, inject, preferred_element_type=jnp.float32)
        new_state = jnp.exp(last_cum)[:, :, None] * carry_state + added
        return (new_state, within + carried)

    final_state, block_outs = lax.scan(
        advance, start_state, (x_blocks, b_blocks, c_blocks, d_blocks, a_blocks)
    )
    return (block_outs.reshape(length, head_count, head_width), final_state)


def normalize_rows(layer_sum, mlp_gain):
    mean_square = jnp.mean(layer_sum * layer_sum, axis=1, keepdims=True)
    return (layer_sum * lax.rsqrt(mean_square + epsilon) * mlp_gain).astype(jnp.bfloat16)


def shards(
    x_in,
    z_in,
    bc,
    dt_raw,
    dt_bias,
    decay_rate,
    d_skip,
    norm_gain,
    out_weight,
    resid,
    mlp_gain,
    gate_weight,
    up_weight,
    down_weight,
):
    out_full, down_full = (
        lax.all_gather(out_weight, "seq", axis=1, tiled=True),
        lax.all_gather(down_weight, "seq", axis=1, tiled=True),
    )
    head_count = dt_raw.shape[0]
    length = dt_raw.shape[1]
    head_width = x_in.shape[1] // head_count
    state_size = bc.shape[2]
    step_size = jax.nn.softplus(dt_raw + dt_bias[:, None])
    log_decay = -decay_rate[:, None] * step_size
    x_heads = x_in.reshape(length, head_count, head_width)
    zero_state = jnp.zeros((head_count, head_width, state_size), jnp.float32)
    local_out, local_state = block_scan(
        x_heads, bc[0], bc[1], step_size, log_decay, BLOCK, zero_state
    )
    running = jnp.cumsum(log_decay, axis=1)
    group_decay = jnp.exp(running[:, -1])

    def relay_step(relay_turn, incoming):
        outgoing = group_decay[:, None, None] * incoming + local_state
        return passed_along(outgoing, "seq", 1)

    entering = lax.fori_loop(0, lax.axis_size("seq") - 1, relay_step, zero_state)
    carried = jnp.einsum(
        "tn,hpn->thp", bc[1].astype(jnp.float32), entering, precision=lax.Precision.HIGHEST
    )
    carried = carried * jnp.exp(running).T[:, :, None]
    ssd_out = local_out + carried + d_skip[None, :, None] * x_heads.astype(jnp.float32)
    gated_out = ssd_out.reshape(length, head_count * head_width) * jax.nn.silu(
        z_in.astype(jnp.float32)
    )
    row_squares = jnp.sum(gated_out * gated_out, axis=1)
    gated_scaled = (gated_out * norm_gain).astype(jnp.bfloat16)
    partial_value = jnp.dot(gated_scaled, out_full, preferred_element_type=jnp.float32)
    part_rows, part_squares = (
        lax.psum_scatter(partial_value, "head", scatter_dimension=0, tiled=True),
        lax.psum_scatter(row_squares, "head", scatter_dimension=0, tiled=True),
    )
    layer_sum = (
        resid.astype(jnp.float32) + part_rows * lax.rsqrt(part_squares / INNER + epsilon)[:, None]
    )
    normed = normalize_rows(layer_sum, mlp_gain)
    rows_piece = lax.all_gather(normed, "head", axis=0, tiled=True)
    gate_part = jnp.dot(rows_piece, gate_weight, preferred_element_type=jnp.float32)
    up_part = jnp.dot(rows_piece, up_weight, preferred_element_type=jnp.float32)
    hidden = (jax.nn.silu(gate_part) * up_part).astype(jnp.bfloat16)
    rows_piece = hidden
    mlp_rows = lax.psum_scatter(
        jnp.dot(rows_piece, down_full, preferred_element_type=jnp.float32),
        "head",
        scatter_dimension=0,
        tiled=True,
    )
    return (layer_sum + mlp_rows).astype(jnp.bfloat16)


def solution(mesh):
    in_specs = (
        P("seq", "head"),
        P("seq", "head"),
        P(None, "seq", None),
        P("head", "seq"),
        P("head"),
        P("head"),
        P("head"),
        P("head"),
        P("head", "seq"),
        P(("seq", "head"), None),
        P(),
        P(None, "head"),
        P(None, "head"),
        P("head", "seq"),
    )
    out_specs = P(("seq", "head"), None)
    return jax.shard_map(shards, mesh=mesh, in_specs=in_specs, out_specs=out_specs, check_vma=False)
```

profile of v0, /device:TPU:8, one launch (start us, length us, event | category | flops | bytes accessed | tf_op | source)
XLA Modules:
  0.0 856.5 jit_solution(15409193931064395106)
XLA Ops:
  8.6 1.6 reshape.124
  14.6 30.4 %while.24 = (s32[]{:T(128)}, f32[8,64,128]{2,1,0:T(8,128)S(1)}, f32[2,256,8,64]{1,0,3,2:T(2,128)}, f32[2,8,256]{2,1,0:T(8,128)S(1)}, bf16[2,256,8,64]{1,3,2,0:T(...) while((s32[]{:T(128)}, f32[8,64,128]{2,1,0:T(8,128)S(1)}, ...), condition=%wide.region_3.4_spmd.clone, body=%wide.region_0.3_spmd.clone.sunk | while | flops 322801696 | bytes 6293764 | solution.py:52
  18.3 11.5 %dynamic_update_slice.6 = f32[2,256,8,64]{1,0,3,2:T(2,128)} dynamic-update-slice(f32[2,256,8,64]{1,0,3,2:T(2,128)} %get-tuple-element.266, f32[1,256,8,64]{1,0,3,2:T(1,128)S(1)} %copy.49, s32[]{:T(128)S(6)} %copy.54, s32[]{:T(128)} %constant.46.clone.1..sunk, s32[]{:T(128)} %constant.46.clone.1..sunk, s32[]{:T(128)} %constant.46.clone.1..sunk) | dynamic-update-slice | bytes 1048580 | tf_op jit(solution)/shard_map/while/body/jit(dynamic_update_index_in_dim)/dynamic_update_slice | solution.py:52
  33.5 11.5 %dynamic_update_slice.6 = f32[2,256,8,64]{1,0,3,2:T(2,128)} dynamic-update-slice(f32[2,256,8,64]{1,0,3,2:T(2,128)} %get-tuple-element.266, f32[1,256,8,64]{1,0,3,2:T(1,128)S(1)} %copy.49, s32[]{:T(128)S(6)} %copy.54, s32[]{:T(128)} %constant.46.clone.1..sunk, s32[]{:T(128)} %constant.46.clone.1..sunk, s32[]{:T(128)} %constant.46.clone.1..sunk) | dynamic-update-slice | bytes 1048580 | tf_op jit(solution)/shard_map/while/body/jit(dynamic_update_index_in_dim)/dynamic_update_slice | solution.py:52
  45.0 2.1 reshape.115
  47.4 221.7 %while.23 = (s32[]{:T(128)}, f32[8,64,128]{2,1,0:T(8,128)S(1)}, f32[8]{0:T(128)S(1)}, f32[8,64,128]{2,1,0:T(8,128)S(1)}, s32[]{:T(128)}) while((s32[]{:T(128)}, f32[8,64,128]{2,1,0:T(8,128)S(1)}, f32[8]{0:T(128)S(1)}, f32[8,64,128]{2,1,0:T(8,128)S(1)}, s32[]{:T(128)}) %tuple.53), condition=%wide.region_7.8_spmd, body=%wide.region_6.7_spmd.sunk | while | flops 131074 | bytes 1835141 | solution.py:101
  47.5 2.1 collective-permute-start
  49.6 22.0 %collective-permute-done = f32[8,64,128]{2,1,0:T(8,128)S(1)} collective-permute-done((f32[8,64,128]{2,1,0:T(8,128)S(1)}, f32[8,64,128]{2,1,0:T(8,128)S(1)}, u32[]{:S(2)}, u32[]{:S(2)}) %collective-permute-start) | collective-permute-done | bytes 262176 | tf_op jit(solution)/shard_map/while/body/eval_jaxpr/ppermute | solution.py:16
  71.7 1.9 collective-permute-start
  73.7 13.0 %collective-permute-done = f32[8,64,128]{2,1,0:T(8,128)S(1)} collective-permute-done((f32[8,64,128]{2,1,0:T(8,128)S(1)}, f32[8,64,128]{2,1,0:T(8,128)S(1)}, u32[]{:S(2)}, u32[]{:S(2)}) %collective-permute-start) | collective-permute-done | bytes 262176 | tf_op jit(solution)/shard_map/while/body/eval_jaxpr/ppermute | solution.py:16
  86.8 1.9 collective-permute-start
  88.7 10.6 %collective-permute-done = f32[8,64,128]{2,1,0:T(8,128)S(1)} collective-permute-done((f32[8,64,128]{2,1,0:T(8,128)S(1)}, f32[8,64,128]{2,1,0:T(8,128)S(1)}, u32[]{:S(2)}, u32[]{:S(2)}) %collective-permute-start) | collective-permute-done | bytes 262176 | tf_op jit(solution)/shard_map/while/body/eval_jaxpr/ppermute | solution.py:16
  99.4 1.9 collective-permute-start
  101.3 10.6 %collective-permute-done = f32[8,64,128]{2,1,0:T(8,128)S(1)} collective-permute-done((f32[8,64,128]{2,1,0:T(8,128)S(1)}, f32[8,64,128]{2,1,0:T(8,128)S(1)}, u32[]{:S(2)}, u32[]{:S(2)}) %collective-permute-start) | collective-permute-done | bytes 262176 | tf_op jit(solution)/shard_map/while/body/eval_jaxpr/ppermute | solution.py:16
  112.0 1.9 collective-permute-start
  113.9 13.5 %collective-permute-done = f32[8,64,128]{2,1,0:T(8,128)S(1)} collective-permute-done((f32[8,64,128]{2,1,0:T(8,128)S(1)}, f32[8,64,128]{2,1,0:T(8,128)S(1)}, u32[]{:S(2)}, u32[]{:S(2)}) %collective-permute-start) | collective-permute-done | bytes 262176 | tf_op jit(solution)/shard_map/while/body/eval_jaxpr/ppermute | solution.py:16
  127.5 1.9 collective-permute-start
  129.4 12.3 %collective-permute-done = f32[8,64,128]{2,1,0:T(8,128)S(1)} collective-permute-done((f32[8,64,128]{2,1,0:T(8,128)S(1)}, f32[8,64,128]{2,1,0:T(8,128)S(1)}, u32[]{:S(2)}, u32[]{:S(2)}) %collective-permute-start) | collective-permute-done | bytes 262176 | tf_op jit(solution)/shard_map/while/body/eval_jaxpr/ppermute | solution.py:16
  141.8 1.9 collective-permute-start
  143.7 10.8 %collective-permute-done = f32[8,64,128]{2,1,0:T(8,128)S(1)} collective-permute-done((f32[8,64,128]{2,1,0:T(8,128)S(1)}, f32[8,64,128]{2,1,0:T(8,128)S(1)}, u32[]{:S(2)}, u32[]{:S(2)}) %collective-permute-start) | collective-permute-done | bytes 262176 | tf_op jit(solution)/shard_map/while/body/eval_jaxpr/ppermute | solution.py:16
  154.6 1.9 collective-permute-start
  156.5 11.7 %collective-permute-done = f32[8,64,128]{2,1,0:T(8,128)S(1)} collective-permute-done((f32[8,64,128]{2,1,0:T(8,128)S(1)}, f32[8,64,128]{2,1,0:T(8,128)S(1)}, u32[]{:S(2)}, u32[]{:S(2)}) %collective-permute-start) | collective-permute-done | bytes 262176 | tf_op jit(solution)/shard_map/while/body/eval_jaxpr/ppermute | solution.py:16
  168.3 1.9 collective-permute-start
  170.2 11.8 %collective-permute-done = f32[8,64,128]{2,1,0:T(8,128)S(1)} collective-permute-done((f32[8,64,128]{2,1,0:T(8,128)S(1)}, f32[8,64,128]{2,1,0:T(8,128)S(1)}, u32[]{:S(2)}, u32[]{:S(2)}) %collective-permute-start) | collective-permute-done | bytes 262176 | tf_op jit(solution)/shard_map/while/body/eval_jaxpr/ppermute | solution.py:16
  182.2 1.9 collective-permute-start
  184.1 12.5 %collective-permute-done = f32[8,64,128]{2,1,0:T(8,128)S(1)} collective-permute-done((f32[8,64,128]{2,1,0:T(8,128)S(1)}, f32[8,64,128]{2,1,0:T(8,128)S(1)}, u32[]{:S(2)}, u32[]{:S(2)}) %collective-permute-start) | collective-permute-done | bytes 262176 | tf_op jit(solution)/shard_map/while/body/eval_jaxpr/ppermute | solution.py:16
  196.7 1.9 collective-permute-start
  198.6 12.5 %collective-permute-done = f32[8,64,128]{2,1,0:T(8,128)S(1)} collective-permute-done((f32[8,64,128]{2,1,0:T(8,128)S(1)}, f32[8,64,128]{2,1,0:T(8,128)S(1)}, u32[]{:S(2)}, u32[]{:S(2)}) %collective-permute-start) | collective-permute-done | bytes 262176 | tf_op jit(solution)/shard_map/while/body/eval_jaxpr/ppermute | solution.py:16
  211.2 1.9 collective-permute-start
  213.1 12.5 %collective-permute-done = f32[8,64,128]{2,1,0:T(8,128)S(1)} collective-permute-done((f32[8,64,128]{2,1,0:T(8,128)S(1)}, f32[8,64,128]{2,1,0:T(8,128)S(1)}, u32[]{:S(2)}, u32[]{:S(2)}) %collective-permute-start) | collective-permute-done | bytes 262176 | tf_op jit(solution)/shard_map/while/body/eval_jaxpr/ppermute | solution.py:16
  225.7 1.9 collective-permute-start
  227.6 12.5 %collective-permute-done = f32[8,64,128]{2,1,0:T(8,128)S(1)} collective-permute-done((f32[8,64,128]{2,1,0:T(8,128)S(1)}, f32[8,64,128]{2,1,0:T(8,128)S(1)}, u32[]{:S(2)}, u32[]{:S(2)}) %collective-permute-start) | collective-permute-done | bytes 262176 | tf_op jit(solution)/shard_map/while/body/eval_jaxpr/ppermute | solution.py:16
  240.2 1.9 collective-permute-start
  242.1 12.5 %collective-permute-done = f32[8,64,128]{2,1,0:T(8,128)S(1)} collective-permute-done((f32[8,64,128]{2,1,0:T(8,128)S(1)}, f32[8,64,128]{2,1,0:T(8,128)S(1)}, u32[]{:S(2)}, u32[]{:S(2)}) %collective-permute-start) | collective-permute-done | bytes 262176 | tf_op jit(solution)/shard_map/while/body/eval_jaxpr/ppermute | solution.py:16
  254.7 1.9 collective-permute-start
  256.6 12.5 %collective-permute-done = f32[8,64,128]{2,1,0:T(8,128)S(1)} collective-permute-done((f32[8,64,128]{2,1,0:T(8,128)S(1)}, f32[8,64,128]{2,1,0:T(8,128)S(1)}, u32[]{:S(2)}, u32[]{:S(2)}) %collective-permute-start) | collective-permute-done | bytes 262176 | tf_op jit(solution)/shard_map/while/body/eval_jaxpr/ppermute | solution.py:16
  269.1 2.5 fusion.34
  271.6 1.6 copy.39
  273.2 7.8 fusion.41
  283.4 49.5 %all-reduce = f32[512]{0:T(512)S(1)} all-reduce(f32[512]{0:T(512)S(1)} %multiply_reduce_fusion), channel_id=3, replica_groups=mesh['seq'=16,'head'=16] {'head'}, use_global_device_ids=true, to_apply=%region_10.11.clone | all-reduce | flops 512 | bytes 4096
  333.0 139.6 %reduce-scatter.3.cloned.1.call-done = f32[32,4096]{1,0:T(8,128)} async-done(((f32[512,4096]{1,0:T(8,128)}), f32[32,4096]{1,0:T(8,128)}) %reduce-scatter.3.cloned.1.call-update) | async-done | bytes 524304 | tf_op jit(solution)/shard_map/reduce_scatter | solution.py:114
  474.0 1.9 multiply_convert_fusion.6
  476.7 99.1 %all-gather.6.cloned.1.call-done = bf16[512,4096]{1,0:T(8,128)(2,1)} async-done(((bf16[32,4096]{1,0:T(8,128)(2,1)}), bf16[512,4096]{1,0:T(8,128)(2,1)}) %all-gather.6.cloned.1.call-update) | async-done | bytes 4194320 | tf_op jit(solution)/shard_map/all_gather | solution.py:121
  575.8 5.8 fusion.52
  581.6 70.7 %all-gather.8.cloned.1.call-done = bf16[512,4096]{1,0:T(8,128)(2,1)} async-done(((bf16[512,256]{1,0:T(8,128)(2,1)}), bf16[512,4096]{1,0:T(8,128)(2,1)}) %all-gather.8.cloned.1.call-update) | async-done | bytes 4194320 | tf_op jit(solution)/shard_map/all_gather | solution.py:81
  652.3 12.5 %fusion.40 = f32[512,4096]{1,0:T(8,128)} fusion(bf16[512,4096]{1,0:T(8,128)(2,1)} %all-gather.8.cloned.1.call-done, bf16[512,4096]{1,0:T(8,128)(2,1)} %all-gather.6.cloned.1.call-done, bf16[4096,512]{1,0:T(8,128)(2,1)} %param.30, f32[512,512]{1,0:T(8,128)S(1)} %fusion.52), kind=kOutput, calls=%fused_computation.61 | convolution fusion | flops 4296540160 | bytes 22020096 | tf_op jit(solution)/shard_map/dot_general | solution.py:127
  664.8 183.2 %reduce-scatter.5.cloned.1.call-done = f32[32,4096]{1,0:T(8,128)} async-done(((f32[512,4096]{1,0:T(8,128)}), f32[32,4096]{1,0:T(8,128)}) %reduce-scatter.5.cloned.1.call-update) | async-done | bytes 524304 | tf_op jit(solution)/shard_map/reduce_scatter | solution.py:126
  848.0 1.9 add_convert_fusion
  (89 shorter events, 19.1 us)
Async XLA Ops:
  6.5 266.7 %all-gather.4.cloned.1.call-start = ((), (), s32[]{:S(2)}) async-start(), calls=%async_computation.2 | async-start | bytes 4456448 | tf_op jit(solution)/shard_map/all_gather | solution.py:80
  7.3 465.4 %reduce-scatter.3.cloned.1.call-start = ((), (), s32[]{:S(2)}) async-start(), calls=%async_computation.3 | async-start | bytes 8912896 | tf_op jit(solution)/shard_map/reduce_scatter | solution.py:114
  45.0 224.1 %copy-start.5 = (f32[8]{0:T(128)S(1)}, f32[8]{0:T(128)}, u32[]{:S(2)}) copy-start(f32[8]{0:T(128)} %param.24) | copy-start | bytes 100
  47.4 225.8 %copy-start.2 = (bf16[512,512]{1,0:T(8,128)(2,1)S(1)}, bf16[512,512]{1,0:T(8,128)(2,1)}, u32[]{:S(2)}) copy-start(bf16[512,512]{1,0:T(8,128)(2,1)} %param.19) | copy-start | bytes 1572868
  47.4 225.8 %copy-start.3 = (f32[512]{0:T(512)S(1)}, f32[512]{0:T(512)}, u32[]{:S(2)}) copy-start(f32[512]{0:T(512)} %param.25) | copy-start | bytes 6148
  47.5 24.1 %collective-permute-start = (f32[8,64,128]{2,1,0:T(8,128)S(1)}, f32[8,64,128]{2,1,0:T(8,128)S(1)}, u32[]{:S(2)}, u32[]{:S(2)}) collective-permute-start(f32[8,64,128]{2,1,0:T(8,128)S(1)} %multiply_add_fusion.3), channel_id=1, source_target_pairs={{0,16},{16,32},{32,48},{48,64},{64,80},{80,96},{96,112},{112,128},... | collective-permute-start | bytes 786440 | tf_op jit(solution)/shard_map/while/body/eval_jaxpr/ppermute | solution.py:16
  71.7 15.0 %collective-permute-start = (f32[8,64,128]{2,1,0:T(8,128)S(1)}, f32[8,64,128]{2,1,0:T(8,128)S(1)}, u32[]{:S(2)}, u32[]{:S(2)}) collective-permute-start(f32[8,64,128]{2,1,0:T(8,128)S(1)} %multiply_add_fusion.3), channel_id=1, source_target_pairs={{0,16},{16,32},{32,48},{48,64},{64,80},{80,96},{96,112},{112,128},... | collective-permute-start | bytes 786440 | tf_op jit(solution)/shard_map/while/body/eval_jaxpr/ppermute | solution.py:16
  86.8 12.5 %collective-permute-start = (f32[8,64,128]{2,1,0:T(8,128)S(1)}, f32[8,64,128]{2,1,0:T(8,128)S(1)}, u32[]{:S(2)}, u32[]{:S(2)}) collective-permute-start(f32[8,64,128]{2,1,0:T(8,128)S(1)} %multiply_add_fusion.3), channel_id=1, source_target_pairs={{0,16},{16,32},{32,48},{48,64},{64,80},{80,96},{96,112},{112,128},... | collective-permute-start | bytes 786440 | tf_op jit(solution)/shard_map/while/body/eval_jaxpr/ppermute | solution.py:16
  99.4 12.5 %collective-permute-start = (f32[8,64,128]{2,1,0:T(8,128)S(1)}, f32[8,64,128]{2,1,0:T(8,128)S(1)}, u32[]{:S(2)}, u32[]{:S(2)}) collective-permute-start(f32[8,64,128]{2,1,0:T(8,128)S(1)} %multiply_add_fusion.3), channel_id=1, source_target_pairs={{0,16},{16,32},{32,48},{48,64},{64,80},{80,96},{96,112},{112,128},... | collective-permute-start | bytes 786440 | tf_op jit(solution)/shard_map/while/body/eval_jaxpr/ppermute | solution.py:16
  112.0 15.4 %collective-permute-start = (f32[8,64,128]{2,1,0:T(8,128)S(1)}, f32[8,64,128]{2,1,0:T(8,128)S(1)}, u32[]{:S(2)}, u32[]{:S(2)}) collective-permute-start(f32[8,64,128]{2,1,0:T(8,128)S(1)} %multiply_add_fusion.3), channel_id=1, source_target_pairs={{0,16},{16,32},{32,48},{48,64},{64,80},{80,96},{96,112},{112,128},... | collective-permute-start | bytes 786440 | tf_op jit(solution)/shard_map/while/body/eval_jaxpr/ppermute | solution.py:16
  127.5 14.2 %collective-permute-start = (f32[8,64,128]{2,1,0:T(8,128)S(1)}, f32[8,64,128]{2,1,0:T(8,128)S(1)}, u32[]{:S(2)}, u32[]{:S(2)}) collective-permute-start(f32[8,64,128]{2,1,0:T(8,128)S(1)} %multiply_add_fusion.3), channel_id=1, source_target_pairs={{0,16},{16,32},{32,48},{48,64},{64,80},{80,96},{96,112},{112,128},... | collective-permute-start | bytes 786440 | tf_op jit(solution)/shard_map/while/body/eval_jaxpr/ppermute | solution.py:16
  141.8 12.7 %collective-permute-start = (f32[8,64,128]{2,1,0:T(8,128)S(1)}, f32[8,64,128]{2,1,0:T(8,128)S(1)}, u32[]{:S(2)}, u32[]{:S(2)}) collective-permute-start(f32[8,64,128]{2,1,0:T(8,128)S(1)} %multiply_add_fusion.3), channel_id=1, source_target_pairs={{0,16},{16,32},{32,48},{48,64},{64,80},{80,96},{96,112},{112,128},... | collective-permute-start | bytes 786440 | tf_op jit(solution)/shard_map/while/body/eval_jaxpr/ppermute | solution.py:16
  154.6 13.6 %collective-permute-start = (f32[8,64,128]{2,1,0:T(8,128)S(1)}, f32[8,64,128]{2,1,0:T(8,128)S(1)}, u32[]{:S(2)}, u32[]{:S(2)}) collective-permute-start(f32[8,64,128]{2,1,0:T(8,128)S(1)} %multiply_add_fusion.3), channel_id=1, source_target_pairs={{0,16},{16,32},{32,48},{48,64},{64,80},{80,96},{96,112},{112,128},... | collective-permute-start | bytes 786440 | tf_op jit(solution)/shard_map/while/body/eval_jaxpr/ppermute | solution.py:16
  168.3 13.8 %collective-permute-start = (f32[8,64,128]{2,1,0:T(8,128)S(1)}, f32[8,64,128]{2,1,0:T(8,128)S(1)}, u32[]{:S(2)}, u32[]{:S(2)}) collective-permute-start(f32[8,64,128]{2,1,0:T(8,128)S(1)} %multiply_add_fusion.3), channel_id=1, source_target_pairs={{0,16},{16,32},{32,48},{48,64},{64,80},{80,96},{96,112},{112,128},... | collective-permute-start | bytes 786440 | tf_op jit(solution)/shard_map/while/body/eval_jaxpr/ppermute | solution.py:16
  182.2 14.4 %collective-permute-start = (f32[8,64,128]{2,1,0:T(8,128)S(1)}, f32[8,64,128]{2,1,0:T(8,128)S(1)}, u32[]{:S(2)}, u32[]{:S(2)}) collective-permute-start(f32[8,64,128]{2,1,0:T(8,128)S(1)} %multiply_add_fusion.3), channel_id=1, source_target_pairs={{0,16},{16,32},{32,48},{48,64},{64,80},{80,96},{96,112},{112,128},... | collective-permute-start | bytes 786440 | tf_op jit(solution)/shard_map/while/body/eval_jaxpr/ppermute | solution.py:16
  196.7 14.4 %collective-permute-start = (f32[8,64,128]{2,1,0:T(8,128)S(1)}, f32[8,64,128]{2,1,0:T(8,128)S(1)}, u32[]{:S(2)}, u32[]{:S(2)}) collective-permute-start(f32[8,64,128]{2,1,0:T(8,128)S(1)} %multiply_add_fusion.3), channel_id=1, source_target_pairs={{0,16},{16,32},{32,48},{48,64},{64,80},{80,96},{96,112},{112,128},... | collective-permute-start | bytes 786440 | tf_op jit(solution)/shard_map/while/body/eval_jaxpr/ppermute | solution.py:16
  211.2 14.4 %collective-permute-start = (f32[8,64,128]{2,1,0:T(8,128)S(1)}, f32[8,64,128]{2,1,0:T(8,128)S(1)}, u32[]{:S(2)}, u32[]{:S(2)}) collective-permute-start(f32[8,64,128]{2,1,0:T(8,128)S(1)} %multiply_add_fusion.3), channel_id=1, source_target_pairs={{0,16},{16,32},{32,48},{48,64},{64,80},{80,96},{96,112},{112,128},... | collective-permute-start | bytes 786440 | tf_op jit(solution)/shard_map/while/body/eval_jaxpr/ppermute | solution.py:16
  225.7 14.4 %collective-permute-start = (f32[8,64,128]{2,1,0:T(8,128)S(1)}, f32[8,64,128]{2,1,0:T(8,128)S(1)}, u32[]{:S(2)}, u32[]{:S(2)}) collective-permute-start(f32[8,64,128]{2,1,0:T(8,128)S(1)} %multiply_add_fusion.3), channel_id=1, source_target_pairs={{0,16},{16,32},{32,48},{48,64},{64,80},{80,96},{96,112},{112,128},... | collective-permute-start | bytes 786440 | tf_op jit(solution)/shard_map/while/body/eval_jaxpr/ppermute | solution.py:16
  240.2 14.4 %collective-permute-start = (f32[8,64,128]{2,1,0:T(8,128)S(1)}, f32[8,64,128]{2,1,0:T(8,128)S(1)}, u32[]{:S(2)}, u32[]{:S(2)}) collective-permute-start(f32[8,64,128]{2,1,0:T(8,128)S(1)} %multiply_add_fusion.3), channel_id=1, source_target_pairs={{0,16},{16,32},{32,48},{48,64},{64,80},{80,96},{96,112},{112,128},... | collective-permute-start | bytes 786440 | tf_op jit(solution)/shard_map/while/body/eval_jaxpr/ppermute | solution.py:16
  254.7 14.4 %collective-permute-start = (f32[8,64,128]{2,1,0:T(8,128)S(1)}, f32[8,64,128]{2,1,0:T(8,128)S(1)}, u32[]{:S(2)}, u32[]{:S(2)}) collective-permute-start(f32[8,64,128]{2,1,0:T(8,128)S(1)} %multiply_add_fusion.3), channel_id=1, source_target_pairs={{0,16},{16,32},{32,48},{48,64},{64,80},{80,96},{96,112},{112,128},... | collective-permute-start | bytes 786440 | tf_op jit(solution)/shard_map/while/body/eval_jaxpr/ppermute | solution.py:16
  281.1 0.7 copy-start.6
  281.1 191.5 %copy-start.1 = (bf16[32,4096]{1,0:T(8,128)(2,1)S(1)}, bf16[32,4096]{1,0:T(8,128)(2,1)}, u32[]{:S(2)}) copy-start(bf16[32,4096]{1,0:T(8,128)(2,1)} %param.27) | copy-start | bytes 786436
  281.1 192.9 %copy-start.4 = (f32[4096]{0:T(1024)S(1)}, f32[4096]{0:T(1024)}, u32[]{:S(2)}) copy-start(f32[4096]{0:T(1024)} %param.28) | copy-start | bytes 49156
  281.1 294.7 %all-gather.6.cloned.1.call-start = ((), (), s32[]{:S(2)}) async-start(), calls=%async_computation.4 | async-start | bytes 4456448 | tf_op jit(solution)/shard_map/all_gather | solution.py:121
  475.9 176.4 %all-gather.8.cloned.1.call-start = ((), (), s32[]{:S(2)}) async-start(), calls=%async_computation.5 | async-start | bytes 4456448 | tf_op jit(solution)/shard_map/all_gather | solution.py:81
  476.5 371.5 %reduce-scatter.5.cloned.1.call-start = ((), (), s32[]{:S(2)}) async-start(), calls=%async_computation.6 | async-start | bytes 8912896 | tf_op jit(solution)/shard_map/reduce_scatter | solution.py:126
  664.8 183.3 %copy-start = (f32[32,4096]{1,0:T(8,128)S(1)}, f32[32,4096]{1,0:T(8,128)}, u32[]{:S(2)}) copy-start(f32[32,4096]{1,0:T(8,128)} %reduce-scatter.3.cloned.1.call-done) | copy-start | bytes 1572868
Sparse Core Ops, SparseCore 0:
  9.9 86.5 all-gather.3
  281.2 191.3 reduce-scatter.2
  476.0 99.7 all-gather.5
  578.2 74.0 all-gather.7
  664.9 183.0 reduce-scatter.4
where the time goes:
time: 859 us; the launch traced here: 856 us
  waiting for transfers between devices  685 us (80%)
  blocking collectives  49.5 us (6%)
  local copies, waits for them, and re-layouts  34.6 us (4%)
  matrix products  32.4 us (4%)
  starting transfers between devices  29.3 us (3%)
  between operations  13.9 us (2%)
  other arithmetic  11.3 us (1%)
    ppermute x15, waiting for transfers between devices, passed_along(): lax.ppermute(value, axis, [(source, source + steps) for source in range(i...  191 us
    reduce_scatter x1, waiting for transfers between devices, shards(): lax.psum_scatter(jnp.dot(rows_piece, down_full, preferred_element_type=jn...  183 us
    reduce_scatter x1, waiting for transfers between devices, shards(): lax.psum_scatter(partial_value, 'head', scatter_dimension=0, tiled=True)  140 us
    all_gather x1, waiting for transfers between devices, shards(): rows_piece = lax.all_gather(normed, 'head', axis=0, tiled=True)  99.1 us
    all_gather x1, waiting for transfers between devices, shards(): lax.all_gather(down_weight, 'seq', axis=1, tiled=True)  70.7 us
    unnamed x1, blocking collectives  49.5 us
    ppermute x15, starting transfers between devices, passed_along(): lax.ppermute(value, axis, [(source, source + steps) for source in range(i...  28.9 us
    dynamic_update_slice x4, local copies, waits for them, and re-layouts, block_scan(): lax.scan(advance, start_state, (x_blocks, b_blocks, c_blocks, d_blocks, a...  24.2 us
  transfers between devices with their start and end apart: 20, of which 19 were waited for; matrix products, arithmetic and copies ran while one was open for 6% of the time, Pallas kernels for 0%

commit v1 on v0

v1 whole, which is shorter than its diff:
```python
import jax
import jax.numpy as jnp
from jax import lax
from jax.sharding import PartitionSpec as P

BLOCK = 256
INNER = 8192


epsilon = 1e-05


def passed_along(value, axis, steps):
    count = lax.axis_size(axis)
    initial, last = (max(0, -steps), min(count, count - steps))
    return lax.ppermute(value, axis, [(source, source + steps) for source in range(initial, last)])


def block_scan(x_heads, b_rows, c_rows, step_size, log_decay, block_len):
    length, head_count, head_width = x_heads.shape
    state_size = b_rows.shape[1]
    block_count = length // block_len
    lower_mask = jnp.tril(jnp.ones((block_len, block_len), dtype=bool))
    carry_state = jnp.zeros((head_count, head_width, state_size), jnp.float32)
    outs = []
    for blk in range(block_count):
        rows = slice(blk * block_len, (blk + 1) * block_len)
        x_block = x_heads[rows]
        b_block = b_rows[rows]
        c_block = c_rows[rows]
        d_block = step_size[:, rows]
        a_block = log_decay[:, rows]
        cumulative = jnp.cumsum(a_block, axis=1)
        gap_values = jnp.where(
            lower_mask[None], cumulative[:, :, None] - cumulative[:, None, :], -jnp.inf
        )
        scores = jnp.dot(c_block, b_block.T, preferred_element_type=jnp.float32)
        mixing = (jnp.exp(gap_values) * scores[None] * d_block[:, None, :]).astype(jnp.bfloat16)
        within = jnp.einsum("hij,jhp->ihp", mixing, x_block, preferred_element_type=jnp.float32)
        if blk > 0:
            carried = jnp.einsum(
                "in,hpn->ihp", c_block.astype(jnp.float32), carry_state,
                precision=lax.Precision.HIGHEST,
            )
            within = within + carried * jnp.exp(cumulative).T[:, :, None]
        last_cum = cumulative[:, -1:]
        inject = (
            (jnp.exp(last_cum - cumulative) * d_block)[:, :, None]
            * b_block.astype(jnp.float32)[None]
        ).astype(jnp.bfloat16)
        added = jnp.einsum("jhp,hjn->hpn", x_block, inject, preferred_element_type=jnp.float32)
        carry_state = jnp.exp(last_cum)[:, :, None] * carry_state + added
        outs.append(within)
    return jnp.concatenate(outs, axis=0), carry_state


def entering_state(group_decay, local_state):
    count = lax.axis_size("seq")
    dec = passed_along(group_decay, "seq", 1)
    st = passed_along(local_state, "seq", 1)
    step = 1
    while step < count:
        sp = passed_along(st, "seq", step)
        if step * 2 < count:
            dp = passed_along(dec, "seq", step)
        st = dec[:, None, None] * sp + st
        if step * 2 < count:
            dec = dp * dec
        step *= 2
    return st


def normalize_rows(layer_sum, mlp_gain):
    mean_square = jnp.mean(layer_sum * layer_sum, axis=1, keepdims=True)
    return (layer_sum * lax.rsqrt(mean_square + epsilon) * mlp_gain).astype(jnp.bfloat16)


def shards(
    x_in,
    z_in,
    bc,
    dt_raw,
    dt_bias,
    decay_rate,
    d_skip,
    norm_gain,
    out_weight,
    resid,
    mlp_gain,
    gate_weight,
    up_weight,
    down_weight,
):
    out_full, down_full = (
        lax.all_gather(out_weight, "seq", axis=1, tiled=True),
        lax.all_gather(down_weight, "seq", axis=1, tiled=True),
    )
    head_count = dt_raw.shape[0]
    length = dt_raw.shape[1]
    head_width = x_in.shape[1] // head_count
    step_size = jax.nn.softplus(dt_raw + dt_bias[:, None])
    log_decay = -decay_rate[:, None] * step_size
    x_heads = x_in.reshape(length, head_count, head_width)
    local_out, local_state = block_scan(x_heads, bc[0], bc[1], step_size, log_decay, BLOCK)
    running = jnp.cumsum(log_decay, axis=1)
    group_decay = jnp.exp(running[:, -1])
    entering = entering_state(group_decay, local_state)
    carried = jnp.einsum(
        "tn,hpn->thp", bc[1].astype(jnp.float32), entering, precision=lax.Precision.HIGHEST
    )
    carried = carried * jnp.exp(running).T[:, :, None]
    ssd_out = local_out + carried + d_skip[None, :, None] * x_heads.astype(jnp.float32)
    gated_out = ssd_out.reshape(length, head_count * head_width) * jax.nn.silu(
        z_in.astype(jnp.float32)
    )
    row_squares = jnp.sum(gated_out * gated_out, axis=1)
    gated_scaled = (gated_out * norm_gain).astype(jnp.bfloat16)
    partial_value = jnp.dot(gated_scaled, out_full, preferred_element_type=jnp.float32)
    width = partial_value.shape[1]
    sq_hi = row_squares.astype(jnp.bfloat16)
    sq_lo = (row_squares - sq_hi.astype(jnp.float32)).astype(jnp.bfloat16)
    extra = jnp.zeros((length, 128), jnp.bfloat16).at[:, 0].set(sq_hi).at[:, 1].set(sq_lo)
    packed = jnp.concatenate([partial_value.astype(jnp.bfloat16), extra], axis=1)
    reduced = lax.psum_scatter(packed, "head", scatter_dimension=0, tiled=True)
    part_rows = reduced[:, :width].astype(jnp.float32)
    part_squares = reduced[:, width].astype(jnp.float32) + reduced[:, width + 1].astype(jnp.float32)
    layer_sum = (
        resid.astype(jnp.float32) + part_rows * lax.rsqrt(part_squares / INNER + epsilon)[:, None]
    )
    normed = normalize_rows(layer_sum, mlp_gain)
    rows_piece = lax.all_gather(normed, "head", axis=0, tiled=True)
    gate_part = jnp.dot(rows_piece, gate_weight, preferred_element_type=jnp.float32)
    up_part = jnp.dot(rows_piece, up_weight, preferred_element_type=jnp.float32)
    hidden = (jax.nn.silu(gate_part) * up_part).astype(jnp.bfloat16)
    mlp_part = jnp.dot(hidden, down_full, preferred_element_type=jnp.float32)
    mlp_rows = lax.psum_scatter(
        mlp_part.astype(jnp.bfloat16), "head", scatter_dimension=0, tiled=True
    )
    return (layer_sum + mlp_rows.astype(jnp.float32)).astype(jnp.bfloat16)


def solution(mesh):
    in_specs = (
        P("seq", "head"),
        P("seq", "head"),
        P(None, "seq", None),
        P("head", "seq"),
        P("head"),
        P("head"),
        P("head"),
        P("head"),
        P("head", "seq"),
        P(("seq", "head"), None),
        P(),
        P(None, "head"),
        P(None, "head"),
        P("head", "seq"),
    )
    out_specs = P(("seq", "head"), None)
    return jax.shard_map(shards, mesh=mesh, in_specs=in_specs, out_specs=out_specs, check_vma=False)
```

time: 859 us -> 525 us (0.61)
  waiting for transfers between devices: 685 us -> 421 us
  blocking collectives: 49.5 us -> 0 us
  local copies, waits for them, and re-layouts: 34.6 us -> 3.17 us
  starting transfers between devices: 29.3 us -> 41.7 us
    ppermute x15 -> x9, waiting for transfers between devices: 191 us -> 43.8 us  [passed_along(): lax.ppermute(value, axis, [(source, source + steps) for source in range(i...]
    reduce_scatter x2, waiting for transfers between devices: 323 us -> 208 us  [the longest x1 106 us: shards(): reduced = lax.psum_scatter(packed, 'head', scatter_dimension=0, tiled=True)]
    unnamed x1 -> x0, blocking collectives: 49.5 us -> none
    dynamic_update_slice x4 -> x0, local copies, waits for them, and re-layouts: 24.2 us -> none  [block_scan(): lax.scan(advance, start_state, (x_blocks, b_blocks, c_blocks, d_blocks, a...]
    ppermute x15 -> x9, starting transfers between devices: 28.9 us -> 41.3 us  [passed_along(): lax.ppermute(value, axis, [(source, source + steps) for source in range(i...]
  transfers between devices with their start and end apart: 20 -> 14, of which waited for: 19 -> 10; matrix products, arithmetic and copies ran while one was open for 6% -> 4% of each run, Pallas kernels for 0% -> 0%
where the time goes in v1:
time: 525 us; the launch traced here: 524 us
  waiting for transfers between devices  421 us (80%)
  starting transfers between devices  41.7 us (8%)
  matrix products  26.3 us (5%)
  other arithmetic  17.9 us (3%)
  between operations  13.5 us (3%)
    reduce_scatter x1, waiting for transfers between devices, shards(): reduced = lax.psum_scatter(packed, 'head', scatter_dimension=0, tiled=True)  106 us
    reduce_scatter x1, waiting for transfers between devices, shards(): lax.psum_scatter(mlp_part.astype(jnp.bfloat16), 'head', scatter_dimension...  102 us
    all_gather x1, waiting for transfers between devices, shards(): rows_piece = lax.all_gather(normed, 'head', axis=0, tiled=True)  98.1 us
    all_gather x1, waiting for transfers between devices, shards(): lax.all_gather(down_weight, 'seq', axis=1, tiled=True)  70.7 us
    ppermute x9, waiting for transfers between devices, passed_along(): lax.ppermute(value, axis, [(source, source + steps) for source in range(i...  43.8 us
    ppermute x9, starting transfers between devices, passed_along(): lax.ppermute(value, axis, [(source, source + steps) for source in range(i...  41.3 us
    dot_general x1, matrix products, shards(): mlp_part = jnp.dot(hidden, down_full, preferred_element_type=jnp.float32)  11.2 us
  transfers between devices with their start and end apart: 14, of which 10 were waited for; matrix products, arithmetic and copies ran while one was open for 4% of the time, Pallas kernels for 0%

profile of v1, /device:TPU:8, one launch (start us, length us, event | category | flops | bytes accessed | tf_op | source)
XLA Modules:
  0.0 523.9 jit_solution(5762854799587462316)
XLA Ops:
  6.5 0.7 all-gather.4.cloned.1.call-update
  7.3 0.7 neg.15
  8.0 0.8 broadcast_multiply_fusion
  8.8 0.6 reduce-window.24
  9.6 0.6 reduce-window.20
  10.3 1.1 fusion.53
  12.2 0.9 bitcast_convert_fusion
  13.1 0.5 fusion.7
  13.6 0.5 fusion.6
  14.1 1.9 collective-permute-start.4
  16.0 1.1 reduce-window.26
  17.4 9.2 %collective-permute-done.4 = f32[8,64,128]{2,1,0:T(8,128)S(1)} collective-permute-done((f32[8,64,128]{2,1,0:T(8,128)S(1)}, f32[8,64,128]{2,1,0:T(8,128)S(1)}, u32[]{:S(2)}, u32[]{:S(2)}) %collective-permute-start.4) | collective-permute-done | bytes 262176 | tf_op jit(solution)/shard_map/ppermute | solution.py:16
  26.7 8.6 %collective-permute-start.5 = (f32[8,64,128]{2,1,0:T(8,128)S(1)}, f32[8,64,128]{2,1,0:T(8,128)S(1)}, u32[]{:S(2)}, u32[]{:S(2)}) collective-permute-start(f32[8,64,128]{2,1,0:T(8,128)S(1)} %collective-permute-done.4), channel_id=1, source_target_pairs={{0,16},{16,32},{32,48},{48,64},{64,80},{80,96},{96,112},{112,128},... | collective-permute-start | bytes 786440 | tf_op jit(solution)/shard_map/ppermute | solution.py:16
  35.4 8.7 %collective-permute-start = (f32[8]{0:T(128)S(1)}, f32[8]{0:T(128)S(1)}, u32[]{:S(2)}, u32[]{:S(2)}) collective-permute-start(f32[8]{0:T(128)S(1)} %fusion.48), channel_id=1, source_target_pairs={{0,16},{16,32},{32,48},{48,64},{64,80},{80,96},{96,112},{112,128},... | collective-permute-start | bytes 104 | tf_op jit(solution)/shard_map/ppermute | solution.py:16
  44.3 0.8 collective-permute-done
  45.2 9.8 %collective-permute-start.6 = (f32[8,64,128]{2,1,0:T(8,128)S(1)}, f32[8,64,128]{2,1,0:T(8,128)S(1)}, u32[]{:S(2)}, u32[]{:S(2)}) collective-permute-start(f32[8,64,128]{2,1,0:T(8,128)S(1)} %multiply_add_fusion.3), channel_id=1, source_target_pairs={{0,32},{16,48},{32,64},{48,80},{64,96},{80,112},{96,128},{112,144}... | collective-permute-start | bytes 786440 | tf_op jit(solution)/shard_map/ppermute | solution.py:16
  55.0 0.9 fusion.37
  56.3 1.9 collective-permute-start.1
  58.2 21.1 %collective-permute-done.1 = f32[8]{0:T(128)S(1)} collective-permute-done((f32[8]{0:T(128)S(1)}, f32[8]{0:T(128)S(1)}, u32[]{:S(2)}, u32[]{:S(2)}) %collective-permute-start.1) | collective-permute-done | bytes 64 | tf_op jit(solution)/shard_map/ppermute | solution.py:16
  79.4 2.3 collective-permute-done.6
  81.7 2.9 collective-permute-start.7
  84.9 0.7 compare_reduce_fusion.1
  85.7 0.6 compare_reduce_fusion
  86.3 0.7 convolution_bitcast_fusion.3
  87.0 4.3 collective-permute-start.2
  91.3 6.0 %collective-permute-done.2 = f32[8]{0:T(128)S(1)} collective-permute-done((f32[8]{0:T(128)S(1)}, f32[8]{0:T(128)S(1)}, u32[]{:S(2)}, u32[]{:S(2)}) %collective-permute-start.2) | collective-permute-done | bytes 64 | tf_op jit(solution)/shard_map/ppermute | solution.py:16
  97.3 1.0 multiply_add_fusion.1
  98.3 1.3 collective-permute-start.8
  99.7 0.7 fusion.4
  100.4 1.9 collective-permute-start.3
  102.3 4.3 collective-permute-done.3
  106.7 0.7 fusion.2
  107.8 0.4 multiply_reduce_fusion
  108.3 1.3 fusion.32
  109.7 0.4 scatter.9
  110.1 4.6 convolution_convert_fusion.1
  114.8 2.3 pad_maximum_fusion
  117.2 106.0 %reduce-scatter.3.cloned.1.call-done = bf16[32,4224]{1,0:T(8,128)(2,1)} async-done(((bf16[512,4224]{1,0:T(8,128)(2,1)}), bf16[32,4224]{1,0:T(8,128)(2,1)}) %reduce-scatter.3.cloned.1.call-update) | async-done | bytes 270352 | tf_op jit(solution)/shard_map/reduce_scatter | solution.py:124
  223.1 1.0 rsqrt_reduce_fusion
  224.1 1.2 multiply_reduce_fusion.1
  225.4 1.8 multiply_convert_fusion.10
  227.3 0.5 all-gather.8.cloned.1.call-update
  228.0 98.1 %all-gather.6.cloned.1.call-done = bf16[512,4096]{1,0:T(8,128)(2,1)} async-done(((bf16[32,4096]{1,0:T(8,128)(2,1)}), bf16[512,4096]{1,0:T(8,128)(2,1)}) %all-gather.6.cloned.1.call-update) | async-done | bytes 4194320 | tf_op jit(solution)/shard_map/all_gather | solution.py:131
  326.1 5.8 %fusion.54 = f32[512,512]{1,0:T(8,128)S(1)} fusion(bf16[512,4096]{1,0:T(8,128)(2,1)} %all-gather.6.cloned.1.call-done, bf16[4096,512]{1,0:T(8,128)(2,1)} %param.29), kind=kOutput, calls=%fused_computation.107 | convolution fusion | flops 2147483648 | bytes 9437184 | tf_op jit(solution)/shard_map/dot_general | solution.py:132
  331.9 70.7 %all-gather.8.cloned.1.call-done = bf16[512,4096]{1,0:T(8,128)(2,1)} async-done(((bf16[512,256]{1,0:T(8,128)(2,1)}), bf16[512,4096]{1,0:T(8,128)(2,1)}) %all-gather.8.cloned.1.call-update) | async-done | bytes 4194320 | tf_op jit(solution)/shard_map/all_gather | solution.py:96
  402.6 11.2 %convolution_convert_fusion = bf16[512,4096]{1,0:T(8,128)(2,1)} fusion(bf16[512,4096]{1,0:T(8,128)(2,1)} %all-gather.8.cloned.1.call-done, bf16[512,4096]{1,0:T(8,128)(2,1)} %all-gather.6.cloned.1.call-done, bf16[4096,512]{1,0:T(8,128)(2,1)} %param.30, f32[512,512]{1,0:T(8,128)S(1)} %fusion.54), kind=kOutput, calls=%fused_computation | convolution fusion | flops 4298637312 | bytes 17825792 | tf_op jit(solution)/shard_map/dot_general | solution.py:135
  413.9 101.7 %reduce-scatter.5.cloned.1.call-done = bf16[32,4096]{1,0:T(8,128)(2,1)} async-done(((bf16[512,4096]{1,0:T(8,128)(2,1)}), bf16[32,4096]{1,0:T(8,128)(2,1)}) %reduce-scatter.5.cloned.1.call-update) | async-done | bytes 262160 | tf_op jit(solution)/shard_map/reduce_scatter | solution.py:136
  515.5 1.8 add_convert_fusion
  (61 shorter events, 3.6 us)
Async XLA Ops:
  6.5 78.2 %copy-start.2 = (bf16[512,512]{1,0:T(8,128)(2,1)S(1)}, bf16[512,512]{1,0:T(8,128)(2,1)}, u32[]{:S(2)}) copy-start(bf16[512,512]{1,0:T(8,128)(2,1)} %param.18) | copy-start | bytes 1572868
  6.5 37.6 %copy-start.3 = (bf16[2,512,128]{2,1,0:T(8,128)(2,1)S(1)}, bf16[2,512,128]{2,1,0:T(8,128)(2,1)}, u32[]{:S(2)}) copy-start(bf16[2,512,128]{2,1,0:T(8,128)(2,1)} %param.20) | copy-start | bytes 786436
  6.5 103.6 %all-gather.4.cloned.1.call-start = ((), (), s32[]{:S(2)}) async-start(), calls=%async_computation.2 | async-start | bytes 4456448 | tf_op jit(solution)/shard_map/all_gather | solution.py:95
  7.3 215.9 %reduce-scatter.3.cloned.1.call-start = ((), (), s32[]{:S(2)}) async-start(), calls=%async_computation.3 | async-start | bytes 4595712 | tf_op jit(solution)/shard_map/reduce_scatter | solution.py:124
  14.1 12.6 %collective-permute-start.4 = (f32[8,64,128]{2,1,0:T(8,128)S(1)}, f32[8,64,128]{2,1,0:T(8,128)S(1)}, u32[]{:S(2)}, u32[]{:S(2)}) collective-permute-start(f32[8,64,128]{2,1,0:T(8,128)S(1)} %fusion.6), channel_id=1, source_target_pairs={{0,16},{16,32},{32,48},{48,64},{64,80},{80,96},{96,112},{112,128},... | collective-permute-start | bytes 786440 | tf_op jit(solution)/shard_map/ppermute | solution.py:16
  26.7 18.4 %collective-permute-start.5 = (f32[8,64,128]{2,1,0:T(8,128)S(1)}, f32[8,64,128]{2,1,0:T(8,128)S(1)}, u32[]{:S(2)}, u32[]{:S(2)}) collective-permute-start(f32[8,64,128]{2,1,0:T(8,128)S(1)} %collective-permute-done.4), channel_id=1, source_target_pairs={{0,16},{16,32},{32,48},{48,64},{64,80},{80,96},{96,112},{112,128},... | collective-permute-start | bytes 786440 | tf_op jit(solution)/shard_map/ppermute | solution.py:16
  35.4 9.7 %collective-permute-start = (f32[8]{0:T(128)S(1)}, f32[8]{0:T(128)S(1)}, u32[]{:S(2)}, u32[]{:S(2)}) collective-permute-start(f32[8]{0:T(128)S(1)} %fusion.48), channel_id=1, source_target_pairs={{0,16},{16,32},{32,48},{48,64},{64,80},{80,96},{96,112},{112,128},... | collective-permute-start | bytes 104 | tf_op jit(solution)/shard_map/ppermute | solution.py:16
  45.2 36.4 %collective-permute-start.6 = (f32[8,64,128]{2,1,0:T(8,128)S(1)}, f32[8,64,128]{2,1,0:T(8,128)S(1)}, u32[]{:S(2)}, u32[]{:S(2)}) collective-permute-start(f32[8,64,128]{2,1,0:T(8,128)S(1)} %multiply_add_fusion.3), channel_id=1, source_target_pairs={{0,32},{16,48},{32,64},{48,80},{64,96},{80,112},{96,128},{112,144}... | collective-permute-start | bytes 786440 | tf_op jit(solution)/shard_map/ppermute | solution.py:16
  56.3 23.0 %collective-permute-start.1 = (f32[8]{0:T(128)S(1)}, f32[8]{0:T(128)S(1)}, u32[]{:S(2)}, u32[]{:S(2)}) collective-permute-start(f32[8]{0:T(128)S(1)} %collective-permute-done), channel_id=1, source_target_pairs={{0,16},{16,32},{32,48},{48,64},{64,80},{80,96},{96,112},{112,128},... | collective-permute-start | bytes 104 | tf_op jit(solution)/shard_map/ppermute | solution.py:16
  81.7 15.6 %collective-permute-start.7 = (f32[8,64,128]{2,1,0:T(8,128)S(1)}, f32[8,64,128]{2,1,0:T(8,128)}, u32[]{:S(2)}, u32[]{:S(2)}) collective-permute-start(f32[8,64,128]{2,1,0:T(8,128)S(1)} %multiply_add_fusion.2), channel_id=1, source_target_pairs={{0,64},{16,80},{32,96},{48,112},{64,128},{80,144},{96,160},{112,17... | collective-permute-start | bytes 786440 | tf_op jit(solution)/shard_map/ppermute | solution.py:16
  84.9 14.7 %copy-start.5 = (f32[256,256]{1,0:T(8,128)S(1)}, f32[256,256]{1,0:T(8,128)}, u32[]{:S(2)}) copy-start(f32[256,256]{1,0:T(8,128)} %fusion.37) | copy-start | bytes 786436
  86.3 20.4 %copy-start.7 = (f32[8]{0:T(128)S(1)}, f32[8]{0:T(128)}, u32[]{:S(2)}) copy-start(f32[8]{0:T(128)} %param.24) | copy-start | bytes 100
  87.0 10.3 %collective-permute-start.2 = (f32[8]{0:T(128)S(1)}, f32[8]{0:T(128)S(1)}, u32[]{:S(2)}, u32[]{:S(2)}) collective-permute-start(f32[8]{0:T(128)S(1)} %mul.238), channel_id=1, source_target_pairs={{0,32},{16,48},{32,64},{48,80},{64,96},{80,112},{96,128},{112,144}... | collective-permute-start | bytes 104 | tf_op jit(solution)/shard_map/ppermute | solution.py:16
  98.3 8.3 %collective-permute-start.8 = (f32[8,64,128]{2,1,0:T(8,128)S(1)}, f32[8,64,128]{2,1,0:T(8,128)S(1)}, u32[]{:S(2)}, u32[]{:S(2)}) collective-permute-start(f32[8,64,128]{2,1,0:T(8,128)S(1)} %multiply_add_fusion.1), channel_id=1, source_target_pairs={{0,128},{16,144},{32,160},{48,176},{64,192},{80,208},{96,224},{112... | collective-permute-start | bytes 786440 | tf_op jit(solution)/shard_map/ppermute | solution.py:16
  99.7 8.1 %copy-start.4 = (bf16[512,512]{1,0:T(8,128)(2,1)S(1)}, bf16[512,512]{1,0:T(8,128)(2,1)}, u32[]{:S(2)}) copy-start(bf16[512,512]{1,0:T(8,128)(2,1)} %param.19) | copy-start | bytes 1572868
  100.4 6.3 %collective-permute-start.3 = (f32[8]{0:T(128)S(1)}, f32[8]{0:T(128)S(1)}, u32[]{:S(2)}, u32[]{:S(2)}) collective-permute-start(f32[8]{0:T(128)S(1)} %mul.239), channel_id=1, source_target_pairs={{0,64},{16,80},{32,96},{48,112},{64,128},{80,144},{96,160},{112,17... | collective-permute-start | bytes 104 | tf_op jit(solution)/shard_map/ppermute | solution.py:16
  106.7 3.5 copy-start.8
  117.1 107.0 %copy-start.1 = (bf16[32,4096]{1,0:T(8,128)(2,1)S(1)}, bf16[32,4096]{1,0:T(8,128)(2,1)}, u32[]{:S(2)}) copy-start(bf16[32,4096]{1,0:T(8,128)(2,1)} %param.27) | copy-start | bytes 786436
  117.1 108.2 %copy-start.6 = (f32[4096]{0:T(1024)S(1)}, f32[4096]{0:T(1024)}, u32[]{:S(2)}) copy-start(f32[4096]{0:T(1024)} %param.28) | copy-start | bytes 49156
  117.1 209.0 %all-gather.6.cloned.1.call-start = ((), (), s32[]{:S(2)}) async-start(), calls=%async_computation.4 | async-start | bytes 4456448 | tf_op jit(solution)/shard_map/all_gather | solution.py:131
  227.2 175.4 %all-gather.8.cloned.1.call-start = ((), (), s32[]{:S(2)}) async-start(), calls=%async_computation.5 | async-start | bytes 4456448 | tf_op jit(solution)/shard_map/all_gather | solution.py:96
  227.8 287.7 %reduce-scatter.5.cloned.1.call-start = ((), (), s32[]{:S(2)}) async-start(), calls=%async_computation.6 | async-start | bytes 4456448 | tf_op jit(solution)/shard_map/reduce_scatter | solution.py:136
  413.8 101.7 %copy-start = (bf16[32,4224]{1,0:T(8,128)(2,1)S(1)}, bf16[32,4224]{1,0:T(8,128)(2,1)}, u32[]{:S(2)}) copy-start(bf16[32,4224]{1,0:T(8,128)(2,1)} %reduce-scatter.3.cloned.1.call-done) | copy-start | bytes 811012
Sparse Core Ops, SparseCore 0:
  9.9 89.3 all-gather.3
  117.3 105.8 reduce-scatter.2
  227.4 98.7 all-gather.5
  328.5 74.0 all-gather.7
  414.0 101.5 reduce-scatter.4

commit v2 on v1

--- a/solution.py
+++ b/solution.py
@@ -70,6 +70,13 @@
     return st
 
 
+def sum_over_head(value):
+    count = lax.axis_size("head")
+    pieces = value.reshape(count, value.shape[0] // count, value.shape[1])
+    pieces = lax.all_to_all(pieces, "head", 0, 0, tiled=False)
+    return jnp.sum(pieces.astype(jnp.float32), axis=0)
+
+
 def normalize_rows(layer_sum, mlp_gain):
     mean_square = jnp.mean(layer_sum * layer_sum, axis=1, keepdims=True)
     return (layer_sum * lax.rsqrt(mean_square + epsilon) * mlp_gain).astype(jnp.bfloat16)
@@ -121,9 +128,10 @@
     sq_lo = (row_squares - sq_hi.astype(jnp.float32)).astype(jnp.bfloat16)
     extra = jnp.zeros((length, 128), jnp.bfloat16).at[:, 0].set(sq_hi).at[:, 1].set(sq_lo)
     packed = jnp.concatenate([partial_value.astype(jnp.bfloat16), extra], axis=1)
-    reduced = lax.psum_scatter(packed, "head", scatter_dimension=0, tiled=True)
-    part_rows = reduced[:, :width].astype(jnp.float32)
-    part_squares = reduced[:, width].astype(jnp.float32) + reduced[:, width + 1].astype(jnp.float32)
+    reduced = sum_over_head(packed)
+    reduced, down_full = lax.optimization_barrier((reduced, down_full))
+    part_rows = reduced[:, :width]
+    part_squares = reduced[:, width] + reduced[:, width + 1]
     layer_sum = (
         resid.astype(jnp.float32) + part_rows * lax.rsqrt(part_squares / INNER + epsilon)[:, None]
     )
@@ -133,10 +141,8 @@
     up_part = jnp.dot(rows_piece, up_weight, preferred_element_type=jnp.float32)
     hidden = (jax.nn.silu(gate_part) * up_part).astype(jnp.bfloat16)
     mlp_part = jnp.dot(hidden, down_full, preferred_element_type=jnp.float32)
-    mlp_rows = lax.psum_scatter(
-        mlp_part.astype(jnp.bfloat16), "head", scatter_dimension=0, tiled=True
-    )
-    return (layer_sum + mlp_rows.astype(jnp.float32)).astype(jnp.bfloat16)
+    mlp_rows = sum_over_head(mlp_part.astype(jnp.bfloat16))
+    return (layer_sum + mlp_rows).astype(jnp.bfloat16)
 
 
 def solution(mesh):

time: 525 us -> 476 us (0.907)
  waiting for transfers between devices: 421 us -> 265 us
  blocking collectives: 0 us -> 98.7 us
  starting transfers between devices: 41.7 us -> 50.1 us
    reduce_scatter x2 -> x0, waiting for transfers between devices: 208 us -> none  [the longest x1 106 us: shards(): reduced = lax.psum_scatter(packed, 'head', scatter_dimension=0, tiled=True)]
    all_to_all x0 -> x1, waiting for transfers between devices: none -> 122 us  [sum_over_head(): pieces = lax.all_to_all(pieces, 'head', 0, 0, tiled=False)]
    all_to_all x0 -> x1, blocking collectives: none -> 98.7 us  [sum_over_head(): pieces = lax.all_to_all(pieces, 'head', 0, 0, tiled=False)]
    all_gather x1, waiting for transfers between devices: 70.7 us -> 0.02 us  [shards(): lax.all_gather(down_weight, 'seq', axis=1, tiled=True)]
    all_to_all x0 -> x1, starting transfers between devices: none -> 8.41 us  [sum_over_head(): pieces = lax.all_to_all(pieces, 'head', 0, 0, tiled=False)]
  transfers between devices with their start and end apart: 14 -> 13, of which waited for: 10 -> 8; matrix products, arithmetic and copies ran while one was open for 4% -> 4% of each run, Pallas kernels for 0% -> 0%
where the time goes in v2:
time: 476 us; the launch traced here: 475 us
  waiting for transfers between devices  265 us (56%)
  blocking collectives  98.7 us (21%)
  starting transfers between devices  50.1 us (11%)
  matrix products  26.3 us (6%)
  other arithmetic  17.9 us (4%)
  between operations  13.5 us (3%)
    all_to_all x1, waiting for transfers between devices, sum_over_head(): pieces = lax.all_to_all(pieces, 'head', 0, 0, tiled=False)  122 us
    all_to_all x1, blocking collectives, sum_over_head(): pieces = lax.all_to_all(pieces, 'head', 0, 0, tiled=False)  98.7 us
    all_gather x1, waiting for transfers between devices, shards(): rows_piece = lax.all_gather(normed, 'head', axis=0, tiled=True)  97.8 us
    ppermute x9, waiting for transfers between devices, passed_along(): lax.ppermute(value, axis, [(source, source + steps) for source in range(i...  43.7 us
    ppermute x9, starting transfers between devices, passed_along(): lax.ppermute(value, axis, [(source, source + steps) for source in range(i...  41.4 us
    dot_general x1, matrix products, shards(): mlp_part = jnp.dot(hidden, down_full, preferred_element_type=jnp.float32)  11.3 us
  transfers between devices with their start and end apart: 13, of which 8 were waited for; matrix products, arithmetic and copies ran while one was open for 4% of the time, Pallas kernels for 0%

profile of v2, /device:TPU:8, one launch (start us, length us, event | category | flops | bytes accessed | tf_op | source)
XLA Modules:
  0.0 475.0 jit_solution(13012639181538995451)
XLA Ops:
  6.5 0.7 all-gather.4.cloned.1.call-update
  7.3 0.7 neg.15
  7.9 0.8 broadcast_multiply_fusion
  8.7 0.6 reduce-window.24
  9.5 0.6 reduce-window.20
  10.3 1.1 fusion.53
  12.1 0.9 bitcast_convert_fusion
  13.0 0.5 fusion.7
  13.5 0.5 fusion.6
  14.0 1.9 collective-permute-start.4
  16.0 1.1 reduce-window.26
  17.4 9.2 %collective-permute-done.4 = f32[8,64,128]{2,1,0:T(8,128)S(1)} collective-permute-done((f32[8,64,128]{2,1,0:T(8,128)S(1)}, f32[8,64,128]{2,1,0:T(8,128)S(1)}, u32[]{:S(2)}, u32[]{:S(2)}) %collective-permute-start.4) | collective-permute-done | bytes 262176 | tf_op jit(solution)/shard_map/ppermute | solution.py:16
  26.6 8.6 %collective-permute-start.5 = (f32[8,64,128]{2,1,0:T(8,128)S(1)}, f32[8,64,128]{2,1,0:T(8,128)S(1)}, u32[]{:S(2)}, u32[]{:S(2)}) collective-permute-start(f32[8,64,128]{2,1,0:T(8,128)S(1)} %collective-permute-done.4), channel_id=1, source_target_pairs={{0,16},{16,32},{32,48},{48,64},{64,80},{80,96},{96,112},{112,128},... | collective-permute-start | bytes 786440 | tf_op jit(solution)/shard_map/ppermute | solution.py:16
  35.4 8.7 %collective-permute-start = (f32[8]{0:T(128)S(1)}, f32[8]{0:T(128)S(1)}, u32[]{:S(2)}, u32[]{:S(2)}) collective-permute-start(f32[8]{0:T(128)S(1)} %fusion.48), channel_id=1, source_target_pairs={{0,16},{16,32},{32,48},{48,64},{64,80},{80,96},{96,112},{112,128},... | collective-permute-start | bytes 104 | tf_op jit(solution)/shard_map/ppermute | solution.py:16
  44.3 0.8 collective-permute-done
  45.2 9.8 %collective-permute-start.6 = (f32[8,64,128]{2,1,0:T(8,128)S(1)}, f32[8,64,128]{2,1,0:T(8,128)S(1)}, u32[]{:S(2)}, u32[]{:S(2)}) collective-permute-start(f32[8,64,128]{2,1,0:T(8,128)S(1)} %multiply_add_fusion.3), channel_id=1, source_target_pairs={{0,32},{16,48},{32,64},{48,80},{64,96},{80,112},{96,128},{112,144}... | collective-permute-start | bytes 786440 | tf_op jit(solution)/shard_map/ppermute | solution.py:16
  55.0 0.9 fusion.37
  56.3 1.9 collective-permute-start.1
  58.2 21.4 %collective-permute-done.1 = f32[8]{0:T(128)S(1)} collective-permute-done((f32[8]{0:T(128)S(1)}, f32[8]{0:T(128)S(1)}, u32[]{:S(2)}, u32[]{:S(2)}) %collective-permute-start.1) | collective-permute-done | bytes 64 | tf_op jit(solution)/shard_map/ppermute | solution.py:16
  79.6 2.0 collective-permute-done.6
  81.7 2.9 collective-permute-start.7
  84.9 0.7 compare_reduce_fusion.1
  85.6 0.6 compare_reduce_fusion
  86.3 0.7 convolution_bitcast_fusion.3
  87.0 4.4 collective-permute-start.2
  91.4 5.9 %collective-permute-done.2 = f32[8]{0:T(128)S(1)} collective-permute-done((f32[8]{0:T(128)S(1)}, f32[8]{0:T(128)S(1)}, u32[]{:S(2)}, u32[]{:S(2)}) %collective-permute-start.2) | collective-permute-done | bytes 64 | tf_op jit(solution)/shard_map/ppermute | solution.py:16
  97.3 1.0 multiply_add_fusion.1
  98.3 1.3 collective-permute-start.8
  99.6 0.7 fusion.4
  100.4 1.9 collective-permute-start.3
  102.3 4.3 collective-permute-done.3
  106.7 0.7 fusion.2
  107.7 0.4 multiply_reduce_fusion
  108.3 1.3 fusion.32
  109.7 0.4 scatter.9
  110.1 4.6 convolution_convert_fusion.1
  114.7 2.4 pad_maximum_fusion
  117.1 8.4 %all-to-all-start = ((bf16[16,32,4224]{2,1,0:T(8,128)(2,1)}), bf16[16,32,4224]{2,1,0:T(8,128)(2,1)}, u32[]{:S(2)}, u32[]{:S(2)}) async-start(bf16[16,32,4224]{2,1,0:T(8,128)(2,1)} %bitcast.80), calls=%async_computation | async-start | bytes 8650752 | tf_op jit(solution)/shard_map/all_to_all | solution.py:76
  125.6 0.7 all-gather.6.cloned.1.call-update
  126.5 122.5 %all-to-all-done = bf16[16,32,4224]{2,1,0:T(8,128)(2,1)} async-done(((bf16[16,32,4224]{2,1,0:T(8,128)(2,1)}), bf16[16,32,4224]{2,1,0:T(8,128)(2,1)}, u32[]{:S(2)}, u32[]{:S(2)}) %all-to-all-start) | async-done | bytes 4325408 | tf_op jit(solution)/shard_map/all_to_all | solution.py:76
  249.0 2.9 convert_reduce_fusion
  252.4 0.9 multiply_convert_fusion.10
  253.3 97.8 %all-gather.8.cloned.1.call-done = bf16[512,4096]{1,0:T(8,128)(2,1)} async-done(((bf16[32,4096]{1,0:T(8,128)(2,1)}), bf16[512,4096]{1,0:T(8,128)(2,1)}) %all-gather.8.cloned.1.call-update) | async-done | bytes 4194320 | tf_op jit(solution)/shard_map/all_gather | solution.py:139
  351.2 5.8 %fusion.54 = f32[512,512]{1,0:T(8,128)S(1)} fusion(bf16[512,4096]{1,0:T(8,128)(2,1)} %all-gather.8.cloned.1.call-done, bf16[4096,512]{1,0:T(8,128)(2,1)} %param.29), kind=kOutput, calls=%fused_computation.109 | convolution fusion | flops 2147483648 | bytes 9437184 | tf_op jit(solution)/shard_map/dot_general | solution.py:140
  356.9 11.3 %convolution_convert_fusion = bf16[512,4096]{1,0:T(8,128)(2,1)} fusion(bf16[512,4096]{1,0:T(8,128)(2,1)} %all-gather.6.cloned.1.call-done, bf16[512,4096]{1,0:T(8,128)(2,1)} %all-gather.8.cloned.1.call-done, bf16[4096,512]{1,0:T(8,128)(2,1)} %param.30, f32[512,512]{1,0:T(8,128)S(1)} %fusion.54), kind=kOutput, calls=%fused_computation.2 | convolution fusion | flops 4298637312 | bytes 17825792 | tf_op jit(solution)/shard_map/dot_general | solution.py:143
  368.2 98.7 %all_to_all.10 = bf16[16,32,4096]{2,1,0:T(8,128)(2,1)S(1)} all-to-all(bf16[16,32,4096]{2,1,0:T(8,128)(2,1)} %bitcast.81), channel_id=1, replica_groups=mesh['seq'=16,'head'=16] {'head'}, dimensions={0} | all-to-all | bytes 8388608 | tf_op jit(solution)/shard_map/all_to_all | solution.py:76
  466.9 0.7 convert_reduce_fusion.1
  467.6 0.8 add_convert_fusion
  (58 shorter events, 3.9 us)
Async XLA Ops:
  6.5 78.1 %copy-start.1 = (bf16[512,512]{1,0:T(8,128)(2,1)S(1)}, bf16[512,512]{1,0:T(8,128)(2,1)}, u32[]{:S(2)}) copy-start(bf16[512,512]{1,0:T(8,128)(2,1)} %param.18) | copy-start | bytes 1572868
  6.5 37.5 %copy-start.2 = (bf16[2,512,128]{2,1,0:T(8,128)(2,1)S(1)}, bf16[2,512,128]{2,1,0:T(8,128)(2,1)}, u32[]{:S(2)}) copy-start(bf16[2,512,128]{2,1,0:T(8,128)(2,1)} %param.20) | copy-start | bytes 786436
  6.5 103.6 %all-gather.4.cloned.1.call-start = ((), (), s32[]{:S(2)}) async-start(), calls=%async_computation.2 | async-start | bytes 4456448 | tf_op jit(solution)/shard_map/all_gather | solution.py:102
  14.0 12.6 %collective-permute-start.4 = (f32[8,64,128]{2,1,0:T(8,128)S(1)}, f32[8,64,128]{2,1,0:T(8,128)S(1)}, u32[]{:S(2)}, u32[]{:S(2)}) collective-permute-start(f32[8,64,128]{2,1,0:T(8,128)S(1)} %fusion.6), channel_id=1, source_target_pairs={{0,16},{16,32},{32,48},{48,64},{64,80},{80,96},{96,112},{112,128},... | collective-permute-start | bytes 786440 | tf_op jit(solution)/shard_map/ppermute | solution.py:16
  26.6 18.5 %collective-permute-start.5 = (f32[8,64,128]{2,1,0:T(8,128)S(1)}, f32[8,64,128]{2,1,0:T(8,128)S(1)}, u32[]{:S(2)}, u32[]{:S(2)}) collective-permute-start(f32[8,64,128]{2,1,0:T(8,128)S(1)} %collective-permute-done.4), channel_id=1, source_target_pairs={{0,16},{16,32},{32,48},{48,64},{64,80},{80,96},{96,112},{112,128},... | collective-permute-start | bytes 786440 | tf_op jit(solution)/shard_map/ppermute | solution.py:16
  35.4 9.7 %collective-permute-start = (f32[8]{0:T(128)S(1)}, f32[8]{0:T(128)S(1)}, u32[]{:S(2)}, u32[]{:S(2)}) collective-permute-start(f32[8]{0:T(128)S(1)} %fusion.48), channel_id=1, source_target_pairs={{0,16},{16,32},{32,48},{48,64},{64,80},{80,96},{96,112},{112,128},... | collective-permute-start | bytes 104 | tf_op jit(solution)/shard_map/ppermute | solution.py:16
  45.2 36.4 %collective-permute-start.6 = (f32[8,64,128]{2,1,0:T(8,128)S(1)}, f32[8,64,128]{2,1,0:T(8,128)S(1)}, u32[]{:S(2)}, u32[]{:S(2)}) collective-permute-start(f32[8,64,128]{2,1,0:T(8,128)S(1)} %multiply_add_fusion.3), channel_id=1, source_target_pairs={{0,32},{16,48},{32,64},{48,80},{64,96},{80,112},{96,128},{112,144}... | collective-permute-start | bytes 786440 | tf_op jit(solution)/shard_map/ppermute | solution.py:16
  56.3 23.3 %collective-permute-start.1 = (f32[8]{0:T(128)S(1)}, f32[8]{0:T(128)S(1)}, u32[]{:S(2)}, u32[]{:S(2)}) collective-permute-start(f32[8]{0:T(128)S(1)} %collective-permute-done), channel_id=1, source_target_pairs={{0,16},{16,32},{32,48},{48,64},{64,80},{80,96},{96,112},{112,128},... | collective-permute-start | bytes 104 | tf_op jit(solution)/shard_map/ppermute | solution.py:16
  81.7 15.6 %collective-permute-start.7 = (f32[8,64,128]{2,1,0:T(8,128)S(1)}, f32[8,64,128]{2,1,0:T(8,128)}, u32[]{:S(2)}, u32[]{:S(2)}) collective-permute-start(f32[8,64,128]{2,1,0:T(8,128)S(1)} %multiply_add_fusion.2), channel_id=1, source_target_pairs={{0,64},{16,80},{32,96},{48,112},{64,128},{80,144},{96,160},{112,17... | collective-permute-start | bytes 786440 | tf_op jit(solution)/shard_map/ppermute | solution.py:16
  84.9 14.7 %copy-start.4 = (f32[256,256]{1,0:T(8,128)S(1)}, f32[256,256]{1,0:T(8,128)}, u32[]{:S(2)}) copy-start(f32[256,256]{1,0:T(8,128)} %fusion.37) | copy-start | bytes 786436
  86.3 20.4 %copy-start.6 = (f32[8]{0:T(128)S(1)}, f32[8]{0:T(128)}, u32[]{:S(2)}) copy-start(f32[8]{0:T(128)} %param.24) | copy-start | bytes 100
  87.0 10.3 %collective-permute-start.2 = (f32[8]{0:T(128)S(1)}, f32[8]{0:T(128)S(1)}, u32[]{:S(2)}, u32[]{:S(2)}) collective-permute-start(f32[8]{0:T(128)S(1)} %mul.238), channel_id=1, source_target_pairs={{0,32},{16,48},{32,64},{48,80},{64,96},{80,112},{96,128},{112,144}... | collective-permute-start | bytes 104 | tf_op jit(solution)/shard_map/ppermute | solution.py:16
  98.3 8.3 %collective-permute-start.8 = (f32[8,64,128]{2,1,0:T(8,128)S(1)}, f32[8,64,128]{2,1,0:T(8,128)S(1)}, u32[]{:S(2)}, u32[]{:S(2)}) collective-permute-start(f32[8,64,128]{2,1,0:T(8,128)S(1)} %multiply_add_fusion.1), channel_id=1, source_target_pairs={{0,128},{16,144},{32,160},{48,176},{64,192},{80,208},{96,224},{112... | collective-permute-start | bytes 786440 | tf_op jit(solution)/shard_map/ppermute | solution.py:16
  99.6 8.1 %copy-start.3 = (bf16[512,512]{1,0:T(8,128)(2,1)S(1)}, bf16[512,512]{1,0:T(8,128)(2,1)}, u32[]{:S(2)}) copy-start(bf16[512,512]{1,0:T(8,128)(2,1)} %param.19) | copy-start | bytes 1572868
  100.4 6.3 %collective-permute-start.3 = (f32[8]{0:T(128)S(1)}, f32[8]{0:T(128)S(1)}, u32[]{:S(2)}, u32[]{:S(2)}) collective-permute-start(f32[8]{0:T(128)S(1)} %mul.239), channel_id=1, source_target_pairs={{0,64},{16,80},{32,96},{48,112},{64,128},{80,144},{96,160},{112,17... | collective-permute-start | bytes 104 | tf_op jit(solution)/shard_map/ppermute | solution.py:16
  106.6 3.5 copy-start.7
  117.1 131.9 %all-to-all-start = ((bf16[16,32,4224]{2,1,0:T(8,128)(2,1)}), bf16[16,32,4224]{2,1,0:T(8,128)(2,1)}, u32[]{:S(2)}, u32[]{:S(2)}) async-start(bf16[16,32,4224]{2,1,0:T(8,128)(2,1)} %bitcast.80), calls=%async_computation | async-start | bytes 8650752 | tf_op jit(solution)/shard_map/all_to_all | solution.py:76
  125.5 126.6 %copy-start = (bf16[32,4096]{1,0:T(8,128)(2,1)S(1)}, bf16[32,4096]{1,0:T(8,128)(2,1)}, u32[]{:S(2)}) copy-start(bf16[32,4096]{1,0:T(8,128)(2,1)} %param.27) | copy-start | bytes 786436
  125.5 126.9 %copy-start.5 = (f32[4096]{0:T(1024)S(1)}, f32[4096]{0:T(1024)}, u32[]{:S(2)}) copy-start(f32[4096]{0:T(1024)} %param.28) | copy-start | bytes 49156
  125.5 126.4 %all-gather.6.cloned.1.call-start = ((), (), s32[]{:S(2)}) async-start(), calls=%async_computation.3 | async-start | bytes 4456448 | tf_op jit(solution)/shard_map/all_gather | solution.py:103
  126.3 224.9 %all-gather.8.cloned.1.call-start = ((), (), s32[]{:S(2)}) async-start(), calls=%async_computation.4 | async-start | bytes 4456448 | tf_op jit(solution)/shard_map/all_gather | solution.py:139
Sparse Core Ops, SparseCore 0:
  9.9 89.5 all-gather.3
  128.9 113.2 all-gather.5
  253.4 97.6 all-gather.7

commit v3 on v2

--- a/solution.py
+++ b/solution.py
@@ -122,27 +122,63 @@
     )
     row_squares = jnp.sum(gated_out * gated_out, axis=1)
     gated_scaled = (gated_out * norm_gain).astype(jnp.bfloat16)
-    partial_value = jnp.dot(gated_scaled, out_full, preferred_element_type=jnp.float32)
-    width = partial_value.shape[1]
-    sq_hi = row_squares.astype(jnp.bfloat16)
-    sq_lo = (row_squares - sq_hi.astype(jnp.float32)).astype(jnp.bfloat16)
-    extra = jnp.zeros((length, 128), jnp.bfloat16).at[:, 0].set(sq_hi).at[:, 1].set(sq_lo)
-    packed = jnp.concatenate([partial_value.astype(jnp.bfloat16), extra], axis=1)
-    reduced = sum_over_head(packed)
-    reduced, down_full = lax.optimization_barrier((reduced, down_full))
-    part_rows = reduced[:, :width]
-    part_squares = reduced[:, width] + reduced[:, width + 1]
-    layer_sum = (
-        resid.astype(jnp.float32) + part_rows * lax.rsqrt(part_squares / INNER + epsilon)[:, None]
-    )
-    normed = normalize_rows(layer_sum, mlp_gain)
-    rows_piece = lax.all_gather(normed, "head", axis=0, tiled=True)
-    gate_part = jnp.dot(rows_piece, gate_weight, preferred_element_type=jnp.float32)
-    up_part = jnp.dot(rows_piece, up_weight, preferred_element_type=jnp.float32)
-    hidden = (jax.nn.silu(gate_part) * up_part).astype(jnp.bfloat16)
-    mlp_part = jnp.dot(hidden, down_full, preferred_element_type=jnp.float32)
-    mlp_rows = sum_over_head(mlp_part.astype(jnp.bfloat16))
-    return (layer_sum + mlp_rows).astype(jnp.bfloat16)
+    head_n = lax.axis_size("head")
+    chunks = 2
+    rows_per = length // head_n // chunks
+    width = out_full.shape[1]
+    gated_parts = gated_scaled.reshape(head_n, chunks, rows_per, -1)
+    square_parts = row_squares.reshape(head_n, chunks, rows_per)
+    resid_parts = resid.reshape(chunks, rows_per, -1)
+
+    def packed_rows(chunk):
+        chunk_rows = gated_parts[:, chunk].reshape(head_n * rows_per, -1)
+        chunk_squares = square_parts[:, chunk].reshape(head_n * rows_per)
+        partial_value = jnp.dot(chunk_rows, out_full, preferred_element_type=jnp.float32)
+        sq_hi = chunk_squares.astype(jnp.bfloat16)
+        sq_lo = (chunk_squares - sq_hi.astype(jnp.float32)).astype(jnp.bfloat16)
+        extra = (
+            jnp.zeros((head_n * rows_per, 128), jnp.bfloat16).at[:, 0].set(sq_hi).at[:, 1].set(sq_lo)
+        )
+        return jnp.concatenate([partial_value.astype(jnp.bfloat16), extra], axis=1)
+
+    def finish_rows(reduced, chunk):
+        part_rows = reduced[:, :width]
+        part_squares = reduced[:, width] + reduced[:, width + 1]
+        layer_sum = (
+            resid_parts[chunk].astype(jnp.float32)
+            + part_rows * lax.rsqrt(part_squares / INNER + epsilon)[:, None]
+        )
+        return layer_sum, normalize_rows(layer_sum, mlp_gain)
+
+    def mlp_rows(rows_piece, down_full):
+        gate_part = jnp.dot(rows_piece, gate_weight, preferred_element_type=jnp.float32)
+        up_part = jnp.dot(rows_piece, up_weight, preferred_element_type=jnp.float32)
+        hidden = (jax.nn.silu(gate_part) * up_part).astype(jnp.bfloat16)
+        mlp_part = jnp.dot(hidden, down_full, preferred_element_type=jnp.float32)
+        return sum_over_head(mlp_part.astype(jnp.bfloat16))
+
+    packs = [packed_rows(chunk) for chunk in range(chunks)]
+    normed_rows = []
+    sums = []
+    for chunk in range(chunks):
+        pack = packs[chunk]
+        if chunk > 0:
+            pack, normed_rows[-1] = lax.optimization_barrier((pack, normed_rows[-1]))
+        reduced = sum_over_head(pack)
+        if chunk == 0:
+            reduced, down_full = lax.optimization_barrier((reduced, down_full))
+        layer_sum, normed = finish_rows(reduced, chunk)
+        sums.append(layer_sum)
+        normed_rows.append(normed)
+    gathered = []
+    for chunk in range(chunks):
+        gathered.append(lax.all_gather(normed_rows[chunk], "head", axis=0, tiled=True))
+        if chunk + 1 < chunks:
+            gathered[-1], normed_rows[chunk + 1] = lax.optimization_barrier(
+                (gathered[-1], normed_rows[chunk + 1])
+            )
+    outs = [sums[c] + mlp_rows(gathered[c], down_full) for c in range(chunks)]
+    return jnp.concatenate(outs, axis=0).astype(jnp.bfloat16)
 
 
 def solution(mesh):

time: 476 us -> 479 us (level)
  blocking collectives: 98.7 us -> 0 us
  waiting for transfers between devices: 265 us -> 342 us
  starting transfers between devices: 50.1 us -> 62.9 us
  matrix products: 26.3 us -> 37.9 us
    all_to_all x1 -> x0, blocking collectives: 98.7 us -> none  [sum_over_head(): pieces = lax.all_to_all(pieces, 'head', 0, 0, tiled=False)]
    all_to_all x1 -> x4, waiting for transfers between devices: 122 us -> 197 us  [sum_over_head(): pieces = lax.all_to_all(pieces, 'head', 0, 0, tiled=False)]
    all_to_all x1 -> x4, starting transfers between devices: 8.41 us -> 21.6 us  [sum_over_head(): pieces = lax.all_to_all(pieces, 'head', 0, 0, tiled=False)]
    dot_general x3 -> x6, matrix products: 21.7 us -> 32.3 us  [the longest x2 15.4 us: mlp_rows(): mlp_part = jnp.dot(hidden, down_full, preferred_element_type=jnp.float32)]
    all_gather x1 -> x2, waiting for transfers between devices: 97.8 us -> 99.5 us  [shards(): lax.all_gather(normed_rows[chunk], 'head', axis=0, tiled=True)]
  transfers between devices with their start and end apart: 13 -> 17, of which waited for: 8 -> 11; matrix products, arithmetic and copies ran while one was open for 4% -> 12% of each run, Pallas kernels for 0% -> 0%
where the time goes in v3:
time: 479 us; the launch traced here: 478 us
  waiting for transfers between devices  342 us (71%)
  starting transfers between devices  62.9 us (13%)
  matrix products  37.9 us (8%)
  other arithmetic  18.1 us (4%)
  between operations  13.6 us (3%)
    all_to_all x4, waiting for transfers between devices, sum_over_head(): pieces = lax.all_to_all(pieces, 'head', 0, 0, tiled=False)  197 us
    all_gather x2, waiting for transfers between devices, shards(): lax.all_gather(normed_rows[chunk], 'head', axis=0, tiled=True)  99.5 us
    ppermute x9, waiting for transfers between devices, passed_along(): lax.ppermute(value, axis, [(source, source + steps) for source in range(i...  44 us
    ppermute x9, starting transfers between devices, passed_along(): lax.ppermute(value, axis, [(source, source + steps) for source in range(i...  41 us
    all_to_all x4, starting transfers between devices, sum_over_head(): pieces = lax.all_to_all(pieces, 'head', 0, 0, tiled=False)  21.6 us
    dot_general x2, matrix products, mlp_rows(): mlp_part = jnp.dot(hidden, down_full, preferred_element_type=jnp.float32)  15.4 us
    dot_general x2, matrix products, mlp_rows(): jnp.dot(rows_piece, gate_weight, preferred_element_type=jnp.float32)  9.94 us
  transfers between devices with their start and end apart: 17, of which 11 were waited for; matrix products, arithmetic and copies ran while one was open for 12% of the time, Pallas kernels for 0%

profile of v3, /device:TPU:8, one launch (start us, length us, event | category | flops | bytes accessed | tf_op | source)
XLA Modules:
  0.0 478.2 jit_solution(7271021649354696022)
XLA Ops:
  6.5 0.7 all-gather.5.cloned.1.call-update
  7.3 1.1 fusion.71
  8.5 0.7 neg.19
  9.2 0.8 broadcast_multiply_fusion
  13.3 1.9 collective-permute-start.4
  15.2 1.1 reduce-window.26
  16.6 9.2 %collective-permute-done.4 = f32[8,64,128]{2,1,0:T(8,128)S(1)} collective-permute-done((f32[8,64,128]{2,1,0:T(8,128)S(1)}, f32[8,64,128]{2,1,0:T(8,128)S(1)}, u32[]{:S(2)}, u32[]{:S(2)}) %collective-permute-start.4) | collective-permute-done | bytes 262176 | tf_op jit(solution)/shard_map/ppermute | solution.py:16
  25.9 6.0 %collective-permute-start.5 = (f32[8,64,128]{2,1,0:T(8,128)S(1)}, f32[8,64,128]{2,1,0:T(8,128)S(1)}, u32[]{:S(2)}, u32[]{:S(2)}) collective-permute-start(f32[8,64,128]{2,1,0:T(8,128)S(1)} %collective-permute-done.4), channel_id=1, source_target_pairs={{0,16},{16,32},{32,48},{48,64},{64,80},{80,96},{96,112},{112,128},... | collective-permute-start | bytes 786440 | tf_op jit(solution)/shard_map/ppermute | solution.py:16
  32.1 11.2 %collective-permute-start = (f32[8]{0:T(128)S(1)}, f32[8]{0:T(128)S(1)}, u32[]{:S(2)}, u32[]{:S(2)}) collective-permute-start(f32[8]{0:T(128)S(1)} %fusion.65), channel_id=1, source_target_pairs={{0,16},{16,32},{32,48},{48,64},{64,80},{80,96},{96,112},{112,128},... | collective-permute-start | bytes 104 | tf_op jit(solution)/shard_map/ppermute | solution.py:16
  44.2 10.1 %collective-permute-start.6 = (f32[8,64,128]{2,1,0:T(8,128)S(1)}, f32[8,64,128]{2,1,0:T(8,128)S(1)}, u32[]{:S(2)}, u32[]{:S(2)}) collective-permute-start(f32[8,64,128]{2,1,0:T(8,128)S(1)} %multiply_add_fusion.3), channel_id=1, source_target_pairs={{0,32},{16,48},{32,64},{48,80},{64,96},{80,112},{96,128},{112,144}... | collective-permute-start | bytes 786440 | tf_op jit(solution)/shard_map/ppermute | solution.py:16
  54.2 0.9 fusion.53
  55.5 1.9 collective-permute-start.1
  57.5 22.3 %collective-permute-done.1 = f32[8]{0:T(128)S(1)} collective-permute-done((f32[8]{0:T(128)S(1)}, f32[8]{0:T(128)S(1)}, u32[]{:S(2)}, u32[]{:S(2)}) %collective-permute-start.1) | collective-permute-done | bytes 64 | tf_op jit(solution)/shard_map/ppermute | solution.py:16
  79.7 1.0 collective-permute-done.6
  80.9 2.9 collective-permute-start.7
  84.0 0.7 compare_reduce_fusion
  85.3 1.7 convolution_bitcast_fusion.3
  87.1 3.8 collective-permute-start.2
  90.9 6.5 %collective-permute-done.2 = f32[8]{0:T(128)S(1)} collective-permute-done((f32[8]{0:T(128)S(1)}, f32[8]{0:T(128)S(1)}, u32[]{:S(2)}, u32[]{:S(2)}) %collective-permute-start.2) | collective-permute-done | bytes 64 | tf_op jit(solution)/shard_map/ppermute | solution.py:16
  97.5 1.3 collective-permute-start.8
  98.8 0.7 fusion.3
  99.5 1.9 collective-permute-start.3
  101.4 4.4 collective-permute-done.3
  105.8 0.7 fusion.2
  107.6 1.2 fusion.47
  109.2 3.4 convolution_convert_fusion.3
  112.7 1.6 pad_maximum_fusion
  114.3 8.5 %all-to-all-start = ((bf16[16,16,4224]{2,1,0:T(8,128)(2,1)}), bf16[16,16,4224]{2,1,0:T(8,128)(2,1)S(1)}, u32[]{:S(2)}, u32[]{:S(2)}) async-start(bf16[16,16,4224]{2,1,0:T(8,128)(2,1)} %bitcast.93), calls=%async_computation | async-start | bytes 4325376 | tf_op jit(solution)/shard_map/all_to_all | solution.py:76
  122.9 1.2 fusion.48
  124.4 3.4 convolution_convert_fusion.2
  127.9 1.5 pad_maximum_fusion.1
  129.4 65.8 %all-to-all-done = bf16[16,16,4224]{2,1,0:T(8,128)(2,1)S(1)} async-done(((bf16[16,16,4224]{2,1,0:T(8,128)(2,1)}), bf16[16,16,4224]{2,1,0:T(8,128)(2,1)S(1)}, u32[]{:S(2)}, u32[]{:S(2)}) %all-to-all-start) | async-done | bytes 2162720 | tf_op jit(solution)/shard_map/all_to_all | solution.py:76
  196.0 0.8 multiply_convert_fusion.10
  196.7 3.8 all-to-all-start.1
  200.6 0.7 all-gather.9.cloned.1.call-update
  201.5 85.3 %all-to-all-done.1 = bf16[16,16,4224]{2,1,0:T(8,128)(2,1)S(1)} async-done(((bf16[16,16,4224]{2,1,0:T(8,128)(2,1)}), bf16[16,16,4224]{2,1,0:T(8,128)(2,1)S(1)}, u32[]{:S(2)}, u32[]{:S(2)}) %all-to-all-start.1) | async-done | bytes 2162720 | tf_op jit(solution)/shard_map/all_to_all | solution.py:76
  287.5 0.8 multiply_convert_fusion.9
  288.3 14.6 %all-gather.9.cloned.1.call-done = bf16[256,4096]{1,0:T(8,128)(2,1)} async-done(((bf16[16,4096]{1,0:T(8,128)(2,1)}), bf16[256,4096]{1,0:T(8,128)(2,1)}) %all-gather.9.cloned.1.call-update) | async-done | bytes 2097168 | tf_op jit(solution)/shard_map/all_gather | solution.py:175
  302.9 5.0 %fusion.72 = f32[256,512]{1,0:T(8,128)} fusion(bf16[256,4096]{1,0:T(8,128)(2,1)} %all-gather.9.cloned.1.call-done, bf16[4096,512]{1,0:T(8,128)(2,1)} %param.33), kind=kOutput, calls=%fused_computation.145 | convolution fusion | flops 1073741824 | bytes 6815744 | tf_op jit(solution)/shard_map/dot_general | solution.py:154
  307.9 7.4 %convolution_convert_fusion.1 = bf16[256,4096]{1,0:T(8,128)(2,1)} fusion(bf16[512,4096]{1,0:T(8,128)(2,1)} %all-gather.7.cloned.1.call-done, bf16[256,4096]{1,0:T(8,128)(2,1)S(1)} %copy-done.8, bf16[4096,512]{1,0:T(8,128)(2,1)} %param.34, f32[256,512]{1,0:T(8,128)} %fusion.72), kind=kOutput, calls=%fused_computation.1 | convolution fusion | flops 2149318656 | bytes 13107200 | tf_op jit(solution)/shard_map/dot_general | solution.py:157
  315.3 4.8 %all-to-all-start.2 = ((bf16[16,16,4096]{2,1,0:T(8,128)(2,1)}), bf16[16,16,4096]{2,1,0:T(8,128)(2,1)S(1)}, u32[]{:S(2)}, u32[]{:S(2)}) async-start(bf16[16,16,4096]{2,1,0:T(8,128)(2,1)} %bitcast.96), calls=%async_computation.2 | async-start | bytes 4194304 | tf_op jit(solution)/shard_map/all_to_all | solution.py:76
  320.1 84.9 %all-gather.11.cloned.1.call-done = bf16[256,4096]{1,0:T(8,128)(2,1)} async-done(((bf16[16,4096]{1,0:T(8,128)(2,1)}), bf16[256,4096]{1,0:T(8,128)(2,1)}) %all-gather.11.cloned.1.call-update) | async-done | bytes 2097168 | tf_op jit(solution)/shard_map/all_gather | solution.py:175
  405.1 4.9 %fusion.73 = f32[256,512]{1,0:T(8,128)} fusion(bf16[256,4096]{1,0:T(8,128)(2,1)} %all-gather.11.cloned.1.call-done, bf16[4096,512]{1,0:T(8,128)(2,1)} %param.33), kind=kOutput, calls=%fused_computation.146 | convolution fusion | flops 1073741824 | bytes 6815744 | tf_op jit(solution)/shard_map/dot_general | solution.py:154
  410.0 8.0 %convolution_convert_fusion = bf16[256,4096]{1,0:T(8,128)(2,1)} fusion(bf16[512,4096]{1,0:T(8,128)(2,1)} %all-gather.7.cloned.1.call-done, bf16[256,4096]{1,0:T(8,128)(2,1)} %all-gather.11.cloned.1.call-done, bf16[4096,512]{1,0:T(8,128)(2,1)} %param.34, f32[256,512]{1,0:T(8,128)} %fusion.73), kind=kOutput, calls=%fused_computation | convolution fusion | flops 2149318656 | bytes 13107200 | tf_op jit(solution)/shard_map/dot_general | solution.py:157
  418.0 4.5 all-to-all-start.3
  422.8 46.1 %all-to-all-done.3 = bf16[16,16,4096]{2,1,0:T(8,128)(2,1)} async-done(((bf16[16,16,4096]{2,1,0:T(8,128)(2,1)}), bf16[16,16,4096]{2,1,0:T(8,128)(2,1)}, u32[]{:S(2)}, u32[]{:S(2)}) %all-to-all-start.3) | async-done | bytes 2097184 | tf_op jit(solution)/shard_map/all_to_all | solution.py:76
  468.9 1.9 convert_reduce_fusion.2
  471.0 0.7 pad_maximum_fusion.2
  (86 shorter events, 10.1 us)
Async XLA Ops:
  6.5 5.7 %copy-start.2 = (bf16[2,512,128]{2,1,0:T(8,128)(2,1)S(1)}, bf16[2,512,128]{2,1,0:T(8,128)(2,1)}, u32[]{:S(2)}) copy-start(bf16[2,512,128]{2,1,0:T(8,128)(2,1)} %param.24) | copy-start | bytes 786436
  6.5 102.7 %all-gather.5.cloned.1.call-start = ((), (), s32[]{:S(2)}) async-start(), calls=%async_computation.4 | async-start | bytes 4456448 | tf_op jit(solution)/shard_map/all_gather | solution.py:102
  7.3 188.2 %all-gather.7.cloned.1.call-start = ((), (), s32[]{:S(2)}) async-start(), calls=%async_computation.5 | async-start | bytes 4456448 | tf_op jit(solution)/shard_map/all_gather | solution.py:103
  8.5 4.2 copy-start.4
  12.8 71.1 %copy-start.1 = (bf16[512,512]{1,0:T(8,128)(2,1)S(1)}, bf16[512,512]{1,0:T(8,128)(2,1)}, u32[]{:S(2)}) copy-start(bf16[512,512]{1,0:T(8,128)(2,1)} %param.22) | copy-start | bytes 1572868
  13.3 12.6 %collective-permute-start.4 = (f32[8,64,128]{2,1,0:T(8,128)S(1)}, f32[8,64,128]{2,1,0:T(8,128)S(1)}, u32[]{:S(2)}, u32[]{:S(2)}) collective-permute-start(f32[8,64,128]{2,1,0:T(8,128)S(1)} %fusion.7), channel_id=1, source_target_pairs={{0,16},{16,32},{32,48},{48,64},{64,80},{80,96},{96,112},{112,128},... | collective-permute-start | bytes 786440 | tf_op jit(solution)/shard_map/ppermute | solution.py:16
  25.9 18.2 %collective-permute-start.5 = (f32[8,64,128]{2,1,0:T(8,128)S(1)}, f32[8,64,128]{2,1,0:T(8,128)S(1)}, u32[]{:S(2)}, u32[]{:S(2)}) collective-permute-start(f32[8,64,128]{2,1,0:T(8,128)S(1)} %collective-permute-done.4), channel_id=1, source_target_pairs={{0,16},{16,32},{32,48},{48,64},{64,80},{80,96},{96,112},{112,128},... | collective-permute-start | bytes 786440 | tf_op jit(solution)/shard_map/ppermute | solution.py:16
  32.1 12.0 %collective-permute-start = (f32[8]{0:T(128)S(1)}, f32[8]{0:T(128)S(1)}, u32[]{:S(2)}, u32[]{:S(2)}) collective-permute-start(f32[8]{0:T(128)S(1)} %fusion.65), channel_id=1, source_target_pairs={{0,16},{16,32},{32,48},{48,64},{64,80},{80,96},{96,112},{112,128},... | collective-permute-start | bytes 104 | tf_op jit(solution)/shard_map/ppermute | solution.py:16
  44.2 36.6 %collective-permute-start.6 = (f32[8,64,128]{2,1,0:T(8,128)S(1)}, f32[8,64,128]{2,1,0:T(8,128)S(1)}, u32[]{:S(2)}, u32[]{:S(2)}) collective-permute-start(f32[8,64,128]{2,1,0:T(8,128)S(1)} %multiply_add_fusion.3), channel_id=1, source_target_pairs={{0,32},{16,48},{32,64},{48,80},{64,96},{80,112},{96,128},{112,144}... | collective-permute-start | bytes 786440 | tf_op jit(solution)/shard_map/ppermute | solution.py:16
  55.5 24.2 %collective-permute-start.1 = (f32[8]{0:T(128)S(1)}, f32[8]{0:T(128)S(1)}, u32[]{:S(2)}, u32[]{:S(2)}) collective-permute-start(f32[8]{0:T(128)S(1)} %collective-permute-done), channel_id=1, source_target_pairs={{0,16},{16,32},{32,48},{48,64},{64,80},{80,96},{96,112},{112,128},... | collective-permute-start | bytes 104 | tf_op jit(solution)/shard_map/ppermute | solution.py:16
  80.9 16.5 %collective-permute-start.7 = (f32[8,64,128]{2,1,0:T(8,128)S(1)}, f32[8,64,128]{2,1,0:T(8,128)S(1)}, u32[]{:S(2)}, u32[]{:S(2)}) collective-permute-start(f32[8,64,128]{2,1,0:T(8,128)S(1)} %multiply_add_fusion.2), channel_id=1, source_target_pairs={{0,64},{16,80},{32,96},{48,112},{64,128},{80,144},{96,160},{112,17... | collective-permute-start | bytes 786440 | tf_op jit(solution)/shard_map/ppermute | solution.py:16
  87.1 10.3 %collective-permute-start.2 = (f32[8]{0:T(128)S(1)}, f32[8]{0:T(128)S(1)}, u32[]{:S(2)}, u32[]{:S(2)}) collective-permute-start(f32[8]{0:T(128)S(1)} %mul.272), channel_id=1, source_target_pairs={{0,32},{16,48},{32,64},{48,80},{64,96},{80,112},{96,128},{112,144}... | collective-permute-start | bytes 104 | tf_op jit(solution)/shard_map/ppermute | solution.py:16
  97.4 8.3 %copy-start.7 = (f32[8]{0:T(128)S(1)}, f32[8]{0:T(128)}, u32[]{:S(2)}) copy-start(f32[8]{0:T(128)} %param.28) | copy-start | bytes 100
  97.5 8.3 %collective-permute-start.8 = (f32[8,64,128]{2,1,0:T(8,128)S(1)}, f32[8,64,128]{2,1,0:T(8,128)S(1)}, u32[]{:S(2)}, u32[]{:S(2)}) collective-permute-start(f32[8,64,128]{2,1,0:T(8,128)S(1)} %multiply_add_fusion.1), channel_id=1, source_target_pairs={{0,128},{16,144},{32,160},{48,176},{64,192},{80,208},{96,224},{112... | collective-permute-start | bytes 786440 | tf_op jit(solution)/shard_map/ppermute | solution.py:16
  99.5 6.3 %collective-permute-start.3 = (f32[8]{0:T(128)S(1)}, f32[8]{0:T(128)S(1)}, u32[]{:S(2)}, u32[]{:S(2)}) collective-permute-start(f32[8]{0:T(128)S(1)} %mul.273), channel_id=1, source_target_pairs={{0,64},{16,80},{32,96},{48,112},{64,128},{80,144},{96,160},{112,17... | collective-permute-start | bytes 104 | tf_op jit(solution)/shard_map/ppermute | solution.py:16
  105.8 1.1 copy-start.3
  105.8 1.1 copy-start.6
  114.3 80.9 %all-to-all-start = ((bf16[16,16,4224]{2,1,0:T(8,128)(2,1)}), bf16[16,16,4224]{2,1,0:T(8,128)(2,1)S(1)}, u32[]{:S(2)}, u32[]{:S(2)}) async-start(bf16[16,16,4224]{2,1,0:T(8,128)(2,1)} %bitcast.93), calls=%async_computation | async-start | bytes 4325376 | tf_op jit(solution)/shard_map/all_to_all | solution.py:76
  129.4 66.3 %copy-start = (bf16[32,4096]{1,0:T(8,128)(2,1)S(1)}, bf16[32,4096]{1,0:T(8,128)(2,1)}, u32[]{:S(2)}) copy-start(bf16[32,4096]{1,0:T(8,128)(2,1)} %param.31) | copy-start | bytes 786436
  129.4 66.6 %copy-start.5 = (f32[4096]{0:T(1024)S(1)}, f32[4096]{0:T(1024)}, u32[]{:S(2)}) copy-start(f32[4096]{0:T(1024)} %param.32) | copy-start | bytes 49156
  196.7 90.0 %all-to-all-start.1 = ((bf16[16,16,4224]{2,1,0:T(8,128)(2,1)}), bf16[16,16,4224]{2,1,0:T(8,128)(2,1)S(1)}, u32[]{:S(2)}, u32[]{:S(2)}) async-start(bf16[16,16,4224]{2,1,0:T(8,128)(2,1)} %bitcast.92), calls=%async_computation.1 | async-start | bytes 4325376 | tf_op jit(solution)/shard_map/all_to_all | solution.py:76
  200.5 102.3 %all-gather.9.cloned.1.call-start = ((), (), s32[]{:S(2)}) async-start(), calls=%async_computation.6 | async-start | bytes 2228224 | tf_op jit(solution)/shard_map/all_gather | solution.py:175
  201.3 203.8 %all-gather.11.cloned.1.call-start = ((), (), s32[]{:S(2)}) async-start(), calls=%async_computation.7 | async-start | bytes 2228224 | tf_op jit(solution)/shard_map/all_gather | solution.py:175
  302.9 5.1 %copy-start.8 = (bf16[256,4096]{1,0:T(8,128)(2,1)S(1)}, bf16[256,4096]{1,0:T(8,128)(2,1)}, u32[]{:S(2)}) copy-start(bf16[256,4096]{1,0:T(8,128)(2,1)} %all-gather.9.cloned.1.call-done) | copy-start | bytes 6291460
  315.3 102.7 %all-to-all-start.2 = ((bf16[16,16,4096]{2,1,0:T(8,128)(2,1)}), bf16[16,16,4096]{2,1,0:T(8,128)(2,1)S(1)}, u32[]{:S(2)}, u32[]{:S(2)}) async-start(bf16[16,16,4096]{2,1,0:T(8,128)(2,1)} %bitcast.96), calls=%async_computation.2 | async-start | bytes 4194304 | tf_op jit(solution)/shard_map/all_to_all | solution.py:76
  418.0 50.9 %all-to-all-start.3 = ((bf16[16,16,4096]{2,1,0:T(8,128)(2,1)}), bf16[16,16,4096]{2,1,0:T(8,128)(2,1)}, u32[]{:S(2)}, u32[]{:S(2)}) async-start(bf16[16,16,4096]{2,1,0:T(8,128)(2,1)} %bitcast.97), calls=%async_computation.3 | async-start | bytes 4194304 | tf_op jit(solution)/shard_map/all_to_all | solution.py:76
Sparse Core Ops, SparseCore 0:
  9.9 89.2 all-gather.4
  101.7 81.0 all-gather.6
  203.1 99.6 all-gather.8
  304.5 100.5 all-gather.10

commit v4 on v3

--- a/solution.py
+++ b/solution.py
@@ -71,10 +71,17 @@
 
 
 def sum_over_head(value):
-    count = lax.axis_size("head")
-    pieces = value.reshape(count, value.shape[0] // count, value.shape[1])
-    pieces = lax.all_to_all(pieces, "head", 0, 0, tiled=False)
+    nx, nz = lax.axis_size("hx"), lax.axis_size("hz")
+    pieces = value.reshape(nx, nz, value.shape[0] // (nx * nz), value.shape[1])
+    pieces = lax.all_to_all(pieces, "hx", 0, 0, tiled=False)
+    pieces = jnp.sum(pieces.astype(jnp.float32), axis=0).astype(jnp.bfloat16)
+    pieces = lax.all_to_all(pieces, "hz", 0, 0, tiled=False)
     return jnp.sum(pieces.astype(jnp.float32), axis=0)
+
+
+def gather_over_head(value):
+    value = lax.all_gather(value, "hz", axis=0, tiled=True)
+    return lax.all_gather(value, "hx", axis=0, tiled=True)
 
 
 def normalize_rows(layer_sum, mlp_gain):
@@ -122,7 +129,7 @@
     )
     row_squares = jnp.sum(gated_out * gated_out, axis=1)
     gated_scaled = (gated_out * norm_gain).astype(jnp.bfloat16)
-    head_n = lax.axis_size("head")
+    head_n = lax.axis_size("hx") * lax.axis_size("hz")
     chunks = 2
     rows_per = length // head_n // chunks
     width = out_full.shape[1]
@@ -172,7 +179,7 @@
         normed_rows.append(normed)
     gathered = []
     for chunk in range(chunks):
-        gathered.append(lax.all_gather(normed_rows[chunk], "head", axis=0, tiled=True))
+        gathered.append(gather_over_head(normed_rows[chunk]))
         if chunk + 1 < chunks:
             gathered[-1], normed_rows[chunk + 1] = lax.optimization_barrier(
                 (gathered[-1], normed_rows[chunk + 1])
@@ -182,21 +189,24 @@
 
 
 def solution(mesh):
+    devices = mesh.devices.reshape(mesh.devices.shape[0], 4, mesh.devices.shape[1] // 4)
+    mesh = jax.sharding.Mesh(devices, ("seq", "hx", "hz"))
+    head = ("hx", "hz")
     in_specs = (
-        P("seq", "head"),
-        P("seq", "head"),
+        P("seq", head),
+        P("seq", head),
         P(None, "seq", None),
-        P("head", "seq"),
-        P("head"),
-        P("head"),
-        P("head"),
-        P("head"),
-        P("head", "seq"),
-        P(("seq", "head"), None),
+        P(head, "seq"),
+        P(head),
+        P(head),
+        P(head),
+        P(head),
+        P(head, "seq"),
+        P(("seq", "hx", "hz"), None),
         P(),
-        P(None, "head"),
-        P(None, "head"),
-        P("head", "seq"),
-    )
-    out_specs = P(("seq", "head"), None)
+        P(None, head),
+        P(None, head),
+        P(head, "seq"),
+    )
+    out_specs = P(("seq", "hx", "hz"), None)
     return jax.shard_map(shards, mesh=mesh, in_specs=in_specs, out_specs=out_specs, check_vma=False)

time: 479 us -> 396 us (0.83)
  waiting for transfers between devices: 342 us -> 180 us
  blocking collectives: 0 us -> 50.3 us
  starting transfers between devices: 62.9 us -> 90.8 us
    all_to_all x4 -> x7, waiting for transfers between devices: 197 us -> 100 us  [the longest x4 54.1 us: sum_over_head(): pieces = lax.all_to_all(pieces, 'hx', 0, 0, tiled=False)]
    all_gather x2, waiting for transfers between devices: 99.5 us -> 32.2 us  [gather_over_head(): return lax.all_gather(value, 'hx', axis=0, tiled=True)]
    all_gather x0 -> x2, blocking collectives: none -> 33.3 us  [gather_over_head(): value = lax.all_gather(value, 'hz', axis=0, tiled=True)]
    all_to_all x4 -> x7, starting transfers between devices: 21.6 us -> 46.4 us  [the longest x3 24 us: sum_over_head(): pieces = lax.all_to_all(pieces, 'hz', 0, 0, tiled=False)]
    all_to_all x0 -> x1, blocking collectives: none -> 17 us  [sum_over_head(): pieces = lax.all_to_all(pieces, 'hz', 0, 0, tiled=False)]
    all_gather x1, waiting for transfers between devices: 0.02 us -> 11 us  [shards(): lax.all_gather(down_weight, 'seq', axis=1, tiled=True)]
    ppermute x9, waiting for transfers between devices: 44 us -> 34.5 us  [passed_along(): lax.ppermute(value, axis, [(source, source + steps) for source in range(i...]
    reduce_sum x0 -> x4, other arithmetic: none -> 5.87 us  [sum_over_head(): pieces = jnp.sum(pieces.astype(jnp.float32), axis=0).astype(jnp.bfloat16)]
  transfers between devices with their start and end apart: 17 -> 20, of which waited for: 11 -> 15; matrix products, arithmetic and copies ran while one was open for 12% -> 15% of each run, Pallas kernels for 0% -> 0%
where the time goes in v4:
time: 396 us; the launch traced here: 395 us
  waiting for transfers between devices  180 us (45%)
  starting transfers between devices  90.8 us (23%)
  blocking collectives  50.3 us (13%)
  matrix products  37.9 us (10%)
  other arithmetic  18.8 us (5%)
  between operations  13.7 us (3%)
    all_to_all x4, waiting for transfers between devices, sum_over_head(): pieces = lax.all_to_all(pieces, 'hx', 0, 0, tiled=False)  54.1 us
    all_to_all x3, waiting for transfers between devices, sum_over_head(): pieces = lax.all_to_all(pieces, 'hz', 0, 0, tiled=False)  46.4 us
    ppermute x9, starting transfers between devices, passed_along(): lax.ppermute(value, axis, [(source, source + steps) for source in range(i...  44.3 us
    ppermute x9, waiting for transfers between devices, passed_along(): lax.ppermute(value, axis, [(source, source + steps) for source in range(i...  34.5 us
    all_gather x2, blocking collectives, gather_over_head(): value = lax.all_gather(value, 'hz', axis=0, tiled=True)  33.3 us
    all_gather x2, waiting for transfers between devices, gather_over_head(): return lax.all_gather(value, 'hx', axis=0, tiled=True)  32.2 us
    all_to_all x3, starting transfers between devices, sum_over_head(): pieces = lax.all_to_all(pieces, 'hz', 0, 0, tiled=False)  24 us
    all_to_all x4, starting transfers between devices, sum_over_head(): pieces = lax.all_to_all(pieces, 'hx', 0, 0, tiled=False)  22.3 us
  transfers between devices with their start and end apart: 20, of which 15 were waited for; matrix products, arithmetic and copies ran while one was open for 15% of the time, Pallas kernels for 0%

profile of v4, /device:TPU:8, one launch (start us, length us, event | category | flops | bytes accessed | tf_op | source)
XLA Modules:
  0.0 394.7 jit_solution(2596642654134442465)
XLA Ops:
  8.0 1.1 fusion.71
  12.7 1.9 collective-permute-start.4
  14.6 1.1 reduce-window.26
  16.0 9.2 %collective-permute-done.4 = f32[8,64,128]{2,1,0:T(8,128)S(1)} collective-permute-done((f32[8,64,128]{2,1,0:T(8,128)S(1)}, f32[8,64,128]{2,1,0:T(8,128)S(1)}, u32[]{:S(2)}, u32[]{:S(2)}) %collective-permute-start.4) | collective-permute-done | bytes 262176 | tf_op jit(solution)/shard_map/ppermute | solution.py:16
  25.3 6.0 %collective-permute-start.5 = (f32[8,64,128]{2,1,0:T(8,128)S(1)}, f32[8,64,128]{2,1,0:T(8,128)S(1)}, u32[]{:S(2)}, u32[]{:S(2)}) collective-permute-start(f32[8,64,128]{2,1,0:T(8,128)S(1)} %collective-permute-done.4), channel_id=1, source_target_pairs={{0,16},{16,32},{32,48},{48,64},{64,80},{80,96},{96,112},{112,128},... | collective-permute-start | bytes 786440 | tf_op jit(solution)/shard_map/ppermute | solution.py:16
  31.5 8.4 %collective-permute-start = (f32[8]{0:T(128)S(1)}, f32[8]{0:T(128)S(1)}, u32[]{:S(2)}, u32[]{:S(2)}) collective-permute-start(f32[8]{0:T(128)S(1)} %fusion.65), channel_id=1, source_target_pairs={{0,16},{16,32},{32,48},{48,64},{64,80},{80,96},{96,112},{112,128},... | collective-permute-start | bytes 104 | tf_op jit(solution)/shard_map/ppermute | solution.py:16
  40.1 1.2 collective-permute-done
  41.3 10.8 %collective-permute-start.6 = (f32[8,64,128]{2,1,0:T(8,128)S(1)}, f32[8,64,128]{2,1,0:T(8,128)S(1)}, u32[]{:S(2)}, u32[]{:S(2)}) collective-permute-start(f32[8,64,128]{2,1,0:T(8,128)S(1)} %multiply_add_fusion.3), channel_id=1, source_target_pairs={{0,32},{16,48},{32,64},{48,80},{64,96},{80,112},{96,128},{112,144}... | collective-permute-start | bytes 786440 | tf_op jit(solution)/shard_map/ppermute | solution.py:16
  53.4 1.9 collective-permute-start.1
  55.4 12.7 %collective-permute-done.1 = f32[8]{0:T(128)S(1)} collective-permute-done((f32[8]{0:T(128)S(1)}, f32[8]{0:T(128)S(1)}, u32[]{:S(2)}, u32[]{:S(2)}) %collective-permute-start.1) | collective-permute-done | bytes 64 | tf_op jit(solution)/shard_map/ppermute | solution.py:16
  68.2 3.5 collective-permute-start.7
  73.3 1.7 convolution_bitcast_fusion.3
  75.0 7.3 %collective-permute-start.2 = (f32[8]{0:T(128)S(1)}, f32[8]{0:T(128)S(1)}, u32[]{:S(2)}, u32[]{:S(2)}) collective-permute-start(f32[8]{0:T(128)S(1)} %mul.272), channel_id=1, source_target_pairs={{0,32},{16,48},{32,64},{48,80},{64,96},{80,112},{96,128},{112,144}... | collective-permute-start | bytes 104 | tf_op jit(solution)/shard_map/ppermute | solution.py:16
  82.3 3.2 collective-permute-done.2
  85.7 1.3 collective-permute-start.8
  87.7 3.1 collective-permute-start.3
  90.8 8.1 %collective-permute-done.3 = f32[8]{0:T(128)S(1)} collective-permute-done((f32[8]{0:T(128)S(1)}, f32[8]{0:T(128)S(1)}, u32[]{:S(2)}, u32[]{:S(2)}) %collective-permute-start.3) | collective-permute-done | bytes 64 | tf_op jit(solution)/shard_map/ppermute | solution.py:16
  100.8 1.2 fusion.47
  102.4 3.4 convolution_convert_fusion.3
  105.9 1.6 pad_maximum_fusion
  107.4 4.2 %all-to-all-start = ((bf16[4,4,16,4224]{3,2,1,0:T(8,128)(2,1)}), bf16[4,4,16,4224]{3,2,1,0:T(8,128)(2,1)S(1)}, u32[]{:S(2)}, u32[]{:S(2)}) async-start(bf16[4,4,16,4224]{3,2,1,0:T(8,128)(2,1)} %bitcast.92), calls=%async_computation | async-start | bytes 4325376 | tf_op jit(solution)/shard_map/all_to_all | solution.py:76
  111.8 1.2 fusion.48
  113.3 24.9 %all-to-all-done = bf16[4,4,16,4224]{3,2,1,0:T(8,128)(2,1)S(1)} async-done(((bf16[4,4,16,4224]{3,2,1,0:T(8,128)(2,1)}), bf16[4,4,16,4224]{3,2,1,0:T(8,128)(2,1)S(1)}, u32[]{:S(2)}, u32[]{:S(2)}) %all-to-all-start) | async-done | bytes 2162720 | tf_op jit(solution)/shard_map/all_to_all | solution.py:76
  138.2 1.3 reduce_sum.112
  139.5 8.9 %all-to-all-start.1 = ((bf16[4,16,4224]{2,1,0:T(8,128)(2,1)}), bf16[4,16,4224]{2,1,0:T(8,128)(2,1)S(1)}, u32[]{:S(2)}, u32[]{:S(2)}) async-start(bf16[4,16,4224]{2,1,0:T(8,128)(2,1)} %reduce_sum.112), calls=%async_computation.1 | async-start | bytes 1081344 | tf_op jit(solution)/shard_map/all_to_all | solution.py:78
  148.3 3.4 convolution_convert_fusion.2
  151.8 1.5 pad_maximum_fusion.1
  153.3 21.7 %all-to-all-done.1 = bf16[4,16,4224]{2,1,0:T(8,128)(2,1)S(1)} async-done(((bf16[4,16,4224]{2,1,0:T(8,128)(2,1)}), bf16[4,16,4224]{2,1,0:T(8,128)(2,1)S(1)}, u32[]{:S(2)}, u32[]{:S(2)}) %all-to-all-start.1) | async-done | bytes 540704 | tf_op jit(solution)/shard_map/all_to_all | solution.py:78
  175.1 11.0 %all-gather.7.cloned.1.call-done = bf16[512,4096]{1,0:T(8,128)(2,1)} async-done(((bf16[512,256]{1,0:T(8,128)(2,1)}), bf16[512,4096]{1,0:T(8,128)(2,1)}) %all-gather.7.cloned.1.call-update) | async-done | bytes 4194320 | tf_op jit(solution)/shard_map/all_gather | solution.py:110
  186.7 3.6 all-to-all-start.2
  190.4 16.8 %all_gather.20 = bf16[64,4096]{1,0:T(8,128)(2,1)} all-gather(bf16[16,4096]{1,0:T(8,128)(2,1)S(1)} %multiply_convert_fusion.10), channel_id=1, replica_groups=mesh['seq'=16,'hx'=4,'hz'=4] {'hz'}, dimensions={0}, use_global_device_ids=true | all-gather | bytes 655360 | tf_op jit(solution)/shard_map/all_gather | solution.py:83
  207.3 10.8 %all-to-all-done.2 = bf16[4,4,16,4224]{3,2,1,0:T(8,128)(2,1)S(1)} async-done(((bf16[4,4,16,4224]{3,2,1,0:T(8,128)(2,1)}), bf16[4,4,16,4224]{3,2,1,0:T(8,128)(2,1)S(1)}, u32[]{:S(2)}, u32[]{:S(2)}) %all-to-all-start.2) | async-done | bytes 2162720 | tf_op jit(solution)/shard_map/all_to_all | solution.py:76
  218.5 17.0 %all_to_all.40 = bf16[4,16,4224]{2,1,0:T(8,128)(2,1)S(1)} all-to-all(bf16[4,16,4224]{2,1,0:T(8,128)(2,1)S(1)} %reduce_sum.115), channel_id=1, replica_groups=mesh['seq'=16,'hx'=4,'hz'=4] {'hz'}, dimensions={0} | all-to-all | bytes 1081344 | tf_op jit(solution)/shard_map/all_to_all | solution.py:78
  237.2 16.5 %all_gather.22 = bf16[64,4096]{1,0:T(8,128)(2,1)} all-gather(bf16[16,4096]{1,0:T(8,128)(2,1)S(1)} %multiply_convert_fusion.9), channel_id=1, replica_groups=mesh['seq'=16,'hx'=4,'hz'=4] {'hz'}, dimensions={0}, use_global_device_ids=true | all-gather | bytes 655360 | tf_op jit(solution)/shard_map/all_gather | solution.py:83
  253.7 5.1 %fusion.72 = f32[256,512]{1,0:T(8,128)} fusion(bf16[256,4096]{1,0:T(8,128)(2,1)} %all-gather.9.cloned.1.call-done, bf16[4096,512]{1,0:T(8,128)(2,1)} %param.33), kind=kOutput, calls=%fused_computation.145 | convolution fusion | flops 1073741824 | bytes 6815744 | tf_op jit(solution)/shard_map/dot_general | solution.py:161
  258.8 7.4 %convolution_convert_fusion.1 = bf16[256,4096]{1,0:T(8,128)(2,1)} fusion(bf16[512,4096]{1,0:T(8,128)(2,1)} %all-gather.7.cloned.1.call-done, bf16[256,4096]{1,0:T(8,128)(2,1)S(1)} %copy-done.10, bf16[4096,512]{1,0:T(8,128)(2,1)} %param.34, f32[256,512]{1,0:T(8,128)} %fusion.72), kind=kOutput, calls=%fused_computation.1 | convolution fusion | flops 2149318656 | bytes 13107200 | tf_op jit(solution)/shard_map/dot_general | solution.py:164
  266.2 3.6 all-to-all-start.4
  269.8 31.1 %all-gather.11.cloned.1.call-done = bf16[256,4096]{1,0:T(8,128)(2,1)} async-done(((bf16[64,4096]{1,0:T(8,128)(2,1)}), bf16[256,4096]{1,0:T(8,128)(2,1)}) %all-gather.11.cloned.1.call-update) | async-done | bytes 2097168 | tf_op jit(solution)/shard_map/all_gather | solution.py:84
  300.9 4.9 %fusion.73 = f32[256,512]{1,0:T(8,128)} fusion(bf16[256,4096]{1,0:T(8,128)(2,1)} %all-gather.11.cloned.1.call-done, bf16[4096,512]{1,0:T(8,128)(2,1)} %param.33), kind=kOutput, calls=%fused_computation.146 | convolution fusion | flops 1073741824 | bytes 6815744 | tf_op jit(solution)/shard_map/dot_general | solution.py:161
  305.8 8.0 %convolution_convert_fusion = bf16[256,4096]{1,0:T(8,128)(2,1)} fusion(bf16[512,4096]{1,0:T(8,128)(2,1)} %all-gather.7.cloned.1.call-done, bf16[256,4096]{1,0:T(8,128)(2,1)} %all-gather.11.cloned.1.call-done, bf16[4096,512]{1,0:T(8,128)(2,1)} %param.34, f32[256,512]{1,0:T(8,128)} %fusion.73), kind=kOutput, calls=%fused_computation | convolution fusion | flops 2149318656 | bytes 13107200 | tf_op jit(solution)/shard_map/dot_general | solution.py:164
  313.9 10.9 %all-to-all-start.6 = ((bf16[4,4,16,4096]{3,2,1,0:T(8,128)(2,1)}), bf16[4,4,16,4096]{3,2,1,0:T(8,128)(2,1)}, u32[]{:S(2)}, u32[]{:S(2)}) async-start(bf16[4,4,16,4096]{3,2,1,0:T(8,128)(2,1)} %bitcast.96), calls=%async_computation.6 | async-start | bytes 4194304 | tf_op jit(solution)/shard_map/all_to_all | solution.py:76
  324.8 1.3 reduce_sum.118
  326.0 18.4 %all-to-all-done.6 = bf16[4,4,16,4096]{3,2,1,0:T(8,128)(2,1)} async-done(((bf16[4,4,16,4096]{3,2,1,0:T(8,128)(2,1)}), bf16[4,4,16,4096]{3,2,1,0:T(8,128)(2,1)}, u32[]{:S(2)}, u32[]{:S(2)}) %all-to-all-start.6) | async-done | bytes 2097184 | tf_op jit(solution)/shard_map/all_to_all | solution.py:76
  344.5 11.7 %all-to-all-start.5 = ((bf16[4,16,4096]{2,1,0:T(8,128)(2,1)}), bf16[4,16,4096]{2,1,0:T(8,128)(2,1)S(1)}, u32[]{:S(2)}, u32[]{:S(2)}) async-start(bf16[4,16,4096]{2,1,0:T(8,128)(2,1)} %reduce_sum.118), calls=%async_computation.5 | async-start | bytes 1048576 | tf_op jit(solution)/shard_map/all_to_all | solution.py:78
  356.1 2.9 reduce_sum.120
  359.0 10.7 %all-to-all-done.5 = bf16[4,16,4096]{2,1,0:T(8,128)(2,1)S(1)} async-done(((bf16[4,16,4096]{2,1,0:T(8,128)(2,1)}), bf16[4,16,4096]{2,1,0:T(8,128)(2,1)S(1)}, u32[]{:S(2)}, u32[]{:S(2)}) %all-to-all-start.5) | async-done | bytes 524320 | tf_op jit(solution)/shard_map/all_to_all | solution.py:78
  369.7 3.5 all-to-all-start.7
  373.3 13.9 %all-to-all-done.7 = bf16[4,16,4096]{2,1,0:T(8,128)(2,1)S(1)} async-done(((bf16[4,16,4096]{2,1,0:T(8,128)(2,1)}), bf16[4,16,4096]{2,1,0:T(8,128)(2,1)S(1)}, u32[]{:S(2)}, u32[]{:S(2)}) %all-to-all-start.7) | async-done | bytes 524320 | tf_op jit(solution)/shard_map/all_to_all | solution.py:78
  (105 shorter events, 15.8 us)
Async XLA Ops:
  6.5 2.7 copy-start.2
  6.5 2.7 copy-start.11
  6.5 2.8 copy-start.6
  6.5 2.8 copy-start.8
  6.5 95.9 %all-gather.5.cloned.1.call-start = ((), (), s32[]{:S(2)}) async-start(), calls=%async_computation.8 | async-start | bytes 4456448 | tf_op jit(solution)/shard_map/all_gather | solution.py:109
  7.3 178.9 %all-gather.7.cloned.1.call-start = ((), (), s32[]{:S(2)}) async-start(), calls=%async_computation.9 | async-start | bytes 4456448 | tf_op jit(solution)/shard_map/all_gather | solution.py:110
  9.2 2.9 copy-start.4
  12.1 59.6 %copy-start.1 = (bf16[512,512]{1,0:T(8,128)(2,1)S(1)}, bf16[512,512]{1,0:T(8,128)(2,1)}, u32[]{:S(2)}) copy-start(bf16[512,512]{1,0:T(8,128)(2,1)} %param.22) | copy-start | bytes 1572868
  12.7 12.6 %collective-permute-start.4 = (f32[8,64,128]{2,1,0:T(8,128)S(1)}, f32[8,64,128]{2,1,0:T(8,128)S(1)}, u32[]{:S(2)}, u32[]{:S(2)}) collective-permute-start(f32[8,64,128]{2,1,0:T(8,128)S(1)} %fusion.7), channel_id=1, source_target_pairs={{0,16},{16,32},{32,48},{48,64},{64,80},{80,96},{96,112},{112,128},... | collective-permute-start | bytes 786440 | tf_op jit(solution)/shard_map/ppermute | solution.py:16
  25.3 16.0 %collective-permute-start.5 = (f32[8,64,128]{2,1,0:T(8,128)S(1)}, f32[8,64,128]{2,1,0:T(8,128)S(1)}, u32[]{:S(2)}, u32[]{:S(2)}) collective-permute-start(f32[8,64,128]{2,1,0:T(8,128)S(1)} %collective-permute-done.4), channel_id=1, source_target_pairs={{0,16},{16,32},{32,48},{48,64},{64,80},{80,96},{96,112},{112,128},... | collective-permute-start | bytes 786440 | tf_op jit(solution)/shard_map/ppermute | solution.py:16
  31.5 9.8 %collective-permute-start = (f32[8]{0:T(128)S(1)}, f32[8]{0:T(128)S(1)}, u32[]{:S(2)}, u32[]{:S(2)}) collective-permute-start(f32[8]{0:T(128)S(1)} %fusion.65), channel_id=1, source_target_pairs={{0,16},{16,32},{32,48},{48,64},{64,80},{80,96},{96,112},{112,128},... | collective-permute-start | bytes 104 | tf_op jit(solution)/shard_map/ppermute | solution.py:16
  41.3 26.8 %collective-permute-start.6 = (f32[8,64,128]{2,1,0:T(8,128)S(1)}, f32[8,64,128]{2,1,0:T(8,128)S(1)}, u32[]{:S(2)}, u32[]{:S(2)}) collective-permute-start(f32[8,64,128]{2,1,0:T(8,128)S(1)} %multiply_add_fusion.3), channel_id=1, source_target_pairs={{0,32},{16,48},{32,64},{48,80},{64,96},{80,112},{96,128},{112,144}... | collective-permute-start | bytes 786440 | tf_op jit(solution)/shard_map/ppermute | solution.py:16
  53.4 14.6 %collective-permute-start.1 = (f32[8]{0:T(128)S(1)}, f32[8]{0:T(128)S(1)}, u32[]{:S(2)}, u32[]{:S(2)}) collective-permute-start(f32[8]{0:T(128)S(1)} %collective-permute-done), channel_id=1, source_target_pairs={{0,16},{16,32},{32,48},{48,64},{64,80},{80,96},{96,112},{112,128},... | collective-permute-start | bytes 104 | tf_op jit(solution)/shard_map/ppermute | solution.py:16
  68.2 17.3 %collective-permute-start.7 = (f32[8,64,128]{2,1,0:T(8,128)S(1)}, f32[8,64,128]{2,1,0:T(8,128)S(1)}, u32[]{:S(2)}, u32[]{:S(2)}) collective-permute-start(f32[8,64,128]{2,1,0:T(8,128)S(1)} %multiply_add_fusion.2), channel_id=1, source_target_pairs={{0,64},{16,80},{32,96},{48,112},{64,128},{80,144},{96,160},{112,17... | collective-permute-start | bytes 786440 | tf_op jit(solution)/shard_map/ppermute | solution.py:16
  75.0 10.5 %collective-permute-start.2 = (f32[8]{0:T(128)S(1)}, f32[8]{0:T(128)S(1)}, u32[]{:S(2)}, u32[]{:S(2)}) collective-permute-start(f32[8]{0:T(128)S(1)} %mul.272), channel_id=1, source_target_pairs={{0,32},{16,48},{32,64},{48,80},{64,96},{80,112},{96,128},{112,144}... | collective-permute-start | bytes 104 | tf_op jit(solution)/shard_map/ppermute | solution.py:16
  85.6 13.3 %copy-start.9 = (f32[8]{0:T(128)S(1)}, f32[8]{0:T(128)}, u32[]{:S(2)}) copy-start(f32[8]{0:T(128)} %param.28) | copy-start | bytes 100
  85.7 13.3 %collective-permute-start.8 = (f32[8,64,128]{2,1,0:T(8,128)S(1)}, f32[8,64,128]{2,1,0:T(8,128)S(1)}, u32[]{:S(2)}, u32[]{:S(2)}) collective-permute-start(f32[8,64,128]{2,1,0:T(8,128)S(1)} %multiply_add_fusion.1), channel_id=1, source_target_pairs={{0,128},{16,144},{32,160},{48,176},{64,192},{80,208},{96,224},{112... | collective-permute-start | bytes 786440 | tf_op jit(solution)/shard_map/ppermute | solution.py:16
  87.7 11.3 %collective-permute-start.3 = (f32[8]{0:T(128)S(1)}, f32[8]{0:T(128)S(1)}, u32[]{:S(2)}, u32[]{:S(2)}) collective-permute-start(f32[8]{0:T(128)S(1)} %mul.273), channel_id=1, source_target_pairs={{0,64},{16,80},{32,96},{48,112},{64,128},{80,144},{96,160},{112,17... | collective-permute-start | bytes 104 | tf_op jit(solution)/shard_map/ppermute | solution.py:16
  99.0 1.1 copy-start.3
  99.0 1.1 copy-start.7
  107.4 30.7 %all-to-all-start = ((bf16[4,4,16,4224]{3,2,1,0:T(8,128)(2,1)}), bf16[4,4,16,4224]{3,2,1,0:T(8,128)(2,1)S(1)}, u32[]{:S(2)}, u32[]{:S(2)}) async-start(bf16[4,4,16,4224]{3,2,1,0:T(8,128)(2,1)} %bitcast.92), calls=%async_computation | async-start | bytes 4325376 | tf_op jit(solution)/shard_map/all_to_all | solution.py:76
  139.5 35.6 %all-to-all-start.1 = ((bf16[4,16,4224]{2,1,0:T(8,128)(2,1)}), bf16[4,16,4224]{2,1,0:T(8,128)(2,1)S(1)}, u32[]{:S(2)}, u32[]{:S(2)}) async-start(bf16[4,16,4224]{2,1,0:T(8,128)(2,1)} %reduce_sum.112), calls=%async_computation.1 | async-start | bytes 1081344 | tf_op jit(solution)/shard_map/all_to_all | solution.py:78
  151.8 34.6 %copy-start = (bf16[32,4096]{1,0:T(8,128)(2,1)S(1)}, bf16[32,4096]{1,0:T(8,128)(2,1)}, u32[]{:S(2)}) copy-start(bf16[32,4096]{1,0:T(8,128)(2,1)} %param.31) | copy-start | bytes 786436
  151.8 34.8 %copy-start.5 = (f32[4096]{0:T(1024)S(1)}, f32[4096]{0:T(1024)}, u32[]{:S(2)}) copy-start(f32[4096]{0:T(1024)} %param.32) | copy-start | bytes 49156
  186.7 31.3 %all-to-all-start.2 = ((bf16[4,4,16,4224]{3,2,1,0:T(8,128)(2,1)}), bf16[4,4,16,4224]{3,2,1,0:T(8,128)(2,1)S(1)}, u32[]{:S(2)}, u32[]{:S(2)}) async-start(bf16[4,4,16,4224]{3,2,1,0:T(8,128)(2,1)} %bitcast.29), calls=%async_computation.2 | async-start | bytes 4325376 | tf_op jit(solution)/shard_map/all_to_all | solution.py:76
  190.3 46.8 %all-gather.9.cloned.1.call-start = ((), (), s32[]{:S(2)}) async-start(), calls=%async_computation.10 | async-start | bytes 2621440 | tf_op jit(solution)/shard_map/all_gather | solution.py:84
  207.2 93.7 %all-gather.11.cloned.1.call-start = ((), (), s32[]{:S(2)}) async-start(), calls=%async_computation.11 | async-start | bytes 2621440 | tf_op jit(solution)/shard_map/all_gather | solution.py:84
  253.7 5.1 %copy-start.10 = (bf16[256,4096]{1,0:T(8,128)(2,1)S(1)}, bf16[256,4096]{1,0:T(8,128)(2,1)}, u32[]{:S(2)}) copy-start(bf16[256,4096]{1,0:T(8,128)(2,1)} %all-gather.9.cloned.1.call-done) | copy-start | bytes 6291460
  266.2 47.7 %all-to-all-start.4 = ((bf16[4,4,16,4096]{3,2,1,0:T(8,128)(2,1)}), bf16[4,4,16,4096]{3,2,1,0:T(8,128)(2,1)S(1)}, u32[]{:S(2)}, u32[]{:S(2)}) async-start(bf16[4,4,16,4096]{3,2,1,0:T(8,128)(2,1)} %bitcast.95), calls=%async_computation.4 | async-start | bytes 4194304 | tf_op jit(solution)/shard_map/all_to_all | solution.py:76
  313.9 30.6 %all-to-all-start.6 = ((bf16[4,4,16,4096]{3,2,1,0:T(8,128)(2,1)}), bf16[4,4,16,4096]{3,2,1,0:T(8,128)(2,1)}, u32[]{:S(2)}, u32[]{:S(2)}) async-start(bf16[4,4,16,4096]{3,2,1,0:T(8,128)(2,1)} %bitcast.96), calls=%async_computation.6 | async-start | bytes 4194304 | tf_op jit(solution)/shard_map/all_to_all | solution.py:76
  344.5 25.3 %all-to-all-start.5 = ((bf16[4,16,4096]{2,1,0:T(8,128)(2,1)}), bf16[4,16,4096]{2,1,0:T(8,128)(2,1)S(1)}, u32[]{:S(2)}, u32[]{:S(2)}) async-start(bf16[4,16,4096]{2,1,0:T(8,128)(2,1)} %reduce_sum.118), calls=%async_computation.5 | async-start | bytes 1048576 | tf_op jit(solution)/shard_map/all_to_all | solution.py:78
  369.7 17.5 %all-to-all-start.7 = ((bf16[4,16,4096]{2,1,0:T(8,128)(2,1)}), bf16[4,16,4096]{2,1,0:T(8,128)(2,1)S(1)}, u32[]{:S(2)}, u32[]{:S(2)}) async-start(bf16[4,16,4096]{2,1,0:T(8,128)(2,1)} %reduce_sum.120), calls=%async_computation.7 | async-start | bytes 1048576 | tf_op jit(solution)/shard_map/all_to_all | solution.py:78
Sparse Core Ops, SparseCore 0:
  9.9 89.1 all-gather.4
  101.7 84.4 all-gather.6
  207.3 29.7 all-gather.8
  253.8 47.0 all-gather.10

commit v5 on v4

--- a/solution.py
+++ b/solution.py
@@ -10,8 +10,13 @@
 epsilon = 1e-05
 
 
+SEQ = ("sy", "sz", "sc")
+
+
 def passed_along(value, axis, steps):
-    count = lax.axis_size(axis)
+    count = 1
+    for name in axis:
+        count *= lax.axis_size(name)
     initial, last = (max(0, -steps), min(count, count - steps))
     return lax.ppermute(value, axis, [(source, source + steps) for source in range(initial, last)])
 
@@ -55,14 +60,16 @@
 
 
 def entering_state(group_decay, local_state):
-    count = lax.axis_size("seq")
-    dec = passed_along(group_decay, "seq", 1)
-    st = passed_along(local_state, "seq", 1)
+    count = 1
+    for name in SEQ:
+        count *= lax.axis_size(name)
+    dec = passed_along(group_decay, SEQ, 1)
+    st = passed_along(local_state, SEQ, 1)
     step = 1
     while step < count:
-        sp = passed_along(st, "seq", step)
+        sp = passed_along(st, SEQ, step)
         if step * 2 < count:
-            dp = passed_along(dec, "seq", step)
+            dp = passed_along(dec, SEQ, step)
         st = dec[:, None, None] * sp + st
         if step * 2 < count:
             dec = dp * dec
@@ -77,6 +84,14 @@
     pieces = jnp.sum(pieces.astype(jnp.float32), axis=0).astype(jnp.bfloat16)
     pieces = lax.all_to_all(pieces, "hz", 0, 0, tiled=False)
     return jnp.sum(pieces.astype(jnp.float32), axis=0)
+
+
+def gather_seq_columns(value):
+    rows, cols = value.shape
+    value = lax.all_gather(value, ("sy", "sz"), axis=0, tiled=False)
+    value = lax.all_gather(value, "sc", axis=0, tiled=False)
+    value = value.transpose(2, 1, 0, 3)
+    return value.reshape(rows, -1)
 
 
 def gather_over_head(value):
@@ -106,8 +121,8 @@
     down_weight,
 ):
     out_full, down_full = (
-        lax.all_gather(out_weight, "seq", axis=1, tiled=True),
-        lax.all_gather(down_weight, "seq", axis=1, tiled=True),
+        gather_seq_columns(out_weight),
+        gather_seq_columns(down_weight),
     )
     head_count = dt_raw.shape[0]
     length = dt_raw.shape[1]
@@ -189,24 +204,25 @@
 
 
 def solution(mesh):
-    devices = mesh.devices.reshape(mesh.devices.shape[0], 4, mesh.devices.shape[1] // 4)
-    mesh = jax.sharding.Mesh(devices, ("seq", "hx", "hz"))
+    seq_n, head_n = mesh.devices.shape
+    devices = mesh.devices.reshape(seq_n // 4, 2, 2, 4, head_n // 4)
+    mesh = jax.sharding.Mesh(devices, ("sy", "sz", "sc", "hx", "hz"))
     head = ("hx", "hz")
     in_specs = (
-        P("seq", head),
-        P("seq", head),
-        P(None, "seq", None),
-        P(head, "seq"),
-        P(head),
-        P(head),
-        P(head),
-        P(head),
-        P(head, "seq"),
-        P(("seq", "hx", "hz"), None),
+        P(SEQ, head),
+        P(SEQ, head),
+        P(None, SEQ, None),
+        P(head, SEQ),
+        P(head),
+        P(head),
+        P(head),
+        P(head),
+        P(head, SEQ),
+        P(SEQ + head, None),
         P(),
         P(None, head),
         P(None, head),
-        P(head, "seq"),
-    )
-    out_specs = P(("seq", "hx", "hz"), None)
+        P(head, SEQ),
+    )
+    out_specs = P(SEQ + head, None)
     return jax.shard_map(shards, mesh=mesh, in_specs=in_specs, out_specs=out_specs, check_vma=False)

time: 396 us -> 461 us (1.16)
  waiting for transfers between devices: 180 us -> 255 us
  starting transfers between devices: 90.8 us -> 67.5 us
  local copies, waits for them, and re-layouts: 3.53 us -> 15.5 us
    all_gather x2 -> x4, waiting for transfers between devices: 11.1 us -> 89.4 us  [the longest x2 77.4 us: gather_seq_columns(): value = lax.all_gather(value, ('sy', 'sz'), axis=0, tiled=False)]
    all_to_all x3, waiting for transfers between devices: 46.4 us -> 27.3 us  [sum_over_head(): pieces = lax.all_to_all(pieces, 'hz', 0, 0, tiled=False)]
    ppermute x9, starting transfers between devices: 44.3 us -> 27.9 us  [passed_along(): lax.ppermute(value, axis, [(source, source + steps) for source in range(i...]
    transpose x0 -> x2, local copies, waits for them, and re-layouts: none -> 13 us  [gather_seq_columns(): value = value.transpose(2, 1, 0, 3)]
    all_gather x2, waiting for transfers between devices: 32.2 us -> 40.5 us  [gather_over_head(): return lax.all_gather(value, 'hx', axis=0, tiled=True)]
    ppermute x9, waiting for transfers between devices: 34.5 us -> 41 us  [passed_along(): lax.ppermute(value, axis, [(source, source + steps) for source in range(i...]
    all_to_all x3, starting transfers between devices: 24 us -> 17.9 us  [sum_over_head(): pieces = lax.all_to_all(pieces, 'hz', 0, 0, tiled=False)]
  transfers between devices with their start and end apart: 20 -> 22, of which waited for: 15 -> 16; matrix products, arithmetic and copies ran while one was open for 15% -> 16% of each run, Pallas kernels for 0% -> 0%
where the time goes in v5:
time: 461 us; the launch traced here: 460 us
  waiting for transfers between devices  255 us (55%)
  starting transfers between devices  67.5 us (15%)
  blocking collectives  48.9 us (11%)
  matrix products  37.9 us (8%)
  other arithmetic  21.5 us (5%)
  local copies, waits for them, and re-layouts  15.5 us (3%)
  between operations  14 us (3%)
    all_gather x2, waiting for transfers between devices, gather_seq_columns(): value = lax.all_gather(value, ('sy', 'sz'), axis=0, tiled=False)  77.4 us
    all_to_all x4, waiting for transfers between devices, sum_over_head(): pieces = lax.all_to_all(pieces, 'hx', 0, 0, tiled=False)  54.8 us
    ppermute x9, waiting for transfers between devices, passed_along(): lax.ppermute(value, axis, [(source, source + steps) for source in range(i...  41 us
    all_gather x2, waiting for transfers between devices, gather_over_head(): return lax.all_gather(value, 'hx', axis=0, tiled=True)  40.5 us
    all_gather x2, blocking collectives, gather_over_head(): value = lax.all_gather(value, 'hz', axis=0, tiled=True)  33 us
    ppermute x9, starting transfers between devices, passed_along(): lax.ppermute(value, axis, [(source, source + steps) for source in range(i...  27.9 us
    all_to_all x3, waiting for transfers between devices, sum_over_head(): pieces = lax.all_to_all(pieces, 'hz', 0, 0, tiled=False)  27.3 us
    all_to_all x4, starting transfers between devices, sum_over_head(): pieces = lax.all_to_all(pieces, 'hx', 0, 0, tiled=False)  21.3 us
  transfers between devices with their start and end apart: 22, of which 16 were waited for; matrix products, arithmetic and copies ran while one was open for 16% of the time, Pallas kernels for 0%

profile of v5, /device:TPU:8, one launch (start us, length us, event | category | flops | bytes accessed | tf_op | source)
XLA Modules:
  0.0 459.8 jit_solution(14137342168134795010)
XLA Ops:
  11.1 77.4 %all-gather.15.cloned.1.call-done = bf16[4096,256]{1,0:T(8,128)(2,1)} async-done(((bf16[512,256]{1,0:T(8,128)(2,1)}), bf16[4096,256]{1,0:T(8,128)(2,1)}) %all-gather.15.cloned.1.call-update) | async-done | bytes 2097168 | tf_op jit(solution)/shard_map/all_gather | solution.py:91
  90.5 1.9 collective-permute-start.4
  93.9 11.4 %collective-permute-done.4 = f32[8,64,128]{2,1,0:T(8,128)S(1)} collective-permute-done((f32[8,64,128]{2,1,0:T(8,128)S(1)}, f32[8,64,128]{2,1,0:T(8,128)S(1)}, u32[]{:S(2)}, u32[]{:S(2)}) %collective-permute-start.4) | collective-permute-done | bytes 262176 | tf_op jit(solution)/shard_map/ppermute | solution.py:21
  105.3 1.9 collective-permute-start.5
  107.4 1.9 collective-permute-start
  109.5 10.9 %collective-permute-done = f32[8]{0:T(128)S(1)} collective-permute-done((f32[8]{0:T(128)S(1)}, f32[8]{0:T(128)S(1)}, u32[]{:S(2)}, u32[]{:S(2)}) %collective-permute-start) | collective-permute-done | bytes 64 | tf_op jit(solution)/shard_map/ppermute | solution.py:21
  120.5 1.9 collective-permute-start.6
  123.7 1.9 collective-permute-start.1
  125.7 7.9 %collective-permute-done.1 = f32[8]{0:T(128)S(1)} collective-permute-done((f32[8]{0:T(128)S(1)}, f32[8]{0:T(128)S(1)}, u32[]{:S(2)}, u32[]{:S(2)}) %collective-permute-start.1) | collective-permute-done | bytes 64 | tf_op jit(solution)/shard_map/ppermute | solution.py:21
  133.5 3.8 collective-permute-done.6
  137.4 5.1 %collective-permute-start.7 = (f32[8,64,128]{2,1,0:T(8,128)S(1)}, f32[8,64,128]{2,1,0:T(8,128)}, u32[]{:S(2)}, u32[]{:S(2)}) collective-permute-start(f32[8,64,128]{2,1,0:T(8,128)S(1)} %multiply_add_fusion.2), channel_id=1, source_target_pairs={{0,64},{16,80},{32,96},{48,112},{64,128},{80,144},{96,160},{112,17... | collective-permute-start | bytes 786440 | tf_op jit(solution)/shard_map/ppermute | solution.py:21
  144.2 1.6 convolution_bitcast_fusion.3
  145.8 7.2 %collective-permute-start.2 = (f32[8]{0:T(128)S(1)}, f32[8]{0:T(128)S(1)}, u32[]{:S(2)}, u32[]{:S(2)}) collective-permute-start(f32[8]{0:T(128)S(1)} %mul.272), channel_id=1, source_target_pairs={{0,32},{16,48},{32,64},{48,80},{64,96},{80,112},{96,128},{112,144}... | collective-permute-start | bytes 104 | tf_op jit(solution)/shard_map/ppermute | solution.py:21
  153.0 3.5 collective-permute-done.2
  157.5 4.1 collective-permute-start.8
  161.6 1.6 fusion.3
  163.2 1.9 collective-permute-start.3
  165.1 3.5 collective-permute-done.3
  168.7 2.0 fusion.2
  173.5 11.9 %all-gather.17.cloned.1.call-done = bf16[16,512,256]{2,1,0:T(8,128)(2,1)} async-done(((bf16[8,512,256]{2,1,0:T(8,128)(2,1)}), bf16[16,512,256]{2,1,0:T(8,128)(2,1)}) %all-gather.17.cloned.1.call-update) | async-done | bytes 4194320 | tf_op jit(solution)/shard_map/all_gather | solution.py:92
  185.4 6.5 %copy.52 = bf16[512,8,2,256]{0,3,2,1:T(8,128)(2,1)} copy(bf16[512,8,2,256]{3,0,1,2:T(8,128)(2,1)} %bitcast.105) | data formatting | bytes 8388608 | tf_op jit(solution)/shard_map/transpose | solution.py:93
  191.9 3.5 convolution_convert_fusion.3
  196.9 4.2 all-to-all-start
  202.9 25.7 %all-to-all-done = bf16[4,4,16,4224]{3,2,1,0:T(8,128)(2,1)S(1)} async-done(((bf16[4,4,16,4224]{3,2,1,0:T(8,128)(2,1)}), bf16[4,4,16,4224]{3,2,1,0:T(8,128)(2,1)S(1)}, u32[]{:S(2)}, u32[]{:S(2)}) %all-to-all-start) | async-done | bytes 2162720 | tf_op jit(solution)/shard_map/all_to_all | solution.py:83
  229.9 4.8 %all-to-all-start.1 = ((bf16[4,16,4224]{2,1,0:T(8,128)(2,1)}), bf16[4,16,4224]{2,1,0:T(8,128)(2,1)S(1)}, u32[]{:S(2)}, u32[]{:S(2)}) async-start(bf16[4,16,4224]{2,1,0:T(8,128)(2,1)} %reduce_sum.112), calls=%async_computation.1 | async-start | bytes 1081344 | tf_op jit(solution)/shard_map/all_to_all | solution.py:85
  234.7 3.5 convolution_convert_fusion.2
  238.2 6.5 %copy.55 = bf16[512,8,2,256]{0,3,2,1:T(8,128)(2,1)} copy(bf16[512,8,2,256]{3,0,1,2:T(8,128)(2,1)} %bitcast.106) | data formatting | bytes 8388608 | tf_op jit(solution)/shard_map/transpose | solution.py:93
  244.7 1.5 pad_maximum_fusion.1
  246.3 2.6 all-to-all-done.1
  249.5 3.6 all-to-all-start.2
  253.2 16.7 %all_gather.44 = bf16[64,4096]{1,0:T(8,128)(2,1)} all-gather(bf16[16,4096]{1,0:T(8,128)(2,1)S(1)} %multiply_convert_fusion.10), channel_id=1, replica_groups=mesh['sy'=4,'sz'=2,'sc'=2,'hx'=4,'hz'=4] {'hz'}, dimensions={0}, use_global_device_ids=true | all-gather | bytes 655360 | tf_op jit(solution)/shard_map/all_gather | solution.py:98
  270.2 9.6 %all-to-all-done.2 = bf16[4,4,16,4224]{3,2,1,0:T(8,128)(2,1)S(1)} async-done(((bf16[4,4,16,4224]{3,2,1,0:T(8,128)(2,1)}), bf16[4,4,16,4224]{3,2,1,0:T(8,128)(2,1)S(1)}, u32[]{:S(2)}, u32[]{:S(2)}) %all-to-all-start.2) | async-done | bytes 2162720 | tf_op jit(solution)/shard_map/all_to_all | solution.py:83
  280.2 15.9 %all_to_all.40 = bf16[4,16,4224]{2,1,0:T(8,128)(2,1)S(1)} all-to-all(bf16[4,16,4224]{2,1,0:T(8,128)(2,1)S(1)} %reduce_sum.115), channel_id=1, replica_groups=mesh['sy'=4,'sz'=2,'sc'=2,'hx'=4,'hz'=4] {'hz'}, dimensions={0} | all-to-all | bytes 1081344 | tf_op jit(solution)/shard_map/all_to_all | solution.py:85
  296.7 7.4 %all-gather.11.cloned.1.call-done = bf16[256,4096]{1,0:T(8,128)(2,1)} async-done(((bf16[64,4096]{1,0:T(8,128)(2,1)}), bf16[256,4096]{1,0:T(8,128)(2,1)}) %all-gather.11.cloned.1.call-update) | async-done | bytes 2097168 | tf_op jit(solution)/shard_map/all_gather | solution.py:99
  304.1 16.3 %all_gather.46 = bf16[64,4096]{1,0:T(8,128)(2,1)} all-gather(bf16[16,4096]{1,0:T(8,128)(2,1)S(1)} %multiply_convert_fusion.9), channel_id=1, replica_groups=mesh['sy'=4,'sz'=2,'sc'=2,'hx'=4,'hz'=4] {'hz'}, dimensions={0}, use_global_device_ids=true | all-gather | bytes 655360 | tf_op jit(solution)/shard_map/all_gather | solution.py:98
  320.5 4.2 fusion.72
  324.7 7.3 %convolution_convert_fusion.1 = bf16[256,4096]{1,0:T(8,128)(2,1)} fusion(bf16[512,4096]{0,1:T(8,128)(2,1)} %bitcast.107, bf16[256,4096]{1,0:T(8,128)(2,1)S(1)} %copy-done.8, bf16[4096,512]{1,0:T(8,128)(2,1)} %param.34, f32[256,512]{1,0:T(8,128)S(1)} %fusion.72), kind=kOutput, calls=%fused_computation.1 | convolution fusion | flops 2149318656 | bytes 13107200 | tf_op jit(solution)/shard_map/dot_general | solution.py:179
  332.0 3.7 all-to-all-start.4
  335.6 33.2 %all-gather.13.cloned.1.call-done = bf16[256,4096]{1,0:T(8,128)(2,1)} async-done(((bf16[64,4096]{1,0:T(8,128)(2,1)}), bf16[256,4096]{1,0:T(8,128)(2,1)}) %all-gather.13.cloned.1.call-update) | async-done | bytes 2097168 | tf_op jit(solution)/shard_map/all_gather | solution.py:99
  368.8 4.1 fusion.73
  372.9 7.8 %convolution_convert_fusion = bf16[256,4096]{1,0:T(8,128)(2,1)} fusion(bf16[512,4096]{0,1:T(8,128)(2,1)} %bitcast.108, bf16[256,4096]{1,0:T(8,128)(2,1)} %all-gather.13.cloned.1.call-done, bf16[4096,512]{1,0:T(8,128)(2,1)} %param.34, f32[256,512]{1,0:T(8,128)S(1)} %fusion.73), kind=kOutput, calls=%fused_computation | convolution fusion | flops 2149318656 | bytes 13107200 | tf_op jit(solution)/shard_map/dot_general | solution.py:179
  380.7 9.8 %all-to-all-start.6 = ((bf16[4,4,16,4096]{3,2,1,0:T(8,128)(2,1)}), bf16[4,4,16,4096]{3,2,1,0:T(8,128)(2,1)}, u32[]{:S(2)}, u32[]{:S(2)}) async-start(bf16[4,4,16,4096]{3,2,1,0:T(8,128)(2,1)} %bitcast.114), calls=%async_computation.6 | async-start | bytes 4194304 | tf_op jit(solution)/shard_map/all_to_all | solution.py:83
  391.7 19.5 %all-to-all-done.6 = bf16[4,4,16,4096]{3,2,1,0:T(8,128)(2,1)} async-done(((bf16[4,4,16,4096]{3,2,1,0:T(8,128)(2,1)}), bf16[4,4,16,4096]{3,2,1,0:T(8,128)(2,1)}, u32[]{:S(2)}, u32[]{:S(2)}) %all-to-all-start.6) | async-done | bytes 2097184 | tf_op jit(solution)/shard_map/all_to_all | solution.py:83
  411.2 9.6 %all-to-all-start.5 = ((bf16[4,16,4096]{2,1,0:T(8,128)(2,1)}), bf16[4,16,4096]{2,1,0:T(8,128)(2,1)S(1)}, u32[]{:S(2)}, u32[]{:S(2)}) async-start(bf16[4,16,4096]{2,1,0:T(8,128)(2,1)} %reduce_sum.118), calls=%async_computation.5 | async-start | bytes 1048576 | tf_op jit(solution)/shard_map/all_to_all | solution.py:85
  420.9 2.9 reduce_sum.120
  423.7 10.7 %all-to-all-done.5 = bf16[4,16,4096]{2,1,0:T(8,128)(2,1)S(1)} async-done(((bf16[4,16,4096]{2,1,0:T(8,128)(2,1)}), bf16[4,16,4096]{2,1,0:T(8,128)(2,1)S(1)}, u32[]{:S(2)}, u32[]{:S(2)}) %all-to-all-start.5) | async-done | bytes 524320 | tf_op jit(solution)/shard_map/all_to_all | solution.py:85
  434.5 3.5 all-to-all-start.7
  438.0 13.9 %all-to-all-done.7 = bf16[4,16,4096]{2,1,0:T(8,128)(2,1)S(1)} async-done(((bf16[4,16,4096]{2,1,0:T(8,128)(2,1)}), bf16[4,16,4096]{2,1,0:T(8,128)(2,1)S(1)}, u32[]{:S(2)}, u32[]{:S(2)}) %all-to-all-start.7) | async-done | bytes 524320 | tf_op jit(solution)/shard_map/all_to_all | solution.py:85
  (107 shorter events, 24.0 us)
Async XLA Ops:
  6.5 82.1 %copy-start.1 = (bf16[512,512]{1,0:T(8,128)(2,1)S(1)}, bf16[512,512]{1,0:T(8,128)(2,1)}, u32[]{:S(2)}) copy-start(bf16[512,512]{1,0:T(8,128)(2,1)} %param.22) | copy-start | bytes 1572868
  6.5 82.0 %all-gather.15.cloned.1.call-start = ((), (), s32[]{:S(2)}) async-start(), calls=%async_computation.10 | async-start | bytes 2359296 | tf_op jit(solution)/shard_map/all_gather | solution.py:91
  7.3 161.4 %all-gather.19.cloned.1.call-start = ((), (), s32[]{:S(2)}) async-start(), calls=%async_computation.12 | async-start | bytes 2359296 | tf_op jit(solution)/shard_map/all_gather | solution.py:91
  8.0 177.4 %all-gather.17.cloned.1.call-start = ((), (), s32[]{:S(2)}) async-start(), calls=%async_computation.11 | async-start | bytes 6291456 | tf_op jit(solution)/shard_map/all_gather | solution.py:92
  88.5 0.9 copy-start.2
  88.6 149.7 %all-gather.21.cloned.1.call-start = ((), (), s32[]{:S(2)}) async-start(), calls=%async_computation.13 | async-start | bytes 6291456 | tf_op jit(solution)/shard_map/all_gather | solution.py:92
  90.5 14.8 %collective-permute-start.4 = (f32[8,64,128]{2,1,0:T(8,128)S(1)}, f32[8,64,128]{2,1,0:T(8,128)S(1)}, u32[]{:S(2)}, u32[]{:S(2)}) collective-permute-start(f32[8,64,128]{2,1,0:T(8,128)S(1)} %fusion.7), channel_id=1, source_target_pairs={{0,16},{16,32},{32,48},{48,64},{64,80},{80,96},{96,112},{112,128},... | collective-permute-start | bytes 786440 | tf_op jit(solution)/shard_map/ppermute | solution.py:21
  105.3 15.1 %collective-permute-start.5 = (f32[8,64,128]{2,1,0:T(8,128)S(1)}, f32[8,64,128]{2,1,0:T(8,128)S(1)}, u32[]{:S(2)}, u32[]{:S(2)}) collective-permute-start(f32[8,64,128]{2,1,0:T(8,128)S(1)} %collective-permute-done.4), channel_id=1, source_target_pairs={{0,16},{16,32},{32,48},{48,64},{64,80},{80,96},{96,112},{112,128},... | collective-permute-start | bytes 786440 | tf_op jit(solution)/shard_map/ppermute | solution.py:21
  107.4 13.0 %collective-permute-start = (f32[8]{0:T(128)S(1)}, f32[8]{0:T(128)S(1)}, u32[]{:S(2)}, u32[]{:S(2)}) collective-permute-start(f32[8]{0:T(128)S(1)} %fusion.65), channel_id=1, source_target_pairs={{0,16},{16,32},{32,48},{48,64},{64,80},{80,96},{96,112},{112,128},... | collective-permute-start | bytes 104 | tf_op jit(solution)/shard_map/ppermute | solution.py:21
  120.5 16.8 %collective-permute-start.6 = (f32[8,64,128]{2,1,0:T(8,128)S(1)}, f32[8,64,128]{2,1,0:T(8,128)S(1)}, u32[]{:S(2)}, u32[]{:S(2)}) collective-permute-start(f32[8,64,128]{2,1,0:T(8,128)S(1)} %multiply_add_fusion.3), channel_id=1, source_target_pairs={{0,32},{16,48},{32,64},{48,80},{64,96},{80,112},{96,128},{112,144}... | collective-permute-start | bytes 786440 | tf_op jit(solution)/shard_map/ppermute | solution.py:21
  123.7 9.8 %collective-permute-start.1 = (f32[8]{0:T(128)S(1)}, f32[8]{0:T(128)S(1)}, u32[]{:S(2)}, u32[]{:S(2)}) collective-permute-start(f32[8]{0:T(128)S(1)} %collective-permute-done), channel_id=1, source_target_pairs={{0,16},{16,32},{32,48},{48,64},{64,80},{80,96},{96,112},{112,128},... | collective-permute-start | bytes 104 | tf_op jit(solution)/shard_map/ppermute | solution.py:21
  137.4 19.1 %collective-permute-start.7 = (f32[8,64,128]{2,1,0:T(8,128)S(1)}, f32[8,64,128]{2,1,0:T(8,128)}, u32[]{:S(2)}, u32[]{:S(2)}) collective-permute-start(f32[8,64,128]{2,1,0:T(8,128)S(1)} %multiply_add_fusion.2), channel_id=1, source_target_pairs={{0,64},{16,80},{32,96},{48,112},{64,128},{80,144},{96,160},{112,17... | collective-permute-start | bytes 786440 | tf_op jit(solution)/shard_map/ppermute | solution.py:21
  144.2 17.4 %copy-start.4 = (f32[256,256]{1,0:T(8,128)S(1)}, f32[256,256]{1,0:T(8,128)}, u32[]{:S(2)}) copy-start(f32[256,256]{1,0:T(8,128)} %fusion.50) | copy-start | bytes 786436
  145.8 10.7 %collective-permute-start.2 = (f32[8]{0:T(128)S(1)}, f32[8]{0:T(128)S(1)}, u32[]{:S(2)}, u32[]{:S(2)}) collective-permute-start(f32[8]{0:T(128)S(1)} %mul.272), channel_id=1, source_target_pairs={{0,32},{16,48},{32,64},{48,80},{64,96},{80,112},{96,128},{112,144}... | collective-permute-start | bytes 104 | tf_op jit(solution)/shard_map/ppermute | solution.py:21
  157.5 11.1 %collective-permute-start.8 = (f32[8,64,128]{2,1,0:T(8,128)S(1)}, f32[8,64,128]{2,1,0:T(8,128)S(1)}, u32[]{:S(2)}, u32[]{:S(2)}) collective-permute-start(f32[8,64,128]{2,1,0:T(8,128)S(1)} %multiply_add_fusion.1), channel_id=1, source_target_pairs={{0,128},{16,144},{32,160},{48,176},{64,192},{80,208},{96,224},{112... | collective-permute-start | bytes 786440 | tf_op jit(solution)/shard_map/ppermute | solution.py:21
  161.6 7.1 %copy-start.7 = (f32[8]{0:T(128)S(1)}, f32[8]{0:T(128)}, u32[]{:S(2)}) copy-start(f32[8]{0:T(128)} %param.28) | copy-start | bytes 100
  163.2 5.5 %collective-permute-start.3 = (f32[8]{0:T(128)S(1)}, f32[8]{0:T(128)S(1)}, u32[]{:S(2)}, u32[]{:S(2)}) collective-permute-start(f32[8]{0:T(128)S(1)} %mul.273), channel_id=1, source_target_pairs={{0,64},{16,80},{32,96},{48,112},{64,128},{80,144},{96,160},{112,17... | collective-permute-start | bytes 104 | tf_op jit(solution)/shard_map/ppermute | solution.py:21
  168.7 2.4 copy-start.3
  168.7 2.4 copy-start.6
  196.9 31.7 %all-to-all-start = ((bf16[4,4,16,4224]{3,2,1,0:T(8,128)(2,1)}), bf16[4,4,16,4224]{3,2,1,0:T(8,128)(2,1)S(1)}, u32[]{:S(2)}, u32[]{:S(2)}) async-start(bf16[4,4,16,4224]{3,2,1,0:T(8,128)(2,1)} %bitcast.104), calls=%async_computation | async-start | bytes 4325376 | tf_op jit(solution)/shard_map/all_to_all | solution.py:83
  229.9 19.0 %all-to-all-start.1 = ((bf16[4,16,4224]{2,1,0:T(8,128)(2,1)}), bf16[4,16,4224]{2,1,0:T(8,128)(2,1)S(1)}, u32[]{:S(2)}, u32[]{:S(2)}) async-start(bf16[4,16,4224]{2,1,0:T(8,128)(2,1)} %reduce_sum.112), calls=%async_computation.1 | async-start | bytes 1081344 | tf_op jit(solution)/shard_map/all_to_all | solution.py:85
  244.7 4.4 copy-start
  244.7 4.7 %copy-start.5 = (f32[4096]{0:T(1024)S(1)}, f32[4096]{0:T(1024)}, u32[]{:S(2)}) copy-start(f32[4096]{0:T(1024)} %param.32) | copy-start | bytes 49156
  249.5 30.2 %all-to-all-start.2 = ((bf16[4,4,16,4224]{3,2,1,0:T(8,128)(2,1)}), bf16[4,4,16,4224]{3,2,1,0:T(8,128)(2,1)S(1)}, u32[]{:S(2)}, u32[]{:S(2)}) async-start(bf16[4,4,16,4224]{3,2,1,0:T(8,128)(2,1)} %bitcast.37), calls=%async_computation.2 | async-start | bytes 4325376 | tf_op jit(solution)/shard_map/all_to_all | solution.py:83
  253.2 50.9 %all-gather.11.cloned.1.call-start = ((), (), s32[]{:S(2)}) async-start(), calls=%async_computation.8 | async-start | bytes 2621440 | tf_op jit(solution)/shard_map/all_gather | solution.py:99
  270.0 98.8 %all-gather.13.cloned.1.call-start = ((), (), s32[]{:S(2)}) async-start(), calls=%async_computation.9 | async-start | bytes 2621440 | tf_op jit(solution)/shard_map/all_gather | solution.py:99
  320.4 4.2 copy-start.8
  332.0 48.7 %all-to-all-start.4 = ((bf16[4,4,16,4096]{3,2,1,0:T(8,128)(2,1)}), bf16[4,4,16,4096]{3,2,1,0:T(8,128)(2,1)S(1)}, u32[]{:S(2)}, u32[]{:S(2)}) async-start(bf16[4,4,16,4096]{3,2,1,0:T(8,128)(2,1)} %bitcast.113), calls=%async_computation.4 | async-start | bytes 4194304 | tf_op jit(solution)/shard_map/all_to_all | solution.py:83
  380.7 30.6 %all-to-all-start.6 = ((bf16[4,4,16,4096]{3,2,1,0:T(8,128)(2,1)}), bf16[4,4,16,4096]{3,2,1,0:T(8,128)(2,1)}, u32[]{:S(2)}, u32[]{:S(2)}) async-start(bf16[4,4,16,4096]{3,2,1,0:T(8,128)(2,1)} %bitcast.114), calls=%async_computation.6 | async-start | bytes 4194304 | tf_op jit(solution)/shard_map/all_to_all | solution.py:83
  411.2 23.2 %all-to-all-start.5 = ((bf16[4,16,4096]{2,1,0:T(8,128)(2,1)}), bf16[4,16,4096]{2,1,0:T(8,128)(2,1)S(1)}, u32[]{:S(2)}, u32[]{:S(2)}) async-start(bf16[4,16,4096]{2,1,0:T(8,128)(2,1)} %reduce_sum.118), calls=%async_computation.5 | async-start | bytes 1048576 | tf_op jit(solution)/shard_map/all_to_all | solution.py:85
  434.5 17.5 %all-to-all-start.7 = ((bf16[4,16,4096]{2,1,0:T(8,128)(2,1)}), bf16[4,16,4096]{2,1,0:T(8,128)(2,1)S(1)}, u32[]{:S(2)}, u32[]{:S(2)}) async-start(bf16[4,16,4096]{2,1,0:T(8,128)(2,1)} %reduce_sum.120), calls=%async_computation.7 | async-start | bytes 1048576 | tf_op jit(solution)/shard_map/all_to_all | solution.py:85
Sparse Core Ops, SparseCore 0:
  10.0 78.5 all-gather.14
  91.2 73.6 all-gather.18
  166.6 18.7 all-gather.16
  187.1 20.2 all-gather.20
  270.1 33.9 all-gather.10
  320.6 48.1 all-gather.12

commit v6 on v4

--- a/solution.py
+++ b/solution.py
@@ -130,7 +130,7 @@
     row_squares = jnp.sum(gated_out * gated_out, axis=1)
     gated_scaled = (gated_out * norm_gain).astype(jnp.bfloat16)
     head_n = lax.axis_size("hx") * lax.axis_size("hz")
-    chunks = 2
+    chunks = 1
     rows_per = length // head_n // chunks
     width = out_full.shape[1]
     gated_parts = gated_scaled.reshape(head_n, chunks, rows_per, -1)

time: 396 us -> 393 us (level)
  blocking collectives: 50.3 us -> 164 us
  waiting for transfers between devices: 180 us -> 125 us
  starting transfers between devices: 90.8 us -> 41.6 us
  matrix products: 37.9 us -> 27.5 us
    all_to_all x0 -> x2, blocking collectives: none -> 105 us  [sum_over_head(): pieces = lax.all_to_all(pieces, 'hx', 0, 0, tiled=False)]
    all_to_all x7 -> x0, waiting for transfers between devices: 100 us -> none  [the longest x4 54.1 us: sum_over_head(): pieces = lax.all_to_all(pieces, 'hx', 0, 0, tiled=False)]
    all_to_all x7 -> x0, starting transfers between devices: 46.4 us -> none  [the longest x3 24 us: sum_over_head(): pieces = lax.all_to_all(pieces, 'hz', 0, 0, tiled=False)]
    all_to_all x1 -> x2, blocking collectives: 17 us -> 58.6 us  [sum_over_head(): pieces = lax.all_to_all(pieces, 'hz', 0, 0, tiled=False)]
    all_gather x2 -> x0, blocking collectives: 33.3 us -> none  [gather_over_head(): value = lax.all_gather(value, 'hz', axis=0, tiled=True)]
    all_gather x0 -> x1, waiting for transfers between devices: none -> 29.1 us  [gather_over_head(): value = lax.all_gather(value, 'hz', axis=0, tiled=True)]
    all_gather x2 -> x1, waiting for transfers between devices: 32.2 us -> 51.3 us  [gather_over_head(): return lax.all_gather(value, 'hx', axis=0, tiled=True)]
    all_gather x1, waiting for transfers between devices: 11 us -> 0.02 us  [shards(): lax.all_gather(down_weight, 'seq', axis=1, tiled=True)]
  transfers between devices with their start and end apart: 20 -> 13, of which waited for: 15 -> 8; matrix products, arithmetic and copies ran while one was open for 15% -> 7% of each run, Pallas kernels for 0% -> 0%
where the time goes in v6:
time: 393 us; the launch traced here: 392 us
  blocking collectives  164 us (42%)
  waiting for transfers between devices  125 us (32%)
  starting transfers between devices  41.6 us (11%)
  matrix products  27.5 us (7%)
  other arithmetic  17.6 us (4%)
  between operations  13.5 us (3%)
    all_to_all x2, blocking collectives, sum_over_head(): pieces = lax.all_to_all(pieces, 'hx', 0, 0, tiled=False)  105 us
    all_to_all x2, blocking collectives, sum_over_head(): pieces = lax.all_to_all(pieces, 'hz', 0, 0, tiled=False)  58.6 us
    all_gather x1, waiting for transfers between devices, gather_over_head(): return lax.all_gather(value, 'hx', axis=0, tiled=True)  51.3 us
    ppermute x9, waiting for transfers between devices, passed_along(): lax.ppermute(value, axis, [(source, source + steps) for source in range(i...  43.4 us
    ppermute x9, starting transfers between devices, passed_along(): lax.ppermute(value, axis, [(source, source + steps) for source in range(i...  41.3 us
    all_gather x1, waiting for transfers between devices, gather_over_head(): value = lax.all_gather(value, 'hz', axis=0, tiled=True)  29.1 us
    dot_general x1, matrix products, mlp_rows(): mlp_part = jnp.dot(hidden, down_full, preferred_element_type=jnp.float32)  11.2 us
  transfers between devices with their start and end apart: 13, of which 8 were waited for; matrix products, arithmetic and copies ran while one was open for 7% of the time, Pallas kernels for 0%

profile of v6, /device:TPU:8, one launch (start us, length us, event | category | flops | bytes accessed | tf_op | source)
XLA Modules:
  0.0 391.8 jit_solution(16154125242360742300)
XLA Ops:
  6.5 0.7 all-gather.5.cloned.1.call-update
  7.3 0.7 neg.15
  8.0 0.8 broadcast_multiply_fusion
  8.8 0.6 reduce-window.24
  9.6 0.6 reduce-window.20
  10.3 1.1 fusion.53
  12.2 0.9 bitcast_convert_fusion
  13.1 0.5 fusion.7
  13.6 0.5 fusion.6
  14.1 1.9 collective-permute-start.4
  16.0 1.1 reduce-window.26
  17.4 9.2 %collective-permute-done.4 = f32[8,64,128]{2,1,0:T(8,128)S(1)} collective-permute-done((f32[8,64,128]{2,1,0:T(8,128)S(1)}, f32[8,64,128]{2,1,0:T(8,128)S(1)}, u32[]{:S(2)}, u32[]{:S(2)}) %collective-permute-start.4) | collective-permute-done | bytes 262176 | tf_op jit(solution)/shard_map/ppermute | solution.py:16
  26.7 8.6 %collective-permute-start.5 = (f32[8,64,128]{2,1,0:T(8,128)S(1)}, f32[8,64,128]{2,1,0:T(8,128)S(1)}, u32[]{:S(2)}, u32[]{:S(2)}) collective-permute-start(f32[8,64,128]{2,1,0:T(8,128)S(1)} %collective-permute-done.4), channel_id=1, source_target_pairs={{0,16},{16,32},{32,48},{48,64},{64,80},{80,96},{96,112},{112,128},... | collective-permute-start | bytes 786440 | tf_op jit(solution)/shard_map/ppermute | solution.py:16
  35.4 8.7 %collective-permute-start = (f32[8]{0:T(128)S(1)}, f32[8]{0:T(128)S(1)}, u32[]{:S(2)}, u32[]{:S(2)}) collective-permute-start(f32[8]{0:T(128)S(1)} %fusion.48), channel_id=1, source_target_pairs={{0,16},{16,32},{32,48},{48,64},{64,80},{80,96},{96,112},{112,128},... | collective-permute-start | bytes 104 | tf_op jit(solution)/shard_map/ppermute | solution.py:16
  44.4 0.7 collective-permute-done
  45.2 9.8 %collective-permute-start.6 = (f32[8,64,128]{2,1,0:T(8,128)S(1)}, f32[8,64,128]{2,1,0:T(8,128)S(1)}, u32[]{:S(2)}, u32[]{:S(2)}) collective-permute-start(f32[8,64,128]{2,1,0:T(8,128)S(1)} %multiply_add_fusion.3), channel_id=1, source_target_pairs={{0,32},{16,48},{32,64},{48,80},{64,96},{80,112},{96,128},{112,144}... | collective-permute-start | bytes 786440 | tf_op jit(solution)/shard_map/ppermute | solution.py:16
  55.1 1.6 convolution_bitcast_fusion.3
  56.7 1.9 collective-permute-start.1
  58.6 20.8 %collective-permute-done.1 = f32[8]{0:T(128)S(1)} collective-permute-done((f32[8]{0:T(128)S(1)}, f32[8]{0:T(128)S(1)}, u32[]{:S(2)}, u32[]{:S(2)}) %collective-permute-start.1) | collective-permute-done | bytes 64 | tf_op jit(solution)/shard_map/ppermute | solution.py:16
  79.3 2.3 collective-permute-done.6
  81.7 2.9 collective-permute-start.7
  84.7 0.4 fusion.5
  85.3 0.7 compare_reduce_fusion.1
  86.0 0.6 compare_reduce_fusion
  86.8 4.3 %collective-permute-start.2 = (f32[8]{0:T(128)S(1)}, f32[8]{0:T(128)S(1)}, u32[]{:S(2)}, u32[]{:S(2)}) collective-permute-start(f32[8]{0:T(128)S(1)} %mul.238), channel_id=1, source_target_pairs={{0,32},{16,48},{32,64},{48,80},{64,96},{80,112},{96,128},{112,144}... | collective-permute-start | bytes 104 | tf_op jit(solution)/shard_map/ppermute | solution.py:16
  91.1 6.0 %collective-permute-done.2 = f32[8]{0:T(128)S(1)} collective-permute-done((f32[8]{0:T(128)S(1)}, f32[8]{0:T(128)S(1)}, u32[]{:S(2)}, u32[]{:S(2)}) %collective-permute-start.2) | collective-permute-done | bytes 64 | tf_op jit(solution)/shard_map/ppermute | solution.py:16
  97.2 1.3 collective-permute-start.8
  98.5 0.7 fusion.4
  99.2 1.9 collective-permute-start.3
  101.1 4.3 %collective-permute-done.3 = f32[8]{0:T(128)S(1)} collective-permute-done((f32[8]{0:T(128)S(1)}, f32[8]{0:T(128)S(1)}, u32[]{:S(2)}, u32[]{:S(2)}) %collective-permute-start.3) | collective-permute-done | bytes 64 | tf_op jit(solution)/shard_map/ppermute | solution.py:16
  105.5 1.7 fusion.2
  107.6 0.4 multiply_reduce_fusion
  108.2 1.3 fusion.32
  109.6 0.4 scatter.9
  110.0 4.6 %convolution_convert_fusion.1 = bf16[512,4096]{1,0:T(8,128)(2,1)S(1)} fusion(bf16[512,4096]{1,0:T(8,128)(2,1)} %all-gather.5.cloned.1.call-done, f32[512]{0:T(512)S(1)} %copy-done.6, f32[512,512]{1,0:T(8,128)S(1)} %copy.35, bf16[512,512]{1,0:T(8,128)(2,1)S(1)} %copy-done.3), kind=kOutput, calls=%fused_computation.1 | convolution fusion | flops 2151677952 | bytes 9963520 | tf_op jit(solution)/shard_map/dot_general | solution.py:143
  114.7 0.4 pad_maximum_fusion
  115.0 50.7 %all_to_all.20 = bf16[4,4,32,4224]{3,2,1,0:T(8,128)(2,1)} all-to-all(bf16[4,4,32,4224]{3,2,1,0:T(8,128)(2,1)S(1)} %bitcast.80), channel_id=1, replica_groups=mesh['seq'=16,'hx'=4,'hz'=4] {'hx'}, dimensions={0} | all-to-all | bytes 8650752 | tf_op jit(solution)/shard_map/all_to_all | solution.py:76
  165.7 3.0 reduce_sum.64
  168.7 29.5 %all_to_all.21 = bf16[4,32,4224]{2,1,0:T(8,128)(2,1)S(1)} all-to-all(bf16[4,32,4224]{2,1,0:T(8,128)(2,1)S(1)} %reduce_sum.64), channel_id=1, replica_groups=mesh['seq'=16,'hx'=4,'hz'=4] {'hz'}, dimensions={0} | all-to-all | bytes 2162688 | tf_op jit(solution)/shard_map/all_to_all | solution.py:78
  198.9 0.9 multiply_convert_fusion.10
  200.0 29.1 %all-gather.9.cloned.1.call-done = bf16[128,4096]{1,0:T(8,128)(2,1)} async-done(((bf16[32,4096]{1,0:T(8,128)(2,1)}), bf16[128,4096]{1,0:T(8,128)(2,1)}) %all-gather.9.cloned.1.call-update) | async-done | bytes 1048592 | tf_op jit(solution)/shard_map/all_gather | solution.py:83
  229.1 51.3 %all-gather.11.cloned.1.call-done = bf16[512,4096]{1,0:T(8,128)(2,1)} async-done(((bf16[128,4096]{1,0:T(8,128)(2,1)}), bf16[512,4096]{1,0:T(8,128)(2,1)}) %all-gather.11.cloned.1.call-update) | async-done | bytes 4194320 | tf_op jit(solution)/shard_map/all_gather | solution.py:84
  280.4 5.8 %fusion.54 = f32[512,512]{1,0:T(8,128)S(1)} fusion(bf16[512,4096]{1,0:T(8,128)(2,1)} %all-gather.11.cloned.1.call-done, bf16[4096,512]{1,0:T(8,128)(2,1)} %param.29), kind=kOutput, calls=%fused_computation.109 | convolution fusion | flops 2147483648 | bytes 9437184 | tf_op jit(solution)/shard_map/dot_general | solution.py:161
  286.2 11.2 %convolution_convert_fusion = bf16[512,4096]{1,0:T(8,128)(2,1)} fusion(bf16[512,4096]{1,0:T(8,128)(2,1)} %all-gather.7.cloned.1.call-done, bf16[512,4096]{1,0:T(8,128)(2,1)} %all-gather.11.cloned.1.call-done, bf16[4096,512]{1,0:T(8,128)(2,1)} %param.30, f32[512,512]{1,0:T(8,128)S(1)} %fusion.54), kind=kOutput, calls=%fused_computation | convolution fusion | flops 4298637312 | bytes 17825792 | tf_op jit(solution)/shard_map/dot_general | solution.py:164
  297.5 54.6 %all_to_all.22 = bf16[4,4,32,4096]{3,2,1,0:T(8,128)(2,1)} all-to-all(bf16[4,4,32,4096]{3,2,1,0:T(8,128)(2,1)} %bitcast.81), channel_id=1, replica_groups=mesh['seq'=16,'hx'=4,'hz'=4] {'hx'}, dimensions={0} | all-to-all | bytes 8388608 | tf_op jit(solution)/shard_map/all_to_all | solution.py:76
  352.1 3.1 reduce_sum.67
  355.1 29.1 %all_to_all.23 = bf16[4,32,4096]{2,1,0:T(8,128)(2,1)S(1)} all-to-all(bf16[4,32,4096]{2,1,0:T(8,128)(2,1)S(1)} %reduce_sum.67), channel_id=1, replica_groups=mesh['seq'=16,'hx'=4,'hz'=4] {'hz'}, dimensions={0} | all-to-all | bytes 2097152 | tf_op jit(solution)/shard_map/all_to_all | solution.py:78
  384.4 0.8 add_convert_fusion
  (62 shorter events, 4.2 us)
Async XLA Ops:
  6.5 37.7 %copy-start.2 = (bf16[2,512,128]{2,1,0:T(8,128)(2,1)S(1)}, bf16[2,512,128]{2,1,0:T(8,128)(2,1)}, u32[]{:S(2)}) copy-start(bf16[2,512,128]{2,1,0:T(8,128)(2,1)} %param.20) | copy-start | bytes 786436
  6.5 103.5 %all-gather.5.cloned.1.call-start = ((), (), s32[]{:S(2)}) async-start(), calls=%async_computation.4 | async-start | bytes 4456448 | tf_op jit(solution)/shard_map/all_gather | solution.py:109
  7.3 191.1 %all-gather.7.cloned.1.call-start = ((), (), s32[]{:S(2)}) async-start(), calls=%async_computation.5 | async-start | bytes 4456448 | tf_op jit(solution)/shard_map/all_gather | solution.py:110
  13.6 71.5 %copy-start.1 = (bf16[512,512]{1,0:T(8,128)(2,1)S(1)}, bf16[512,512]{1,0:T(8,128)(2,1)}, u32[]{:S(2)}) copy-start(bf16[512,512]{1,0:T(8,128)(2,1)} %param.18) | copy-start | bytes 1572868
  14.1 12.6 %collective-permute-start.4 = (f32[8,64,128]{2,1,0:T(8,128)S(1)}, f32[8,64,128]{2,1,0:T(8,128)S(1)}, u32[]{:S(2)}, u32[]{:S(2)}) collective-permute-start(f32[8,64,128]{2,1,0:T(8,128)S(1)} %fusion.6), channel_id=1, source_target_pairs={{0,16},{16,32},{32,48},{48,64},{64,80},{80,96},{96,112},{112,128},... | collective-permute-start | bytes 786440 | tf_op jit(solution)/shard_map/ppermute | solution.py:16
  26.7 18.5 %collective-permute-start.5 = (f32[8,64,128]{2,1,0:T(8,128)S(1)}, f32[8,64,128]{2,1,0:T(8,128)S(1)}, u32[]{:S(2)}, u32[]{:S(2)}) collective-permute-start(f32[8,64,128]{2,1,0:T(8,128)S(1)} %collective-permute-done.4), channel_id=1, source_target_pairs={{0,16},{16,32},{32,48},{48,64},{64,80},{80,96},{96,112},{112,128},... | collective-permute-start | bytes 786440 | tf_op jit(solution)/shard_map/ppermute | solution.py:16
  35.4 9.7 %collective-permute-start = (f32[8]{0:T(128)S(1)}, f32[8]{0:T(128)S(1)}, u32[]{:S(2)}, u32[]{:S(2)}) collective-permute-start(f32[8]{0:T(128)S(1)} %fusion.48), channel_id=1, source_target_pairs={{0,16},{16,32},{32,48},{48,64},{64,80},{80,96},{96,112},{112,128},... | collective-permute-start | bytes 104 | tf_op jit(solution)/shard_map/ppermute | solution.py:16
  44.1 185.0 %all-gather.9.cloned.1.call-start = ((), (), s32[]{:S(2)}) async-start(), calls=%async_computation.6 | async-start | bytes 1310720 | tf_op jit(solution)/shard_map/all_gather | solution.py:83
  45.2 36.4 %collective-permute-start.6 = (f32[8,64,128]{2,1,0:T(8,128)S(1)}, f32[8,64,128]{2,1,0:T(8,128)S(1)}, u32[]{:S(2)}, u32[]{:S(2)}) collective-permute-start(f32[8,64,128]{2,1,0:T(8,128)S(1)} %multiply_add_fusion.3), channel_id=1, source_target_pairs={{0,32},{16,48},{32,64},{48,80},{64,96},{80,112},{96,128},{112,144}... | collective-permute-start | bytes 786440 | tf_op jit(solution)/shard_map/ppermute | solution.py:16
  56.7 22.7 %collective-permute-start.1 = (f32[8]{0:T(128)S(1)}, f32[8]{0:T(128)S(1)}, u32[]{:S(2)}, u32[]{:S(2)}) collective-permute-start(f32[8]{0:T(128)S(1)} %collective-permute-done), channel_id=1, source_target_pairs={{0,16},{16,32},{32,48},{48,64},{64,80},{80,96},{96,112},{112,128},... | collective-permute-start | bytes 104 | tf_op jit(solution)/shard_map/ppermute | solution.py:16
  79.3 26.2 %copy-start.5 = (f32[8]{0:T(128)S(1)}, f32[8]{0:T(128)}, u32[]{:S(2)}) copy-start(f32[8]{0:T(128)} %param.24) | copy-start | bytes 100
  81.7 15.3 %collective-permute-start.7 = (f32[8,64,128]{2,1,0:T(8,128)S(1)}, f32[8,64,128]{2,1,0:T(8,128)S(1)}, u32[]{:S(2)}, u32[]{:S(2)}) collective-permute-start(f32[8,64,128]{2,1,0:T(8,128)S(1)} %multiply_add_fusion.2), channel_id=1, source_target_pairs={{0,64},{16,80},{32,96},{48,112},{64,128},{80,144},{96,160},{112,17... | collective-permute-start | bytes 786440 | tf_op jit(solution)/shard_map/ppermute | solution.py:16
  86.8 10.3 %collective-permute-start.2 = (f32[8]{0:T(128)S(1)}, f32[8]{0:T(128)S(1)}, u32[]{:S(2)}, u32[]{:S(2)}) collective-permute-start(f32[8]{0:T(128)S(1)} %mul.238), channel_id=1, source_target_pairs={{0,32},{16,48},{32,64},{48,80},{64,96},{80,112},{96,128},{112,144}... | collective-permute-start | bytes 104 | tf_op jit(solution)/shard_map/ppermute | solution.py:16
  97.2 8.3 %collective-permute-start.8 = (f32[8,64,128]{2,1,0:T(8,128)S(1)}, f32[8,64,128]{2,1,0:T(8,128)S(1)}, u32[]{:S(2)}, u32[]{:S(2)}) collective-permute-start(f32[8,64,128]{2,1,0:T(8,128)S(1)} %multiply_add_fusion.1), channel_id=1, source_target_pairs={{0,128},{16,144},{32,160},{48,176},{64,192},{80,208},{96,224},{112... | collective-permute-start | bytes 786440 | tf_op jit(solution)/shard_map/ppermute | solution.py:16
  98.5 9.1 %copy-start.3 = (bf16[512,512]{1,0:T(8,128)(2,1)S(1)}, bf16[512,512]{1,0:T(8,128)(2,1)}, u32[]{:S(2)}) copy-start(bf16[512,512]{1,0:T(8,128)(2,1)} %param.19) | copy-start | bytes 1572868
  99.2 6.3 %collective-permute-start.3 = (f32[8]{0:T(128)S(1)}, f32[8]{0:T(128)S(1)}, u32[]{:S(2)}, u32[]{:S(2)}) collective-permute-start(f32[8]{0:T(128)S(1)} %mul.239), channel_id=1, source_target_pairs={{0,64},{16,80},{32,96},{48,112},{64,128},{80,144},{96,160},{112,17... | collective-permute-start | bytes 104 | tf_op jit(solution)/shard_map/ppermute | solution.py:16
  105.5 4.5 %copy-start.6 = (f32[512]{0:T(512)S(1)}, f32[512]{0:T(512)}, u32[]{:S(2)}) copy-start(f32[512]{0:T(512)} %param.25) | copy-start | bytes 6148
  165.7 32.9 %copy-start = (bf16[32,4096]{1,0:T(8,128)(2,1)S(1)}, bf16[32,4096]{1,0:T(8,128)(2,1)}, u32[]{:S(2)}) copy-start(bf16[32,4096]{1,0:T(8,128)(2,1)} %param.27) | copy-start | bytes 786436
  165.7 33.2 %copy-start.4 = (f32[4096]{0:T(1024)S(1)}, f32[4096]{0:T(1024)}, u32[]{:S(2)}) copy-start(f32[4096]{0:T(1024)} %param.28) | copy-start | bytes 49156
  199.8 80.6 %all-gather.11.cloned.1.call-start = ((), (), s32[]{:S(2)}) async-start(), calls=%async_computation.7 | async-start | bytes 5242880 | tf_op jit(solution)/shard_map/all_gather | solution.py:84
Sparse Core Ops, SparseCore 0:
  9.9 89.4 all-gather.4
  101.9 76.9 all-gather.6
  199.9 29.1 all-gather.8
  230.8 49.6 all-gather.10

commit v7 on v5

--- a/solution.py
+++ b/solution.py
@@ -8,17 +8,7 @@
 
 
 epsilon = 1e-05
-
-
 SEQ = ("sy", "sz", "sc")
-
-
-def passed_along(value, axis, steps):
-    count = 1
-    for name in axis:
-        count *= lax.axis_size(name)
-    initial, last = (max(0, -steps), min(count, count - steps))
-    return lax.ppermute(value, axis, [(source, source + steps) for source in range(initial, last)])
 
 
 def block_scan(x_heads, b_rows, c_rows, step_size, log_decay, block_len):
@@ -59,22 +49,47 @@
     return jnp.concatenate(outs, axis=0), carry_state
 
 
+def combine(first, second):
+    (d1, s1), (d2, s2) = first, second
+    return d1 * d2, d2[:, None, None] * s1 + s2
+
+
+def send(pair, pairs, axes):
+    return tuple(lax.ppermute(v, axes, pairs) for v in pair)
+
+
 def entering_state(group_decay, local_state):
-    count = 1
-    for name in SEQ:
-        count *= lax.axis_size(name)
-    dec = passed_along(group_decay, SEQ, 1)
-    st = passed_along(local_state, SEQ, 1)
-    step = 1
-    while step < count:
-        sp = passed_along(st, SEQ, step)
-        if step * 2 < count:
-            dp = passed_along(dec, SEQ, step)
-        st = dec[:, None, None] * sp + st
-        if step * 2 < count:
-            dec = dp * dec
-        step *= 2
-    return st
+    block = ("sz", "sc")
+    j = lax.axis_index("sz") * 2 + lax.axis_index("sc")
+    y = lax.axis_index("sy")
+    ny = lax.axis_size("sy")
+    own = (group_decay, local_state)
+    ident = (jnp.ones_like(group_decay), jnp.zeros_like(local_state))
+
+    def pick(cond, a, b):
+        return tuple(jnp.where(cond, u, v) for u, v in zip(a, b))
+
+    got = send(own, [(0, 1), (2, 3)], block)
+    pair_agg = combine(got, own)
+    lower = send(pair_agg, [(1, 2)], block)
+    lower3 = send(lower, [(2, 3)], block)
+    inner = pick(j == 1, got, ident)
+    inner = pick(j == 2, lower, inner)
+    inner = pick(j == 3, combine(lower3, got), inner)
+    block_agg = combine(lower3, pair_agg)
+    full = SEQ
+    before = ident
+    for k in range(ny - 1, 0, -1):
+        pairs = [(4 * src + 3, 4 * (src + k) + 3) for src in range(ny - k)]
+        got_k = send(block_agg, pairs, full)
+        before = combine(before, pick(y >= k, got_k, ident))
+    to_2 = send(before, [(3, 2)], block)
+    to_1 = send(before, [(3, 1)], block)
+    to_0 = send(to_1, [(1, 0)], block)
+    prefix = pick(j == 3, before, to_0)
+    prefix = pick(j == 2, to_2, prefix)
+    prefix = pick(j == 1, to_1, prefix)
+    return combine(prefix, inner)[1]
 
 
 def sum_over_head(value):
@@ -84,14 +99,6 @@
     pieces = jnp.sum(pieces.astype(jnp.float32), axis=0).astype(jnp.bfloat16)
     pieces = lax.all_to_all(pieces, "hz", 0, 0, tiled=False)
     return jnp.sum(pieces.astype(jnp.float32), axis=0)
-
-
-def gather_seq_columns(value):
-    rows, cols = value.shape
-    value = lax.all_gather(value, ("sy", "sz"), axis=0, tiled=False)
-    value = lax.all_gather(value, "sc", axis=0, tiled=False)
-    value = value.transpose(2, 1, 0, 3)
-    return value.reshape(rows, -1)
 
 
 def gather_over_head(value):
@@ -121,8 +128,8 @@
     down_weight,
 ):
     out_full, down_full = (
-        gather_seq_columns(out_weight),
-        gather_seq_columns(down_weight),
+        lax.all_gather(out_weight, SEQ, axis=1, tiled=True),
+        lax.all_gather(down_weight, SEQ, axis=1, tiled=True),
     )
     head_count = dt_raw.shape[0]
     length = dt_raw.shape[1]
@@ -145,7 +152,7 @@
     row_squares = jnp.sum(gated_out * gated_out, axis=1)
     gated_scaled = (gated_out * norm_gain).astype(jnp.bfloat16)
     head_n = lax.axis_size("hx") * lax.axis_size("hz")
-    chunks = 2
+    chunks = 1
     rows_per = length // head_n // chunks
     width = out_full.shape[1]
     gated_parts = gated_scaled.reshape(head_n, chunks, rows_per, -1)

time: 461 us -> 383 us (0.83)
  blocking collectives: 48.9 us -> 169 us
  waiting for transfers between devices: 255 us -> 135 us
  starting transfers between devices: 67.5 us -> 12.7 us
  local copies, waits for them, and re-layouts: 15.5 us -> 3.19 us
  matrix products: 37.9 us -> 29.3 us
    all_to_all x0 -> x2, blocking collectives: none -> 109 us  [sum_over_head(): pieces = lax.all_to_all(pieces, 'hx', 0, 0, tiled=False)]
    all_to_all x7 -> x0, waiting for transfers between devices: 82.1 us -> none  [the longest x4 54.8 us: sum_over_head(): pieces = lax.all_to_all(pieces, 'hx', 0, 0, tiled=False)]
    all_gather x4 -> x3, waiting for transfers between devices: 89.4 us -> 41.6 us  [the longest x1 28.4 us: gather_over_head(): value = lax.all_gather(value, 'hz', axis=0, tiled=True)]
    all_to_all x1 -> x2, blocking collectives: 15.9 us -> 60.1 us  [sum_over_head(): pieces = lax.all_to_all(pieces, 'hz', 0, 0, tiled=False)]
    all_to_all x7 -> x0, starting transfers between devices: 39.2 us -> none  [the longest x4 21.3 us: sum_over_head(): pieces = lax.all_to_all(pieces, 'hx', 0, 0, tiled=False)]
    all_gather x2 -> x0, blocking collectives: 33 us -> none  [gather_over_head(): value = lax.all_gather(value, 'hz', axis=0, tiled=True)]
    ppermute x9 -> x15, starting transfers between devices: 27.9 us -> 12.4 us  [send(): return tuple((lax.ppermute(v, axes, pairs) for v in pair))]
    transpose x2 -> x0, local copies, waits for them, and re-layouts: 13 us -> none  [gather_seq_columns(): value = value.transpose(2, 1, 0, 3)]
  transfers between devices with their start and end apart: 22 -> 19, of which waited for: 16 -> 4; matrix products, arithmetic and copies ran while one was open for 16% -> 8% of each run, Pallas kernels for 0% -> 0%
where the time goes in v7:
time: 383 us; the launch traced here: 382 us
  blocking collectives  169 us (44%)
  waiting for transfers between devices  135 us (35%)
  matrix products  29.3 us (8%)
  other arithmetic  18.8 us (5%)
  between operations  13.7 us (4%)
  starting transfers between devices  12.7 us (3%)
    all_to_all x2, blocking collectives, sum_over_head(): pieces = lax.all_to_all(pieces, 'hx', 0, 0, tiled=False)  109 us
    all_to_all x2, blocking collectives, sum_over_head(): pieces = lax.all_to_all(pieces, 'hz', 0, 0, tiled=False)  60.1 us
    all_gather x1, waiting for transfers between devices, gather_over_head(): return lax.all_gather(value, 'hx', axis=0, tiled=True)  51.3 us
    ppermute x15, waiting for transfers between devices, send(): return tuple((lax.ppermute(v, axes, pairs) for v in pair))  41.2 us
    all_gather x1, waiting for transfers between devices, gather_over_head(): value = lax.all_gather(value, 'hz', axis=0, tiled=True)  28.4 us
    all_gather x1, waiting for transfers between devices, shards(): lax.all_gather(out_weight, SEQ, axis=1, tiled=True)  13.2 us
    ppermute x15, starting transfers between devices, send(): return tuple((lax.ppermute(v, axes, pairs) for v in pair))  12.4 us
    dot_general x1, matrix products, mlp_rows(): mlp_part = jnp.dot(hidden, down_full, preferred_element_type=jnp.float32)  11.2 us
  transfers between devices with their start and end apart: 19, of which 4 were waited for; matrix products, arithmetic and copies ran while one was open for 8% of the time, Pallas kernels for 0%

profile of v7, /device:TPU:8, one launch (start us, length us, event | category | flops | bytes accessed | tf_op | source)
XLA Modules:
  0.0 381.9 jit_solution(6687073552328226396)
XLA Ops:
  6.5 0.7 all-gather.5.cloned.1.call-update
  7.3 0.7 neg.15
  8.0 0.8 broadcast_multiply_fusion
  8.8 0.6 reduce-window.24
  9.6 0.6 reduce-window.20
  10.3 1.1 fusion.68
  12.2 0.9 bitcast_convert_fusion
  13.1 0.5 fusion.7
  14.1 1.8 collective-permute-start.6
  15.9 1.1 reduce-window.26
  17.5 1.3 collective-permute-start
  18.9 0.9 fusion.53
  19.9 0.7 collective-permute-start.7
  20.8 1.2 fusion.5
  22.0 0.7 collective-permute-start.1
  22.7 0.7 collective-permute-start.2
  23.4 0.7 collective-permute-start.8
  24.1 0.7 collective-permute-start.5
  24.8 0.7 collective-permute-start.4
  25.4 0.7 collective-permute-start.3
  26.2 0.7 collective-permute-start.11
  26.9 0.7 collective-permute-start.10
  27.6 0.7 collective-permute-start.9
  28.5 0.7 collective-permute-start.12
  29.5 0.7 compare_reduce_fusion.1
  30.2 0.7 compare_reduce_fusion
  30.9 1.7 convolution_bitcast_fusion.3
  32.6 0.7 collective-permute-start.13
  33.3 1.3 collective-permute-start.14
  34.6 1.8 fusion.4
  36.4 41.1 %collective-permute-done.14 = f32[8,64,128]{2,1,0:T(8,128)S(1)} collective-permute-done((f32[8,64,128]{2,1,0:T(8,128)S(1)}, f32[8,64,128]{2,1,0:T(8,128)S(1)}, u32[]{:S(2)}, u32[]{:S(2)}) %collective-permute-start.14) | collective-permute-done | bytes 262176 | tf_op jit(solution)/shard_map/ppermute | solution.py:58
  77.5 0.8 fusion.2
  78.7 1.5 multiply_reduce_fusion
  80.3 1.4 fusion.40
  82.1 13.2 %all-gather.5.cloned.1.call-done = bf16[512,4096]{1,0:T(8,128)(2,1)} async-done(((bf16[512,256]{1,0:T(8,128)(2,1)}), bf16[512,4096]{1,0:T(8,128)(2,1)}) %all-gather.5.cloned.1.call-update) | async-done | bytes 4194320 | tf_op jit(solution)/shard_map/all_gather | solution.py:131
  95.3 4.6 %convolution_convert_fusion.1 = bf16[512,4096]{1,0:T(8,128)(2,1)S(1)} fusion(bf16[512,4096]{1,0:T(8,128)(2,1)} %all-gather.5.cloned.1.call-done, f32[512]{0:T(512)S(1)} %copy-done.10, f32[512,512]{1,0:T(8,128)S(1)} %copy.35, bf16[512,512]{1,0:T(8,128)(2,1)S(1)} %copy-done.3), kind=kOutput, calls=%fused_computation.1 | convolution fusion | flops 2151677952 | bytes 9963520 | tf_op jit(solution)/shard_map/dot_general | solution.py:165
  100.3 54.8 %all_to_all.20 = bf16[4,4,32,4224]{3,2,1,0:T(8,128)(2,1)} all-to-all(bf16[4,4,32,4224]{3,2,1,0:T(8,128)(2,1)S(1)} %bitcast.80), channel_id=1, replica_groups=mesh['sy'=4,'sz'=2,'sc'=2,'hx'=4,'hz'=4] {'hx'}, dimensions={0} | all-to-all | bytes 8650752 | tf_op jit(solution)/shard_map/all_to_all | solution.py:98
  155.1 3.0 reduce_sum.64
  158.1 31.0 %all_to_all.21 = bf16[4,32,4224]{2,1,0:T(8,128)(2,1)S(1)} all-to-all(bf16[4,32,4224]{2,1,0:T(8,128)(2,1)S(1)} %reduce_sum.64), channel_id=1, replica_groups=mesh['sy'=4,'sz'=2,'sc'=2,'hx'=4,'hz'=4] {'hz'}, dimensions={0} | all-to-all | bytes 2162688 | tf_op jit(solution)/shard_map/all_to_all | solution.py:100
  189.7 0.9 multiply_convert_fusion.10
  190.8 28.4 %all-gather.9.cloned.1.call-done = bf16[128,4096]{1,0:T(8,128)(2,1)} async-done(((bf16[32,4096]{1,0:T(8,128)(2,1)}), bf16[128,4096]{1,0:T(8,128)(2,1)}) %all-gather.9.cloned.1.call-update) | async-done | bytes 1048592 | tf_op jit(solution)/shard_map/all_gather | solution.py:105
  219.3 51.3 %all-gather.11.cloned.1.call-done = bf16[512,4096]{1,0:T(8,128)(2,1)} async-done(((bf16[128,4096]{1,0:T(8,128)(2,1)}), bf16[512,4096]{1,0:T(8,128)(2,1)}) %all-gather.11.cloned.1.call-update) | async-done | bytes 4194320 | tf_op jit(solution)/shard_map/all_gather | solution.py:106
  270.6 5.8 %fusion.69 = f32[512,512]{1,0:T(8,128)S(1)} fusion(bf16[512,4096]{1,0:T(8,128)(2,1)} %all-gather.11.cloned.1.call-done, bf16[4096,512]{1,0:T(8,128)(2,1)} %param.29), kind=kOutput, calls=%fused_computation.130 | convolution fusion | flops 2147483648 | bytes 9437184 | tf_op jit(solution)/shard_map/dot_general | solution.py:183
  276.4 11.2 %convolution_convert_fusion = bf16[512,4096]{1,0:T(8,128)(2,1)} fusion(bf16[512,4096]{1,0:T(8,128)(2,1)} %all-gather.7.cloned.1.call-done, bf16[512,4096]{1,0:T(8,128)(2,1)} %all-gather.11.cloned.1.call-done, bf16[4096,512]{1,0:T(8,128)(2,1)} %param.30, f32[512,512]{1,0:T(8,128)S(1)} %fusion.69), kind=kOutput, calls=%fused_computation | convolution fusion | flops 4298637312 | bytes 17825792 | tf_op jit(solution)/shard_map/dot_general | solution.py:186
  287.6 54.6 %all_to_all.22 = bf16[4,4,32,4096]{3,2,1,0:T(8,128)(2,1)} all-to-all(bf16[4,4,32,4096]{3,2,1,0:T(8,128)(2,1)} %bitcast.81), channel_id=1, replica_groups=mesh['sy'=4,'sz'=2,'sc'=2,'hx'=4,'hz'=4] {'hx'}, dimensions={0} | all-to-all | bytes 8388608 | tf_op jit(solution)/shard_map/all_to_all | solution.py:98
  342.2 3.1 reduce_sum.67
  345.3 29.1 %all_to_all.23 = bf16[4,32,4096]{2,1,0:T(8,128)(2,1)S(1)} all-to-all(bf16[4,32,4096]{2,1,0:T(8,128)(2,1)S(1)} %reduce_sum.67), channel_id=1, replica_groups=mesh['sy'=4,'sz'=2,'sc'=2,'hx'=4,'hz'=4] {'hz'}, dimensions={0} | all-to-all | bytes 2097152 | tf_op jit(solution)/shard_map/all_to_all | solution.py:100
  374.5 0.8 add_convert_fusion
  (84 shorter events, 5.4 us)
Async XLA Ops:
  6.5 12.3 %copy-start.2 = (bf16[2,512,128]{2,1,0:T(8,128)(2,1)S(1)}, bf16[2,512,128]{2,1,0:T(8,128)(2,1)}, u32[]{:S(2)}) copy-start(bf16[2,512,128]{2,1,0:T(8,128)(2,1)} %param.20) | copy-start | bytes 786436
  6.5 88.7 %all-gather.5.cloned.1.call-start = ((), (), s32[]{:S(2)}) async-start(), calls=%async_computation.4 | async-start | bytes 4456448 | tf_op jit(solution)/shard_map/all_gather | solution.py:131
  7.3 182.0 %all-gather.7.cloned.1.call-start = ((), (), s32[]{:S(2)}) async-start(), calls=%async_computation.5 | async-start | bytes 4456448 | tf_op jit(solution)/shard_map/all_gather | solution.py:132
  11.4 17.8 %copy-start.1 = (bf16[512,512]{1,0:T(8,128)(2,1)S(1)}, bf16[512,512]{1,0:T(8,128)(2,1)}, u32[]{:S(2)}) copy-start(bf16[512,512]{1,0:T(8,128)(2,1)} %param.18) | copy-start | bytes 1572868
  11.7 1.9 copy-start.4
  14.1 5.7 %collective-permute-start.6 = (f32[8,64,128]{2,1,0:T(8,128)S(1)}, f32[8,64,128]{2,1,0:T(8,128)S(1)}, u32[]{:S(2)}, u32[]{:S(2)}) collective-permute-start(f32[8,64,128]{2,1,0:T(8,128)S(1)} %fusion.6), channel_id=1, source_target_pairs={{0,16},{32,48},{1,17},{33,49},{2,18},{34,50},{3,19},{35,51},{4,20}... | collective-permute-start | bytes 786440 | tf_op jit(solution)/shard_map/ppermute | solution.py:58
  17.5 4.5 %collective-permute-start = (f32[8]{0:T(128)S(1)}, f32[8]{0:T(128)S(1)}, u32[]{:S(2)}, u32[]{:S(2)}) collective-permute-start(f32[8]{0:T(128)S(1)} %fusion.61), channel_id=1, source_target_pairs={{0,16},{32,48},{1,17},{33,49},{2,18},{34,50},{3,19},{35,51},{4,20}... | collective-permute-start | bytes 104 | tf_op jit(solution)/shard_map/ppermute | solution.py:58
  18.8 200.5 %all-gather.9.cloned.1.call-start = ((), (), s32[]{:S(2)}) async-start(), calls=%async_computation.6 | async-start | bytes 1310720 | tf_op jit(solution)/shard_map/all_gather | solution.py:105
  19.9 3.5 collective-permute-start.7
  22.0 0.7 collective-permute-start.1
  22.7 1.4 collective-permute-start.2
  23.4 5.8 %copy-start.5 = (f32[8,64,128]{2,1,0:T(8,128)}, f32[8,64,128]{2,1,0:T(8,128)S(1)}, u32[]{:S(2)}) copy-start(f32[8,64,128]{2,1,0:T(8,128)S(1)} %collective-permute-done.7) | copy-start | bytes 786436
  23.4 2.7 collective-permute-start.8
  24.1 2.0 collective-permute-start.5
  24.8 3.5 collective-permute-start.4
  25.4 2.9 collective-permute-start.3
  26.2 2.1 collective-permute-start.11
  26.9 1.4 collective-permute-start.10
  27.6 0.8 collective-permute-start.9
  28.5 4.8 %collective-permute-start.12 = (f32[8,64,128]{2,1,0:T(8,128)S(1)}, f32[8,64,128]{2,1,0:T(8,128)S(1)}, u32[]{:S(2)}, u32[]{:S(2)}) collective-permute-start(f32[8,64,128]{2,1,0:T(8,128)S(1)} %select_add_fusion), channel_id=1, source_target_pairs={{48,16},{49,17},{50,18},{51,19},{52,20},{53,21},{54,22},{55,23},{5... | collective-permute-start | bytes 786440 | tf_op jit(solution)/shard_map/ppermute | solution.py:58
  29.4 48.1 %copy-start.6 = (f32[8,64,128]{2,1,0:T(8,128)S(1)}, f32[8,64,128]{2,1,0:T(8,128)}, u32[]{:S(2)}) copy-start(f32[8,64,128]{2,1,0:T(8,128)} %copy-done.5) | copy-start | bytes 786436
  29.4 48.1 %copy-start.9 = (f32[8]{0:T(128)S(1)}, f32[8]{0:T(128)}, u32[]{:S(2)}) copy-start(f32[8]{0:T(128)} %param.24) | copy-start | bytes 100
  32.6 3.8 collective-permute-start.13
  33.3 44.2 %copy-start.7 = (f32[8,64,128]{2,1,0:T(8,128)}, f32[8,64,128]{2,1,0:T(8,128)S(1)}, u32[]{:S(2)}) copy-start(f32[8,64,128]{2,1,0:T(8,128)S(1)} %collective-permute-done.12) | copy-start | bytes 786436
  33.3 44.2 %collective-permute-start.14 = (f32[8,64,128]{2,1,0:T(8,128)S(1)}, f32[8,64,128]{2,1,0:T(8,128)S(1)}, u32[]{:S(2)}, u32[]{:S(2)}) collective-permute-start(f32[8,64,128]{2,1,0:T(8,128)S(1)} %collective-permute-done.12), channel_id=1, source_target_pairs={{16,0},{17,1},{18,2},{19,3},{20,4},{21,5},{22,6},{23,7},{24,8},{25... | collective-permute-start | bytes 786440 | tf_op jit(solution)/shard_map/ppermute | solution.py:58
  77.5 17.8 %copy-start.10 = (f32[512]{0:T(512)S(1)}, f32[512]{0:T(512)}, u32[]{:S(2)}) copy-start(f32[512]{0:T(512)} %param.25) | copy-start | bytes 6148
  78.3 17.0 %copy-start.3 = (bf16[512,512]{1,0:T(8,128)(2,1)S(1)}, bf16[512,512]{1,0:T(8,128)(2,1)}, u32[]{:S(2)}) copy-start(bf16[512,512]{1,0:T(8,128)(2,1)} %param.19) | copy-start | bytes 1572868
  155.1 34.4 %copy-start = (bf16[32,4096]{1,0:T(8,128)(2,1)S(1)}, bf16[32,4096]{1,0:T(8,128)(2,1)}, u32[]{:S(2)}) copy-start(bf16[32,4096]{1,0:T(8,128)(2,1)} %param.27) | copy-start | bytes 786436
  155.1 34.6 %copy-start.8 = (f32[4096]{0:T(1024)S(1)}, f32[4096]{0:T(1024)}, u32[]{:S(2)}) copy-start(f32[4096]{0:T(1024)} %param.28) | copy-start | bytes 49156
  190.6 80.0 %all-gather.11.cloned.1.call-start = ((), (), s32[]{:S(2)}) async-start(), calls=%async_computation.7 | async-start | bytes 5242880 | tf_op jit(solution)/shard_map/all_gather | solution.py:106
Sparse Core Ops, SparseCore 0:
  9.9 85.3 all-gather.4
  97.8 76.5 all-gather.6
  190.7 28.4 all-gather.8
  220.9 49.6 all-gather.10

commit v8 on v7

--- a/solution.py
+++ b/solution.py
@@ -92,11 +92,27 @@
     return combine(prefix, inner)[1]
 
 
+def ring_sum_x(pieces):
+    nx = pieces.shape[0]
+    x = lax.axis_index("hx")
+    half = pieces.shape[2] // 2
+    ways = ((1, pieces[:, :, :half]), (-1, pieces[:, :, half:]))
+    accs = []
+    for way, part in ways:
+        pairs = [(src, (src + way) % nx) for src in range(nx)]
+        acc = jnp.take(part, (x - way) % nx, axis=0).astype(jnp.float32)
+        for step in range(nx - 1):
+            got = lax.ppermute(acc.astype(jnp.bfloat16), "hx", pairs)
+            chunk = (x - way * (step + 2)) % nx
+            acc = got.astype(jnp.float32) + jnp.take(part, chunk, axis=0).astype(jnp.float32)
+        accs.append(acc)
+    return jnp.concatenate(accs, axis=1)
+
+
 def sum_over_head(value):
     nx, nz = lax.axis_size("hx"), lax.axis_size("hz")
     pieces = value.reshape(nx, nz, value.shape[0] // (nx * nz), value.shape[1])
-    pieces = lax.all_to_all(pieces, "hx", 0, 0, tiled=False)
-    pieces = jnp.sum(pieces.astype(jnp.float32), axis=0).astype(jnp.bfloat16)
+    pieces = ring_sum_x(pieces).astype(jnp.bfloat16)
     pieces = lax.all_to_all(pieces, "hz", 0, 0, tiled=False)
     return jnp.sum(pieces.astype(jnp.float32), axis=0)
 

time: 383 us -> 369 us (0.963)
  blocking collectives: 169 us -> 61.6 us
  waiting for transfers between devices: 135 us -> 212 us
  starting transfers between devices: 12.7 us -> 32.1 us
  other arithmetic: 18.8 us -> 13.2 us
    all_to_all x2 -> x0, blocking collectives: 109 us -> none  [sum_over_head(): pieces = lax.all_to_all(pieces, 'hx', 0, 0, tiled=False)]
    ppermute x0 -> x12, waiting for transfers between devices: none -> 69.8 us  [ring_sum_x(): got = lax.ppermute(acc.astype(jnp.bfloat16), 'hx', pairs)]
    ppermute x0 -> x12, starting transfers between devices: none -> 19.4 us  [ring_sum_x(): got = lax.ppermute(acc.astype(jnp.bfloat16), 'hx', pairs)]
    reduce_sum x2 -> x0, other arithmetic: 6.06 us -> none  [sum_over_head(): pieces = jnp.sum(pieces.astype(jnp.float32), axis=0).astype(jnp.bfloat16)]
    all_gather x1, waiting for transfers between devices: 28.4 us -> 33.4 us  [gather_over_head(): value = lax.all_gather(value, 'hz', axis=0, tiled=True)]
    all_gather x1, waiting for transfers between devices: 13.2 us -> 18 us  [shards(): lax.all_gather(out_weight, SEQ, axis=1, tiled=True)]
  transfers between devices with their start and end apart: 19 -> 31, of which waited for: 4 -> 12; matrix products, arithmetic and copies ran while one was open for 8% -> 7% of each run, Pallas kernels for 0% -> 0%
where the time goes in v8:
time: 369 us; the launch traced here: 368 us
  waiting for transfers between devices  212 us (57%)
  blocking collectives  61.6 us (17%)
  starting transfers between devices  32.1 us (9%)
  matrix products  28.3 us (8%)
  between operations  14.1 us (4%)
  other arithmetic  13.2 us (4%)
  local copies, waits for them, and re-layouts  6.94 us (2%)
    ppermute x12, waiting for transfers between devices, ring_sum_x(): got = lax.ppermute(acc.astype(jnp.bfloat16), 'hx', pairs)  69.8 us
    all_to_all x2, blocking collectives, sum_over_head(): pieces = lax.all_to_all(pieces, 'hz', 0, 0, tiled=False)  61.6 us
    all_gather x1, waiting for transfers between devices, gather_over_head(): return lax.all_gather(value, 'hx', axis=0, tiled=True)  51.3 us
    ppermute x15, waiting for transfers between devices, send(): return tuple((lax.ppermute(v, axes, pairs) for v in pair))  38.6 us
    all_gather x1, waiting for transfers between devices, gather_over_head(): value = lax.all_gather(value, 'hz', axis=0, tiled=True)  33.4 us
    ppermute x12, starting transfers between devices, ring_sum_x(): got = lax.ppermute(acc.astype(jnp.bfloat16), 'hx', pairs)  19.4 us
    all_gather x1, waiting for transfers between devices, shards(): lax.all_gather(out_weight, SEQ, axis=1, tiled=True)  18 us
    ppermute x15, starting transfers between devices, send(): return tuple((lax.ppermute(v, axes, pairs) for v in pair))  12.6 us
  transfers between devices with their start and end apart: 31, of which 12 were waited for; matrix products, arithmetic and copies ran while one was open for 7% of the time, Pallas kernels for 0%

profile of v8, /device:TPU:8, one launch (start us, length us, event | category | flops | bytes accessed | tf_op | source)
XLA Modules:
  0.0 368.1 jit_solution(86507266269265216)
XLA Ops:
  6.5 0.7 all-gather.5.cloned.1.call-update
  8.0 0.8 broadcast_multiply_fusion
  10.3 1.1 fusion.70
  13.2 1.8 collective-permute-start.6
  15.0 1.1 reduce-window.26
  16.6 1.3 collective-permute-start
  18.0 0.9 fusion.53
  19.0 0.8 collective-permute-start.7
  20.0 1.2 fusion.5
  25.5 0.7 collective-permute-start.11
  26.1 0.7 collective-permute-start.10
  26.8 0.7 collective-permute-start.9
  28.9 0.7 compare_reduce_fusion.1
  29.6 0.7 compare_reduce_fusion
  30.3 1.7 convolution_bitcast_fusion.3
  32.1 0.8 collective-permute-start.13
  32.9 1.3 collective-permute-start.14
  34.2 0.7 fusion.4
  35.0 38.5 %collective-permute-done.14 = f32[8,64,128]{2,1,0:T(8,128)S(1)} collective-permute-done((f32[8,64,128]{2,1,0:T(8,128)S(1)}, f32[8,64,128]{2,1,0:T(8,128)S(1)}, u32[]{:S(2)}, u32[]{:S(2)}) %collective-permute-start.14) | collective-permute-done | bytes 262176 | tf_op jit(solution)/shard_map/ppermute | solution.py:58
  73.5 0.8 fusion.2
  74.7 0.7 copy-done.3
  75.9 1.4 fusion.40
  77.8 18.0 %all-gather.5.cloned.1.call-done = bf16[512,4096]{1,0:T(8,128)(2,1)} async-done(((bf16[512,256]{1,0:T(8,128)(2,1)}), bf16[512,4096]{1,0:T(8,128)(2,1)}) %all-gather.5.cloned.1.call-update) | async-done | bytes 4194320 | tf_op jit(solution)/shard_map/all_gather | solution.py:147
  95.8 4.6 %convolution_convert_fusion.1 = bf16[512,4096]{1,0:T(8,128)(2,1)S(1)} fusion(bf16[512,4096]{1,0:T(8,128)(2,1)} %all-gather.5.cloned.1.call-done, f32[512]{0:T(512)S(1)} %copy-done.11, f32[512,512]{1,0:T(8,128)S(1)} %copy.29, bf16[512,512]{1,0:T(8,128)(2,1)S(1)} %copy-done.3), kind=kOutput, calls=%fused_computation.1 | convolution fusion | flops 2151677952 | bytes 9963520 | tf_op jit(solution)/shard_map/dot_general | solution.py:181
  101.2 2.8 collective-permute-start.18
  104.3 11.6 %collective-permute-done.18 = bf16[4,16,4224]{2,1,0:T(8,128)(2,1)S(1)} collective-permute-done((bf16[4,16,4224]{2,1,0:T(8,128)(2,1)S(1)}, bf16[4,16,4224]{2,1,0:T(8,128)(2,1)S(1)}, u32[]{:S(2)}, u32[]{:S(2)}) %collective-permute-start.18) | collective-permute-done | bytes 540704 | tf_op jit(solution)/shard_map/ppermute | solution.py:105
  116.1 3.8 %collective-permute-start.19 = (bf16[4,16,4224]{2,1,0:T(8,128)(2,1)S(1)}, bf16[4,16,4224]{2,1,0:T(8,128)(2,1)S(1)}, u32[]{:S(2)}, u32[]{:S(2)}) collective-permute-start(bf16[4,16,4224]{2,1,0:T(8,128)(2,1)S(1)} %add_convert_fusion.2), channel_id=1, source_target_pairs={{0,12},{4,0},{8,4},{12,8},{1,13},{5,1},{9,5},{13,9},{2,14},{6,2},{... | collective-permute-start | bytes 1622024 | tf_op jit(solution)/shard_map/ppermute | solution.py:105
  120.1 10.8 %collective-permute-done.19 = bf16[4,16,4224]{2,1,0:T(8,128)(2,1)S(1)} collective-permute-done((bf16[4,16,4224]{2,1,0:T(8,128)(2,1)S(1)}, bf16[4,16,4224]{2,1,0:T(8,128)(2,1)S(1)}, u32[]{:S(2)}, u32[]{:S(2)}) %collective-permute-start.19) | collective-permute-done | bytes 540704 | tf_op jit(solution)/shard_map/ppermute | solution.py:105
  131.1 3.8 %collective-permute-start.20 = (bf16[4,16,4224]{2,1,0:T(8,128)(2,1)S(1)}, bf16[4,16,4224]{2,1,0:T(8,128)(2,1)S(1)}, u32[]{:S(2)}, u32[]{:S(2)}) collective-permute-start(bf16[4,16,4224]{2,1,0:T(8,128)(2,1)S(1)} %add_convert_fusion.1), channel_id=1, source_target_pairs={{0,12},{4,0},{8,4},{12,8},{1,13},{5,1},{9,5},{13,9},{2,14},{6,2},{... | collective-permute-start | bytes 1622024 | tf_op jit(solution)/shard_map/ppermute | solution.py:105
  135.2 10.0 %collective-permute-done.20 = bf16[4,16,4224]{2,1,0:T(8,128)(2,1)S(1)} collective-permute-done((bf16[4,16,4224]{2,1,0:T(8,128)(2,1)S(1)}, bf16[4,16,4224]{2,1,0:T(8,128)(2,1)S(1)}, u32[]{:S(2)}, u32[]{:S(2)}) %collective-permute-start.20) | collective-permute-done | bytes 540704 | tf_op jit(solution)/shard_map/ppermute | solution.py:105
  145.3 3.5 collective-permute-done.17
  149.1 34.4 %all_to_all.10 = bf16[4,32,4224]{2,1,0:T(8,128)(2,1)S(1)} all-to-all(bf16[4,32,4224]{2,1,0:T(8,128)(2,1)S(1)} %pad_maximum_fusion.1), channel_id=1, replica_groups=mesh['sy'=4,'sz'=2,'sc'=2,'hx'=4,'hz'=4] {'hz'}, dimensions={0} | all-to-all | bytes 2162688 | tf_op jit(solution)/shard_map/all_to_all | solution.py:116
  184.1 0.9 multiply_convert_fusion.10
  185.0 33.4 %all-gather.9.cloned.1.call-done = bf16[128,4096]{1,0:T(8,128)(2,1)} async-done(((bf16[32,4096]{1,0:T(8,128)(2,1)}), bf16[128,4096]{1,0:T(8,128)(2,1)}) %all-gather.9.cloned.1.call-update) | async-done | bytes 1048592 | tf_op jit(solution)/shard_map/all_gather | solution.py:121
  218.4 51.3 %all-gather.11.cloned.1.call-done = bf16[512,4096]{1,0:T(8,128)(2,1)} async-done(((bf16[128,4096]{1,0:T(8,128)(2,1)}), bf16[512,4096]{1,0:T(8,128)(2,1)}) %all-gather.11.cloned.1.call-update) | async-done | bytes 4194320 | tf_op jit(solution)/shard_map/all_gather | solution.py:122
  269.7 5.8 %fusion.71 = f32[512,512]{1,0:T(8,128)S(1)} fusion(bf16[512,4096]{1,0:T(8,128)(2,1)} %all-gather.11.cloned.1.call-done, bf16[4096,512]{1,0:T(8,128)(2,1)} %param.33), kind=kOutput, calls=%fused_computation.150 | convolution fusion | flops 2147483648 | bytes 9437184 | tf_op jit(solution)/shard_map/dot_general | solution.py:199
  275.5 11.3 %convolution_convert_fusion = bf16[512,4096]{1,0:T(8,128)(2,1)} fusion(bf16[512,4096]{1,0:T(8,128)(2,1)} %all-gather.7.cloned.1.call-done, bf16[512,4096]{1,0:T(8,128)(2,1)} %all-gather.11.cloned.1.call-done, bf16[4096,512]{1,0:T(8,128)(2,1)} %param.34, f32[512,512]{1,0:T(8,128)S(1)} %fusion.71), kind=kOutput, calls=%fused_computation | convolution fusion | flops 4298637312 | bytes 17825792 | tf_op jit(solution)/shard_map/dot_general | solution.py:202
  286.8 2.7 fusion.69
  289.6 1.2 collective-permute-start.24
  290.9 1.0 collective-permute-start.21
  291.8 11.3 %collective-permute-done.24 = bf16[4,16,4096]{2,1,0:T(8,128)(2,1)S(1)} collective-permute-done((bf16[4,16,4096]{2,1,0:T(8,128)(2,1)S(1)}, bf16[4,16,4096]{2,1,0:T(8,128)(2,1)S(1)}, u32[]{:S(2)}, u32[]{:S(2)}) %collective-permute-start.24) | collective-permute-done | bytes 524320 | tf_op jit(solution)/shard_map/ppermute | solution.py:105
  303.3 2.7 collective-permute-start.25
  306.2 10.0 %collective-permute-done.25 = bf16[4,16,4096]{2,1,0:T(8,128)(2,1)S(1)} collective-permute-done((bf16[4,16,4096]{2,1,0:T(8,128)(2,1)S(1)}, bf16[4,16,4096]{2,1,0:T(8,128)(2,1)S(1)}, u32[]{:S(2)}, u32[]{:S(2)}) %collective-permute-start.25) | collective-permute-done | bytes 524320 | tf_op jit(solution)/shard_map/ppermute | solution.py:105
  316.4 3.6 collective-permute-start.26
  320.3 9.1 %collective-permute-done.26 = bf16[4,16,4096]{2,1,0:T(8,128)(2,1)S(1)} collective-permute-done((bf16[4,16,4096]{2,1,0:T(8,128)(2,1)S(1)}, bf16[4,16,4096]{2,1,0:T(8,128)(2,1)S(1)}, u32[]{:S(2)}, u32[]{:S(2)}) %collective-permute-start.26) | collective-permute-done | bytes 524320 | tf_op jit(solution)/shard_map/ppermute | solution.py:105
  329.5 3.5 collective-permute-done.23
  333.3 27.3 %all_to_all.11 = bf16[4,32,4096]{2,1,0:T(8,128)(2,1)S(1)} all-to-all(bf16[4,32,4096]{2,1,0:T(8,128)(2,1)S(1)} %pad_maximum_fusion.2), channel_id=1, replica_groups=mesh['sy'=4,'sz'=2,'sc'=2,'hx'=4,'hz'=4] {'hz'}, dimensions={0} | all-to-all | bytes 2097152 | tf_op jit(solution)/shard_map/all_to_all | solution.py:116
  360.7 0.8 add_convert_fusion.12
  (126 shorter events, 15.9 us)
Async XLA Ops:
  6.5 5.6 %copy-start.2 = (bf16[2,512,128]{2,1,0:T(8,128)(2,1)S(1)}, bf16[2,512,128]{2,1,0:T(8,128)(2,1)}, u32[]{:S(2)}) copy-start(bf16[2,512,128]{2,1,0:T(8,128)(2,1)} %param.24) | copy-start | bytes 786436
  6.5 89.2 %all-gather.5.cloned.1.call-start = ((), (), s32[]{:S(2)}) async-start(), calls=%async_computation.2 | async-start | bytes 4456448 | tf_op jit(solution)/shard_map/all_gather | solution.py:147
  7.3 176.4 %all-gather.7.cloned.1.call-start = ((), (), s32[]{:S(2)}) async-start(), calls=%async_computation.3 | async-start | bytes 4456448 | tf_op jit(solution)/shard_map/all_gather | solution.py:148
  11.7 1.0 copy-start.5
  13.2 5.7 %collective-permute-start.6 = (f32[8,64,128]{2,1,0:T(8,128)S(1)}, f32[8,64,128]{2,1,0:T(8,128)S(1)}, u32[]{:S(2)}, u32[]{:S(2)}) collective-permute-start(f32[8,64,128]{2,1,0:T(8,128)S(1)} %fusion.6), channel_id=1, source_target_pairs={{0,16},{32,48},{1,17},{33,49},{2,18},{34,50},{3,19},{35,51},{4,20}... | collective-permute-start | bytes 786440 | tf_op jit(solution)/shard_map/ppermute | solution.py:58
  16.6 4.6 %collective-permute-start = (f32[8]{0:T(128)S(1)}, f32[8]{0:T(128)S(1)}, u32[]{:S(2)}, u32[]{:S(2)}) collective-permute-start(f32[8]{0:T(128)S(1)} %fusion.61), channel_id=1, source_target_pairs={{0,16},{32,48},{1,17},{33,49},{2,18},{34,50},{3,19},{35,51},{4,20}... | collective-permute-start | bytes 104 | tf_op jit(solution)/shard_map/ppermute | solution.py:58
  17.9 200.5 %all-gather.9.cloned.1.call-start = ((), (), s32[]{:S(2)}) async-start(), calls=%async_computation.4 | async-start | bytes 1310720 | tf_op jit(solution)/shard_map/all_gather | solution.py:121
  18.9 9.7 %copy-start.1 = (bf16[512,512]{1,0:T(8,128)(2,1)S(1)}, bf16[512,512]{1,0:T(8,128)(2,1)}, u32[]{:S(2)}) copy-start(bf16[512,512]{1,0:T(8,128)(2,1)} %param.22) | copy-start | bytes 1572868
  19.0 3.6 collective-permute-start.7
  21.3 0.7 collective-permute-start.1
  21.9 1.4 collective-permute-start.2
  22.6 6.0 %copy-start.6 = (f32[8,64,128]{2,1,0:T(8,128)}, f32[8,64,128]{2,1,0:T(8,128)S(1)}, u32[]{:S(2)}) copy-start(f32[8,64,128]{2,1,0:T(8,128)S(1)} %collective-permute-done.7) | copy-start | bytes 786436
  22.6 2.7 collective-permute-start.8
  23.3 2.0 collective-permute-start.5
  24.0 3.5 collective-permute-start.4
  24.7 2.9 collective-permute-start.3
  25.5 2.1 collective-permute-start.11
  26.1 1.4 collective-permute-start.10
  26.8 0.8 collective-permute-start.9
  27.7 5.2 %collective-permute-start.12 = (f32[8,64,128]{2,1,0:T(8,128)S(1)}, f32[8,64,128]{2,1,0:T(8,128)S(1)}, u32[]{:S(2)}, u32[]{:S(2)}) collective-permute-start(f32[8,64,128]{2,1,0:T(8,128)S(1)} %select_add_fusion), channel_id=1, source_target_pairs={{48,16},{49,17},{50,18},{51,19},{52,20},{53,21},{54,22},{55,23},{5... | collective-permute-start | bytes 786440 | tf_op jit(solution)/shard_map/ppermute | solution.py:58
  28.9 5.4 %copy-start.4 = (f32[256,8,64]{0,2,1:T(8,128)S(1)}, f32[256,8,64]{0,2,1:T(8,128)}, u32[]{:S(2)}) copy-start(f32[256,8,64]{0,2,1:T(8,128)} %fusion.5) | copy-start | bytes 1572868
  32.1 41.5 %copy-start.7 = (f32[8,64,128]{2,1,0:T(8,128)S(1)}, f32[8,64,128]{2,1,0:T(8,128)}, u32[]{:S(2)}) copy-start(f32[8,64,128]{2,1,0:T(8,128)} %copy-done.6) | copy-start | bytes 786436
  32.1 41.4 %copy-start.10 = (f32[8]{0:T(128)S(1)}, f32[8]{0:T(128)}, u32[]{:S(2)}) copy-start(f32[8]{0:T(128)} %param.28) | copy-start | bytes 100
  32.1 2.9 collective-permute-start.13
  32.9 40.6 %copy-start.8 = (f32[8,64,128]{2,1,0:T(8,128)}, f32[8,64,128]{2,1,0:T(8,128)S(1)}, u32[]{:S(2)}) copy-start(f32[8,64,128]{2,1,0:T(8,128)S(1)} %collective-permute-done.12) | copy-start | bytes 786436
  32.9 40.6 %collective-permute-start.14 = (f32[8,64,128]{2,1,0:T(8,128)S(1)}, f32[8,64,128]{2,1,0:T(8,128)S(1)}, u32[]{:S(2)}, u32[]{:S(2)}) collective-permute-start(f32[8,64,128]{2,1,0:T(8,128)S(1)} %collective-permute-done.12), channel_id=1, source_target_pairs={{16,0},{17,1},{18,2},{19,3},{20,4},{21,5},{22,6},{23,7},{24,8},{25... | collective-permute-start | bytes 786440 | tf_op jit(solution)/shard_map/ppermute | solution.py:58
  74.3 1.0 copy-start.3
  74.3 21.4 %copy-start.11 = (f32[512]{0:T(512)S(1)}, f32[512]{0:T(512)}, u32[]{:S(2)}) copy-start(f32[512]{0:T(512)} %param.29) | copy-start | bytes 6148
  101.2 14.7 %collective-permute-start.18 = (bf16[4,16,4224]{2,1,0:T(8,128)(2,1)S(1)}, bf16[4,16,4224]{2,1,0:T(8,128)(2,1)S(1)}, u32[]{:S(2)}, u32[]{:S(2)}) collective-permute-start(bf16[4,16,4224]{2,1,0:T(8,128)(2,1)S(1)} %select_bitcast_fusion), channel_id=1, source_target_pairs={{0,12},{4,0},{8,4},{12,8},{1,13},{5,1},{9,5},{13,9},{2,14},{6,2},{... | collective-permute-start | bytes 1622024 | tf_op jit(solution)/shard_map/ppermute | solution.py:105
  104.0 15.8 %collective-permute-start.15 = (bf16[4,16,4224]{2,1,0:T(8,128)(2,1)S(1)}, bf16[4,16,4224]{2,1,0:T(8,128)(2,1)S(1)}, u32[]{:S(2)}, u32[]{:S(2)}) collective-permute-start(bf16[4,16,4224]{2,1,0:T(8,128)(2,1)S(1)} %select_bitcast_fusion.1), channel_id=1, source_target_pairs={{0,4},{4,8},{8,12},{12,0},{1,5},{5,9},{9,13},{13,1},{2,6},{6,10},{... | collective-permute-start | bytes 1622024 | tf_op jit(solution)/shard_map/ppermute | solution.py:105
  116.1 14.9 %collective-permute-start.19 = (bf16[4,16,4224]{2,1,0:T(8,128)(2,1)S(1)}, bf16[4,16,4224]{2,1,0:T(8,128)(2,1)S(1)}, u32[]{:S(2)}, u32[]{:S(2)}) collective-permute-start(bf16[4,16,4224]{2,1,0:T(8,128)(2,1)S(1)} %add_convert_fusion.2), channel_id=1, source_target_pairs={{0,12},{4,0},{8,4},{12,8},{1,13},{5,1},{9,5},{13,9},{2,14},{6,2},{... | collective-permute-start | bytes 1622024 | tf_op jit(solution)/shard_map/ppermute | solution.py:105
  120.0 14.9 %collective-permute-start.16 = (bf16[4,16,4224]{2,1,0:T(8,128)(2,1)S(1)}, bf16[4,16,4224]{2,1,0:T(8,128)(2,1)S(1)}, u32[]{:S(2)}, u32[]{:S(2)}) collective-permute-start(bf16[4,16,4224]{2,1,0:T(8,128)(2,1)S(1)} %add_convert_fusion.5), channel_id=1, source_target_pairs={{0,4},{4,8},{8,12},{12,0},{1,5},{5,9},{9,13},{13,1},{2,6},{6,10},{... | collective-permute-start | bytes 1622024 | tf_op jit(solution)/shard_map/ppermute | solution.py:105
  131.1 14.0 %collective-permute-start.20 = (bf16[4,16,4224]{2,1,0:T(8,128)(2,1)S(1)}, bf16[4,16,4224]{2,1,0:T(8,128)(2,1)S(1)}, u32[]{:S(2)}, u32[]{:S(2)}) collective-permute-start(bf16[4,16,4224]{2,1,0:T(8,128)(2,1)S(1)} %add_convert_fusion.1), channel_id=1, source_target_pairs={{0,12},{4,0},{8,4},{12,8},{1,13},{5,1},{9,5},{13,9},{2,14},{6,2},{... | collective-permute-start | bytes 1622024 | tf_op jit(solution)/shard_map/ppermute | solution.py:105
  135.1 13.7 %collective-permute-start.17 = (bf16[4,16,4224]{2,1,0:T(8,128)(2,1)S(1)}, bf16[4,16,4224]{2,1,0:T(8,128)(2,1)S(1)}, u32[]{:S(2)}, u32[]{:S(2)}) collective-permute-start(bf16[4,16,4224]{2,1,0:T(8,128)(2,1)S(1)} %add_convert_fusion.4), channel_id=1, source_target_pairs={{0,4},{4,8},{8,12},{12,0},{1,5},{5,9},{9,13},{13,1},{2,6},{6,10},{... | collective-permute-start | bytes 1622024 | tf_op jit(solution)/shard_map/ppermute | solution.py:105
  149.0 34.8 %copy-start = (bf16[32,4096]{1,0:T(8,128)(2,1)S(1)}, bf16[32,4096]{1,0:T(8,128)(2,1)}, u32[]{:S(2)}) copy-start(bf16[32,4096]{1,0:T(8,128)(2,1)} %param.31) | copy-start | bytes 786436
  149.1 35.0 %copy-start.9 = (f32[4096]{0:T(1024)S(1)}, f32[4096]{0:T(1024)}, u32[]{:S(2)}) copy-start(f32[4096]{0:T(1024)} %param.32) | copy-start | bytes 49156
  185.0 84.7 %all-gather.11.cloned.1.call-start = ((), (), s32[]{:S(2)}) async-start(), calls=%async_computation.5 | async-start | bytes 5242880 | tf_op jit(solution)/shard_map/all_gather | solution.py:122
  289.6 13.6 %collective-permute-start.24 = (bf16[4,16,4096]{2,1,0:T(8,128)(2,1)S(1)}, bf16[4,16,4096]{2,1,0:T(8,128)(2,1)S(1)}, u32[]{:S(2)}, u32[]{:S(2)}) collective-permute-start(bf16[4,16,4096]{2,1,0:T(8,128)(2,1)S(1)} %select_bitcast_fusion.2), channel_id=1, source_target_pairs={{0,12},{4,0},{8,4},{12,8},{1,13},{5,1},{9,5},{13,9},{2,14},{6,2},{... | collective-permute-start | bytes 1572872 | tf_op jit(solution)/shard_map/ppermute | solution.py:105
  290.9 15.1 %collective-permute-start.21 = (bf16[4,16,4096]{2,1,0:T(8,128)(2,1)S(1)}, bf16[4,16,4096]{2,1,0:T(8,128)(2,1)S(1)}, u32[]{:S(2)}, u32[]{:S(2)}) collective-permute-start(bf16[4,16,4096]{2,1,0:T(8,128)(2,1)S(1)} %select_bitcast_fusion.3), channel_id=1, source_target_pairs={{0,4},{4,8},{8,12},{12,0},{1,5},{5,9},{9,13},{13,1},{2,6},{6,10},{... | collective-permute-start | bytes 1572872 | tf_op jit(solution)/shard_map/ppermute | solution.py:105
  303.3 12.9 %collective-permute-start.25 = (bf16[4,16,4096]{2,1,0:T(8,128)(2,1)S(1)}, bf16[4,16,4096]{2,1,0:T(8,128)(2,1)S(1)}, u32[]{:S(2)}, u32[]{:S(2)}) collective-permute-start(bf16[4,16,4096]{2,1,0:T(8,128)(2,1)S(1)} %add_convert_fusion.8), channel_id=1, source_target_pairs={{0,12},{4,0},{8,4},{12,8},{1,13},{5,1},{9,5},{13,9},{2,14},{6,2},{... | collective-permute-start | bytes 1572872 | tf_op jit(solution)/shard_map/ppermute | solution.py:105
  306.1 13.9 %collective-permute-start.22 = (bf16[4,16,4096]{2,1,0:T(8,128)(2,1)S(1)}, bf16[4,16,4096]{2,1,0:T(8,128)(2,1)S(1)}, u32[]{:S(2)}, u32[]{:S(2)}) collective-permute-start(bf16[4,16,4096]{2,1,0:T(8,128)(2,1)S(1)} %add_convert_fusion.11), channel_id=1, source_target_pairs={{0,4},{4,8},{8,12},{12,0},{1,5},{5,9},{9,13},{13,1},{2,6},{6,10},{... | collective-permute-start | bytes 1572872 | tf_op jit(solution)/shard_map/ppermute | solution.py:105
  316.4 13.0 %collective-permute-start.26 = (bf16[4,16,4096]{2,1,0:T(8,128)(2,1)S(1)}, bf16[4,16,4096]{2,1,0:T(8,128)(2,1)S(1)}, u32[]{:S(2)}, u32[]{:S(2)}) collective-permute-start(bf16[4,16,4096]{2,1,0:T(8,128)(2,1)S(1)} %add_convert_fusion.7), channel_id=1, source_target_pairs={{0,12},{4,0},{8,4},{12,8},{1,13},{5,1},{9,5},{13,9},{2,14},{6,2},{... | collective-permute-start | bytes 1572872 | tf_op jit(solution)/shard_map/ppermute | solution.py:105
  320.2 12.8 %collective-permute-start.23 = (bf16[4,16,4096]{2,1,0:T(8,128)(2,1)S(1)}, bf16[4,16,4096]{2,1,0:T(8,128)(2,1)S(1)}, u32[]{:S(2)}, u32[]{:S(2)}) collective-permute-start(bf16[4,16,4096]{2,1,0:T(8,128)(2,1)S(1)} %add_convert_fusion.10), channel_id=1, source_target_pairs={{0,4},{4,8},{8,12},{12,0},{1,5},{5,9},{9,13},{13,1},{2,6},{6,10},{... | collective-permute-start | bytes 1572872 | tf_op jit(solution)/shard_map/ppermute | solution.py:105
Sparse Core Ops, SparseCore 0:
  9.9 85.8 all-gather.4
  98.3 78.7 all-gather.6
  185.1 33.2 all-gather.8
  220.1 49.6 all-gather.10

commit v9 on v8

--- a/solution.py
+++ b/solution.py
@@ -117,9 +117,25 @@
     return jnp.sum(pieces.astype(jnp.float32), axis=0)
 
 
+def ring_gather_x(value):
+    nx = lax.axis_size("hx")
+    x = lax.axis_index("hx")
+    half = value.shape[0] // 2
+    slots = jnp.arange(nx)
+    outs = []
+    for way, part in ((1, value[:half]), (-1, value[half:])):
+        pairs = [(src, (src + way) % nx) for src in range(nx)]
+        got = [part]
+        for step in range(nx - 1):
+            got.append(lax.ppermute(got[-1], "hx", pairs))
+        stacked = jnp.stack(got)
+        outs.append(jnp.take(stacked, (way * (x - slots)) % nx, axis=0))
+    return jnp.concatenate(outs, axis=1).reshape(nx * value.shape[0], value.shape[1])
+
+
 def gather_over_head(value):
     value = lax.all_gather(value, "hz", axis=0, tiled=True)
-    return lax.all_gather(value, "hx", axis=0, tiled=True)
+    return ring_gather_x(value)
 
 
 def normalize_rows(layer_sum, mlp_gain):

time: 369 us -> 360 us (0.976)
  waiting for transfers between devices: 212 us -> 181 us
  starting transfers between devices: 32.1 us -> 45.5 us
  local copies, waits for them, and re-layouts: 6.94 us -> 15.8 us
  other arithmetic: 13.2 us -> 20.5 us
  blocking collectives: 61.6 us -> 57.2 us
    all_gather x1 -> x0, waiting for transfers between devices: 51.3 us -> none  [gather_over_head(): return lax.all_gather(value, 'hx', axis=0, tiled=True)]
    ppermute x0 -> x6, waiting for transfers between devices: none -> 28.2 us  [ring_gather_x(): got.append(lax.ppermute(got[-1], 'hx', pairs))]
    ppermute x0 -> x6, starting transfers between devices: none -> 10.5 us  [ring_gather_x(): got.append(lax.ppermute(got[-1], 'hx', pairs))]
    ppermute x12, waiting for transfers between devices: 69.8 us -> 62.1 us  [ring_sum_x(): got = lax.ppermute(acc.astype(jnp.bfloat16), 'hx', pairs)]
    select_n x0 -> x4, other arithmetic: none -> 5.26 us  [ring_gather_x(): outs.append(jnp.take(stacked, way * (x - slots) % nx, axis=0))]
    all_to_all x2, blocking collectives: 61.6 us -> 57.2 us  [sum_over_head(): pieces = lax.all_to_all(pieces, 'hz', 0, 0, tiled=False)]
    gather x0 -> x2, local copies, waits for them, and re-layouts: none -> 4.04 us  [ring_gather_x(): outs.append(jnp.take(stacked, way * (x - slots) % nx, axis=0))]
    another operation x14 -> x16, other arithmetic: 5.9 us -> 7.47 us
  transfers between devices with their start and end apart: 31 -> 36, of which waited for: 12 -> 14; matrix products, arithmetic and copies ran while one was open for 7% -> 9% of each run, Pallas kernels for 0% -> 0%
where the time goes in v9:
time: 360 us; the launch traced here: 359 us
  waiting for transfers between devices  181 us (50%)
  blocking collectives  57.2 us (16%)
  starting transfers between devices  45.5 us (13%)
  matrix products  24.8 us (7%)
  other arithmetic  20.5 us (6%)
  local copies, waits for them, and re-layouts  15.8 us (4%)
  between operations  14.1 us (4%)
    ppermute x12, waiting for transfers between devices, ring_sum_x(): got = lax.ppermute(acc.astype(jnp.bfloat16), 'hx', pairs)  62.1 us
    all_to_all x2, blocking collectives, sum_over_head(): pieces = lax.all_to_all(pieces, 'hz', 0, 0, tiled=False)  57.2 us
    ppermute x15, waiting for transfers between devices, send(): return tuple((lax.ppermute(v, axes, pairs) for v in pair))  38.7 us
    all_gather x1, waiting for transfers between devices, gather_over_head(): value = lax.all_gather(value, 'hz', axis=0, tiled=True)  33.4 us
    ppermute x6, waiting for transfers between devices, ring_gather_x(): got.append(lax.ppermute(got[-1], 'hx', pairs))  28.2 us
    ppermute x12, starting transfers between devices, ring_sum_x(): got = lax.ppermute(acc.astype(jnp.bfloat16), 'hx', pairs)  22.3 us
    all_gather x1, waiting for transfers between devices, shards(): lax.all_gather(out_weight, SEQ, axis=1, tiled=True)  18.1 us
    ppermute x15, starting transfers between devices, send(): return tuple((lax.ppermute(v, axes, pairs) for v in pair))  12.6 us
  transfers between devices with their start and end apart: 36, of which 14 were waited for; matrix products, arithmetic and copies ran while one was open for 9% of the time, Pallas kernels for 0%

profile of v9, /device:TPU:8, one launch (start us, length us, event | category | flops | bytes accessed | tf_op | source)
XLA Modules:
  0.0 359.0 jit_solution(9432830692213116851)
XLA Ops:
  10.3 1.1 fusion.72
  13.2 1.8 collective-permute-start.6
  15.0 1.1 reduce-window.26
  16.6 1.3 collective-permute-start
  18.0 0.9 fusion.53
  20.0 1.2 fusion.5
  30.2 1.8 convolution_bitcast_fusion.3
  32.9 1.3 collective-permute-start.14
  34.9 38.6 %collective-permute-done.14 = f32[8,64,128]{2,1,0:T(8,128)S(1)} collective-permute-done((f32[8,64,128]{2,1,0:T(8,128)S(1)}, f32[8,64,128]{2,1,0:T(8,128)S(1)}, u32[]{:S(2)}, u32[]{:S(2)}) %collective-permute-start.14) | collective-permute-done | bytes 262176 | tf_op jit(solution)/shard_map/ppermute | solution.py:58
  75.9 1.3 fusion.40
  77.7 18.1 %all-gather.4.cloned.1.call-done = bf16[512,4096]{1,0:T(8,128)(2,1)} async-done(((bf16[512,256]{1,0:T(8,128)(2,1)}), bf16[512,4096]{1,0:T(8,128)(2,1)}) %all-gather.4.cloned.1.call-update) | async-done | bytes 4194320 | tf_op jit(solution)/shard_map/all_gather | solution.py:163
  95.8 4.6 %convolution_convert_fusion.1 = bf16[512,4096]{1,0:T(8,128)(2,1)S(1)} fusion(bf16[512,4096]{1,0:T(8,128)(2,1)} %all-gather.4.cloned.1.call-done, f32[512]{0:T(512)S(1)} %copy-done.16, f32[512,512]{1,0:T(8,128)S(1)} %copy.29, bf16[512,512]{1,0:T(8,128)(2,1)S(1)} %copy-done.5), kind=kOutput, calls=%fused_computation.3 | convolution fusion | flops 2151677952 | bytes 9963520 | tf_op jit(solution)/shard_map/dot_general | solution.py:197
  101.2 2.8 collective-permute-start.18
  104.3 11.6 %collective-permute-done.18 = bf16[4,16,4224]{2,1,0:T(8,128)(2,1)S(1)} collective-permute-done((bf16[4,16,4224]{2,1,0:T(8,128)(2,1)S(1)}, bf16[4,16,4224]{2,1,0:T(8,128)(2,1)S(1)}, u32[]{:S(2)}, u32[]{:S(2)}) %collective-permute-start.18) | collective-permute-done | bytes 540704 | tf_op jit(solution)/shard_map/ppermute | solution.py:105
  116.1 3.8 %collective-permute-start.19 = (bf16[4,16,4224]{2,1,0:T(8,128)(2,1)S(1)}, bf16[4,16,4224]{2,1,0:T(8,128)(2,1)S(1)}, u32[]{:S(2)}, u32[]{:S(2)}) collective-permute-start(bf16[4,16,4224]{2,1,0:T(8,128)(2,1)S(1)} %add_convert_fusion.2), channel_id=1, source_target_pairs={{0,12},{4,0},{8,4},{12,8},{1,13},{5,1},{9,5},{13,9},{2,14},{6,2},{... | collective-permute-start | bytes 1622024 | tf_op jit(solution)/shard_map/ppermute | solution.py:105
  120.1 10.8 %collective-permute-done.19 = bf16[4,16,4224]{2,1,0:T(8,128)(2,1)S(1)} collective-permute-done((bf16[4,16,4224]{2,1,0:T(8,128)(2,1)S(1)}, bf16[4,16,4224]{2,1,0:T(8,128)(2,1)S(1)}, u32[]{:S(2)}, u32[]{:S(2)}) %collective-permute-start.19) | collective-permute-done | bytes 540704 | tf_op jit(solution)/shard_map/ppermute | solution.py:105
  131.1 3.8 %collective-permute-start.20 = (bf16[4,16,4224]{2,1,0:T(8,128)(2,1)S(1)}, bf16[4,16,4224]{2,1,0:T(8,128)(2,1)S(1)}, u32[]{:S(2)}, u32[]{:S(2)}) collective-permute-start(bf16[4,16,4224]{2,1,0:T(8,128)(2,1)S(1)} %add_convert_fusion.1), channel_id=1, source_target_pairs={{0,12},{4,0},{8,4},{12,8},{1,13},{5,1},{9,5},{13,9},{2,14},{6,2},{... | collective-permute-start | bytes 1622024 | tf_op jit(solution)/shard_map/ppermute | solution.py:105
  135.1 10.0 %collective-permute-done.20 = bf16[4,16,4224]{2,1,0:T(8,128)(2,1)S(1)} collective-permute-done((bf16[4,16,4224]{2,1,0:T(8,128)(2,1)S(1)}, bf16[4,16,4224]{2,1,0:T(8,128)(2,1)S(1)}, u32[]{:S(2)}, u32[]{:S(2)}) %collective-permute-start.20) | collective-permute-done | bytes 540704 | tf_op jit(solution)/shard_map/ppermute | solution.py:105
  145.3 3.5 collective-permute-done.17
  149.1 34.4 %all_to_all.10 = bf16[4,32,4224]{2,1,0:T(8,128)(2,1)S(1)} all-to-all(bf16[4,32,4224]{2,1,0:T(8,128)(2,1)S(1)} %pad_maximum_fusion.4), channel_id=1, replica_groups=mesh['sy'=4,'sz'=2,'sc'=2,'hx'=4,'hz'=4] {'hz'}, dimensions={0} | all-to-all | bytes 2162688 | tf_op jit(solution)/shard_map/all_to_all | solution.py:116
  184.1 0.9 multiply_convert_fusion.10
  185.0 33.4 %all-gather.8.cloned.1.call-done = bf16[128,4096]{1,0:T(8,128)(2,1)} async-done(((bf16[32,4096]{1,0:T(8,128)(2,1)}), bf16[128,4096]{1,0:T(8,128)(2,1)}) %all-gather.8.cloned.1.call-update) | async-done | bytes 1048592 | tf_op jit(solution)/shard_map/all_gather | solution.py:137
  218.4 1.4 slice_bitcast_fusion.3
  219.8 2.8 collective-permute-start.24
  222.6 10.4 %collective-permute-done.24 = bf16[64,4096]{1,0:T(8,128)(2,1)S(1)} collective-permute-done((bf16[64,4096]{1,0:T(8,128)(2,1)S(1)}, bf16[64,4096]{1,0:T(8,128)(2,1)S(1)}, u32[]{:S(2)}, u32[]{:S(2)}) %collective-permute-start.24) | collective-permute-done | bytes 524320 | tf_op jit(solution)/shard_map/ppermute | solution.py:130
  233.0 3.7 %collective-permute-start.25 = (bf16[64,4096]{1,0:T(8,128)(2,1)S(1)}, bf16[64,4096]{1,0:T(8,128)(2,1)S(1)}, u32[]{:S(2)}, u32[]{:S(2)}) collective-permute-start(bf16[64,4096]{1,0:T(8,128)(2,1)S(1)} %collective-permute-done.24), channel_id=1, source_target_pairs={{0,12},{4,0},{8,4},{12,8},{1,13},{5,1},{9,5},{13,9},{2,14},{6,2},{... | collective-permute-start | bytes 1572872 | tf_op jit(solution)/shard_map/ppermute | solution.py:130
  236.7 9.5 %collective-permute-done.25 = bf16[64,4096]{1,0:T(8,128)(2,1)S(1)} collective-permute-done((bf16[64,4096]{1,0:T(8,128)(2,1)S(1)}, bf16[64,4096]{1,0:T(8,128)(2,1)S(1)}, u32[]{:S(2)}, u32[]{:S(2)}) %collective-permute-start.25) | collective-permute-done | bytes 524320 | tf_op jit(solution)/shard_map/ppermute | solution.py:130
  246.2 3.7 %collective-permute-start.26 = (bf16[64,4096]{1,0:T(8,128)(2,1)S(1)}, bf16[64,4096]{1,0:T(8,128)(2,1)S(1)}, u32[]{:S(2)}, u32[]{:S(2)}) collective-permute-start(bf16[64,4096]{1,0:T(8,128)(2,1)S(1)} %collective-permute-done.25), channel_id=1, source_target_pairs={{0,12},{4,0},{8,4},{12,8},{1,13},{5,1},{9,5},{13,9},{2,14},{6,2},{... | collective-permute-start | bytes 1572872 | tf_op jit(solution)/shard_map/ppermute | solution.py:130
  250.3 8.3 %collective-permute-done.26 = bf16[64,4096]{1,0:T(8,128)(2,1)S(1)} collective-permute-done((bf16[64,4096]{1,0:T(8,128)(2,1)S(1)}, bf16[64,4096]{1,0:T(8,128)(2,1)S(1)}, u32[]{:S(2)}, u32[]{:S(2)}) %collective-permute-start.26) | collective-permute-done | bytes 524320 | tf_op jit(solution)/shard_map/ppermute | solution.py:130
  258.9 2.0 gather_fusion.1
  260.9 3.2 broadcast_select_fusion
  264.1 1.5 pad_maximum_fusion.2
  265.6 2.0 gather_fusion
  267.6 2.0 broadcast_select_fusion.1
  270.3 2.1 copy-done.1
  272.5 1.1 copy-done.15
  273.5 2.3 fusion.73
  275.9 11.2 %convolution_convert_fusion = bf16[512,4096]{1,0:T(8,128)(2,1)} fusion(bf16[512,4096]{1,0:T(8,128)(2,1)} %all-gather.6.cloned.1.call-done, bf16[512,4096]{1,0:T(8,128)(2,1)} %bitcast.126, bf16[4096,512]{1,0:T(8,128)(2,1)} %param.36, f32[512,512]{1,0:T(8,128)S(1)} %fusion.73), kind=kOutput, calls=%fused_computation.2 | convolution fusion | flops 4298637312 | bytes 17825792 | tf_op jit(solution)/shard_map/dot_general | solution.py:218
  287.1 2.7 fusion.71
  289.9 3.8 %collective-permute-start.30 = (bf16[4,16,4096]{2,1,0:T(8,128)(2,1)S(1)}, bf16[4,16,4096]{2,1,0:T(8,128)(2,1)S(1)}, u32[]{:S(2)}, u32[]{:S(2)}) collective-permute-start(bf16[4,16,4096]{2,1,0:T(8,128)(2,1)S(1)} %select_bitcast_fusion.2), channel_id=1, source_target_pairs={{0,12},{4,0},{8,4},{12,8},{1,13},{5,1},{9,5},{13,9},{2,14},{6,2},{... | collective-permute-start | bytes 1572872 | tf_op jit(solution)/shard_map/ppermute | solution.py:105
  293.8 8.0 %collective-permute-done.30 = bf16[4,16,4096]{2,1,0:T(8,128)(2,1)S(1)} collective-permute-done((bf16[4,16,4096]{2,1,0:T(8,128)(2,1)S(1)}, bf16[4,16,4096]{2,1,0:T(8,128)(2,1)S(1)}, u32[]{:S(2)}, u32[]{:S(2)}) %collective-permute-start.30) | collective-permute-done | bytes 524320 | tf_op jit(solution)/shard_map/ppermute | solution.py:105
  302.0 3.8 %collective-permute-start.31 = (bf16[4,16,4096]{2,1,0:T(8,128)(2,1)S(1)}, bf16[4,16,4096]{2,1,0:T(8,128)(2,1)S(1)}, u32[]{:S(2)}, u32[]{:S(2)}) collective-permute-start(bf16[4,16,4096]{2,1,0:T(8,128)(2,1)S(1)} %add_convert_fusion.8), channel_id=1, source_target_pairs={{0,12},{4,0},{8,4},{12,8},{1,13},{5,1},{9,5},{13,9},{2,14},{6,2},{... | collective-permute-start | bytes 1572872 | tf_op jit(solution)/shard_map/ppermute | solution.py:105
  306.0 7.9 %collective-permute-done.31 = bf16[4,16,4096]{2,1,0:T(8,128)(2,1)S(1)} collective-permute-done((bf16[4,16,4096]{2,1,0:T(8,128)(2,1)S(1)}, bf16[4,16,4096]{2,1,0:T(8,128)(2,1)S(1)}, u32[]{:S(2)}, u32[]{:S(2)}) %collective-permute-start.31) | collective-permute-done | bytes 524320 | tf_op jit(solution)/shard_map/ppermute | solution.py:105
  314.1 3.8 %collective-permute-start.32 = (bf16[4,16,4096]{2,1,0:T(8,128)(2,1)S(1)}, bf16[4,16,4096]{2,1,0:T(8,128)(2,1)S(1)}, u32[]{:S(2)}, u32[]{:S(2)}) collective-permute-start(bf16[4,16,4096]{2,1,0:T(8,128)(2,1)S(1)} %add_convert_fusion.7), channel_id=1, source_target_pairs={{0,12},{4,0},{8,4},{12,8},{1,13},{5,1},{9,5},{13,9},{2,14},{6,2},{... | collective-permute-start | bytes 1572872 | tf_op jit(solution)/shard_map/ppermute | solution.py:105
  318.1 6.4 %collective-permute-done.32 = bf16[4,16,4096]{2,1,0:T(8,128)(2,1)S(1)} collective-permute-done((bf16[4,16,4096]{2,1,0:T(8,128)(2,1)S(1)}, bf16[4,16,4096]{2,1,0:T(8,128)(2,1)S(1)}, u32[]{:S(2)}, u32[]{:S(2)}) %collective-permute-start.32) | collective-permute-done | bytes 524320 | tf_op jit(solution)/shard_map/ppermute | solution.py:105
  324.7 3.8 %collective-permute-done.29 = bf16[4,16,4096]{2,1,0:T(8,128)(2,1)S(1)} collective-permute-done((bf16[4,16,4096]{2,1,0:T(8,128)(2,1)S(1)}, bf16[4,16,4096]{2,1,0:T(8,128)(2,1)S(1)}, u32[]{:S(2)}, u32[]{:S(2)}) %collective-permute-start.29) | collective-permute-done | bytes 524320 | tf_op jit(solution)/shard_map/ppermute | solution.py:105
  328.7 22.8 %all_to_all.11 = bf16[4,32,4096]{2,1,0:T(8,128)(2,1)S(1)} all-to-all(bf16[4,32,4096]{2,1,0:T(8,128)(2,1)S(1)} %pad_maximum_fusion.5), channel_id=1, replica_groups=mesh['sy'=4,'sz'=2,'sc'=2,'hx'=4,'hz'=4] {'hz'}, dimensions={0} | all-to-all | bytes 2097152 | tf_op jit(solution)/shard_map/all_to_all | solution.py:116
  351.7 0.8 add_convert_fusion.12
  (158 shorter events, 25.9 us)
Async XLA Ops:
  6.5 5.6 %copy-start.4 = (bf16[2,512,128]{2,1,0:T(8,128)(2,1)S(1)}, bf16[2,512,128]{2,1,0:T(8,128)(2,1)}, u32[]{:S(2)}) copy-start(bf16[2,512,128]{2,1,0:T(8,128)(2,1)} %param.26) | copy-start | bytes 786436
  6.5 89.2 %all-gather.4.cloned.1.call-start = ((), (), s32[]{:S(2)}) async-start(), calls=%async_computation.2 | async-start | bytes 4456448 | tf_op jit(solution)/shard_map/all_gather | solution.py:163
  7.3 176.4 %all-gather.6.cloned.1.call-start = ((), (), s32[]{:S(2)}) async-start(), calls=%async_computation.3 | async-start | bytes 4456448 | tf_op jit(solution)/shard_map/all_gather | solution.py:164
  13.2 5.7 %collective-permute-start.6 = (f32[8,64,128]{2,1,0:T(8,128)S(1)}, f32[8,64,128]{2,1,0:T(8,128)S(1)}, u32[]{:S(2)}, u32[]{:S(2)}) collective-permute-start(f32[8,64,128]{2,1,0:T(8,128)S(1)} %fusion.6), channel_id=1, source_target_pairs={{0,16},{32,48},{1,17},{33,49},{2,18},{34,50},{3,19},{35,51},{4,20}... | collective-permute-start | bytes 786440 | tf_op jit(solution)/shard_map/ppermute | solution.py:58
  16.6 4.6 %collective-permute-start = (f32[8]{0:T(128)S(1)}, f32[8]{0:T(128)S(1)}, u32[]{:S(2)}, u32[]{:S(2)}) collective-permute-start(f32[8]{0:T(128)S(1)} %fusion.61), channel_id=1, source_target_pairs={{0,16},{32,48},{1,17},{33,49},{2,18},{34,50},{3,19},{35,51},{4,20}... | collective-permute-start | bytes 104 | tf_op jit(solution)/shard_map/ppermute | solution.py:58
  17.9 200.5 %all-gather.8.cloned.1.call-start = ((), (), s32[]{:S(2)}) async-start(), calls=%async_computation.4 | async-start | bytes 1310720 | tf_op jit(solution)/shard_map/all_gather | solution.py:137
  18.9 9.7 %copy-start.3 = (bf16[512,512]{1,0:T(8,128)(2,1)S(1)}, bf16[512,512]{1,0:T(8,128)(2,1)}, u32[]{:S(2)}) copy-start(bf16[512,512]{1,0:T(8,128)(2,1)} %param.24) | copy-start | bytes 1572868
  19.0 3.6 %collective-permute-start.7 = (f32[8,64,128]{2,1,0:T(8,128)S(1)}, f32[8,64,128]{2,1,0:T(8,128)S(1)}, u32[]{:S(2)}, u32[]{:S(2)}) collective-permute-start(f32[8,64,128]{2,1,0:T(8,128)S(1)} %multiply_add_fusion.2), channel_id=1, source_target_pairs={{16,32},{17,33},{18,34},{19,35},{20,36},{21,37},{22,38},{23,39},{2... | collective-permute-start | bytes 786440 | tf_op jit(solution)/shard_map/ppermute | solution.py:58
  21.2 0.7 collective-permute-start.1
  21.9 1.4 collective-permute-start.2
  22.6 6.0 %copy-start.10 = (f32[8,64,128]{2,1,0:T(8,128)}, f32[8,64,128]{2,1,0:T(8,128)S(1)}, u32[]{:S(2)}) copy-start(f32[8,64,128]{2,1,0:T(8,128)S(1)} %collective-permute-done.7) | copy-start | bytes 786436
  22.6 2.7 collective-permute-start.8
  23.3 2.0 collective-permute-start.5
  24.0 3.5 collective-permute-start.4
  24.7 2.9 collective-permute-start.3
  25.5 2.1 collective-permute-start.11
  26.1 1.4 collective-permute-start.10
  26.8 0.8 collective-permute-start.9
  27.7 5.1 %collective-permute-start.12 = (f32[8,64,128]{2,1,0:T(8,128)S(1)}, f32[8,64,128]{2,1,0:T(8,128)S(1)}, u32[]{:S(2)}, u32[]{:S(2)}) collective-permute-start(f32[8,64,128]{2,1,0:T(8,128)S(1)} %select_add_fusion), channel_id=1, source_target_pairs={{48,16},{49,17},{50,18},{51,19},{52,20},{53,21},{54,22},{55,23},{5... | collective-permute-start | bytes 786440 | tf_op jit(solution)/shard_map/ppermute | solution.py:58
  28.9 5.3 %copy-start.6 = (f32[256,8,64]{0,2,1:T(8,128)S(1)}, f32[256,8,64]{0,2,1:T(8,128)}, u32[]{:S(2)}) copy-start(f32[256,8,64]{0,2,1:T(8,128)} %fusion.5) | copy-start | bytes 1572868
  32.0 41.5 %copy-start.11 = (f32[8,64,128]{2,1,0:T(8,128)S(1)}, f32[8,64,128]{2,1,0:T(8,128)}, u32[]{:S(2)}) copy-start(f32[8,64,128]{2,1,0:T(8,128)} %copy-done.10) | copy-start | bytes 786436
  32.0 41.5 %copy-start.14 = (f32[8]{0:T(128)S(1)}, f32[8]{0:T(128)}, u32[]{:S(2)}) copy-start(f32[8]{0:T(128)} %param.30) | copy-start | bytes 100
  32.0 2.9 collective-permute-start.13
  32.8 40.7 %copy-start.12 = (f32[8,64,128]{2,1,0:T(8,128)}, f32[8,64,128]{2,1,0:T(8,128)S(1)}, u32[]{:S(2)}) copy-start(f32[8,64,128]{2,1,0:T(8,128)S(1)} %collective-permute-done.12) | copy-start | bytes 786436
  32.9 40.7 %collective-permute-start.14 = (f32[8,64,128]{2,1,0:T(8,128)S(1)}, f32[8,64,128]{2,1,0:T(8,128)S(1)}, u32[]{:S(2)}, u32[]{:S(2)}) collective-permute-start(f32[8,64,128]{2,1,0:T(8,128)S(1)} %collective-permute-done.12), channel_id=1, source_target_pairs={{16,0},{17,1},{18,2},{19,3},{20,4},{21,5},{22,6},{23,7},{24,8},{25... | collective-permute-start | bytes 786440 | tf_op jit(solution)/shard_map/ppermute | solution.py:58
  74.3 21.4 %copy-start.16 = (f32[512]{0:T(512)S(1)}, f32[512]{0:T(512)}, u32[]{:S(2)}) copy-start(f32[512]{0:T(512)} %param.31) | copy-start | bytes 6148
  101.2 14.7 %collective-permute-start.18 = (bf16[4,16,4224]{2,1,0:T(8,128)(2,1)S(1)}, bf16[4,16,4224]{2,1,0:T(8,128)(2,1)S(1)}, u32[]{:S(2)}, u32[]{:S(2)}) collective-permute-start(bf16[4,16,4224]{2,1,0:T(8,128)(2,1)S(1)} %select_bitcast_fusion), channel_id=1, source_target_pairs={{0,12},{4,0},{8,4},{12,8},{1,13},{5,1},{9,5},{13,9},{2,14},{6,2},{... | collective-permute-start | bytes 1622024 | tf_op jit(solution)/shard_map/ppermute | solution.py:105
  104.0 15.8 %collective-permute-start.15 = (bf16[4,16,4224]{2,1,0:T(8,128)(2,1)S(1)}, bf16[4,16,4224]{2,1,0:T(8,128)(2,1)S(1)}, u32[]{:S(2)}, u32[]{:S(2)}) collective-permute-start(bf16[4,16,4224]{2,1,0:T(8,128)(2,1)S(1)} %select_bitcast_fusion.1), channel_id=1, source_target_pairs={{0,4},{4,8},{8,12},{12,0},{1,5},{5,9},{9,13},{13,1},{2,6},{6,10},{... | collective-permute-start | bytes 1622024 | tf_op jit(solution)/shard_map/ppermute | solution.py:105
  116.1 14.9 %collective-permute-start.19 = (bf16[4,16,4224]{2,1,0:T(8,128)(2,1)S(1)}, bf16[4,16,4224]{2,1,0:T(8,128)(2,1)S(1)}, u32[]{:S(2)}, u32[]{:S(2)}) collective-permute-start(bf16[4,16,4224]{2,1,0:T(8,128)(2,1)S(1)} %add_convert_fusion.2), channel_id=1, source_target_pairs={{0,12},{4,0},{8,4},{12,8},{1,13},{5,1},{9,5},{13,9},{2,14},{6,2},{... | collective-permute-start | bytes 1622024 | tf_op jit(solution)/shard_map/ppermute | solution.py:105
  120.0 14.9 %collective-permute-start.16 = (bf16[4,16,4224]{2,1,0:T(8,128)(2,1)S(1)}, bf16[4,16,4224]{2,1,0:T(8,128)(2,1)S(1)}, u32[]{:S(2)}, u32[]{:S(2)}) collective-permute-start(bf16[4,16,4224]{2,1,0:T(8,128)(2,1)S(1)} %add_convert_fusion.5), channel_id=1, source_target_pairs={{0,4},{4,8},{8,12},{12,0},{1,5},{5,9},{9,13},{13,1},{2,6},{6,10},{... | collective-permute-start | bytes 1622024 | tf_op jit(solution)/shard_map/ppermute | solution.py:105
  131.1 14.0 %collective-permute-start.20 = (bf16[4,16,4224]{2,1,0:T(8,128)(2,1)S(1)}, bf16[4,16,4224]{2,1,0:T(8,128)(2,1)S(1)}, u32[]{:S(2)}, u32[]{:S(2)}) collective-permute-start(bf16[4,16,4224]{2,1,0:T(8,128)(2,1)S(1)} %add_convert_fusion.1), channel_id=1, source_target_pairs={{0,12},{4,0},{8,4},{12,8},{1,13},{5,1},{9,5},{13,9},{2,14},{6,2},{... | collective-permute-start | bytes 1622024 | tf_op jit(solution)/shard_map/ppermute | solution.py:105
  135.1 13.7 %collective-permute-start.17 = (bf16[4,16,4224]{2,1,0:T(8,128)(2,1)S(1)}, bf16[4,16,4224]{2,1,0:T(8,128)(2,1)S(1)}, u32[]{:S(2)}, u32[]{:S(2)}) collective-permute-start(bf16[4,16,4224]{2,1,0:T(8,128)(2,1)S(1)} %add_convert_fusion.4), channel_id=1, source_target_pairs={{0,4},{4,8},{8,12},{12,0},{1,5},{5,9},{9,13},{13,1},{2,6},{6,10},{... | collective-permute-start | bytes 1622024 | tf_op jit(solution)/shard_map/ppermute | solution.py:105
  149.0 34.8 %copy-start.2 = (bf16[32,4096]{1,0:T(8,128)(2,1)S(1)}, bf16[32,4096]{1,0:T(8,128)(2,1)}, u32[]{:S(2)}) copy-start(bf16[32,4096]{1,0:T(8,128)(2,1)} %param.33) | copy-start | bytes 786436
  149.0 35.1 %copy-start.13 = (f32[4096]{0:T(1024)S(1)}, f32[4096]{0:T(1024)}, u32[]{:S(2)}) copy-start(f32[4096]{0:T(1024)} %param.34) | copy-start | bytes 49156
  219.8 13.2 %collective-permute-start.24 = (bf16[64,4096]{1,0:T(8,128)(2,1)S(1)}, bf16[64,4096]{1,0:T(8,128)(2,1)S(1)}, u32[]{:S(2)}, u32[]{:S(2)}) collective-permute-start(bf16[64,4096]{1,0:T(8,128)(2,1)S(1)} %get-tuple-element.74), channel_id=1, source_target_pairs={{0,12},{4,0},{8,4},{12,8},{1,13},{5,1},{9,5},{13,9},{2,14},{6,2},{... | collective-permute-start | bytes 1572872 | tf_op jit(solution)/shard_map/ppermute | solution.py:130
  222.6 14.1 %collective-permute-start.21 = (bf16[64,4096]{1,0:T(8,128)(2,1)S(1)}, bf16[64,4096]{1,0:T(8,128)(2,1)S(1)}, u32[]{:S(2)}, u32[]{:S(2)}) collective-permute-start(bf16[64,4096]{1,0:T(8,128)(2,1)S(1)} %get-tuple-element.75), channel_id=1, source_target_pairs={{0,4},{4,8},{8,12},{12,0},{1,5},{5,9},{9,13},{13,1},{2,6},{6,10},{... | collective-permute-start | bytes 1572872 | tf_op jit(solution)/shard_map/ppermute | solution.py:130
  233.0 13.2 %collective-permute-start.25 = (bf16[64,4096]{1,0:T(8,128)(2,1)S(1)}, bf16[64,4096]{1,0:T(8,128)(2,1)S(1)}, u32[]{:S(2)}, u32[]{:S(2)}) collective-permute-start(bf16[64,4096]{1,0:T(8,128)(2,1)S(1)} %collective-permute-done.24), channel_id=1, source_target_pairs={{0,12},{4,0},{8,4},{12,8},{1,13},{5,1},{9,5},{13,9},{2,14},{6,2},{... | collective-permute-start | bytes 1572872 | tf_op jit(solution)/shard_map/ppermute | solution.py:130
  236.7 21.9 %copy-start.7 = (bf16[64,4096]{1,0:T(8,128)(2,1)}, bf16[64,4096]{1,0:T(8,128)(2,1)S(1)}, u32[]{:S(2)}) copy-start(bf16[64,4096]{1,0:T(8,128)(2,1)S(1)} %collective-permute-done.21) | copy-start | bytes 1572868
  236.7 13.3 %collective-permute-start.22 = (bf16[64,4096]{1,0:T(8,128)(2,1)S(1)}, bf16[64,4096]{1,0:T(8,128)(2,1)}, u32[]{:S(2)}, u32[]{:S(2)}) collective-permute-start(bf16[64,4096]{1,0:T(8,128)(2,1)S(1)} %collective-permute-done.21), channel_id=1, source_target_pairs={{0,4},{4,8},{8,12},{12,0},{1,5},{5,9},{9,13},{13,1},{2,6},{6,10},{... | collective-permute-start | bytes 1572872 | tf_op jit(solution)/shard_map/ppermute | solution.py:130
  246.2 12.4 %collective-permute-start.26 = (bf16[64,4096]{1,0:T(8,128)(2,1)S(1)}, bf16[64,4096]{1,0:T(8,128)(2,1)S(1)}, u32[]{:S(2)}, u32[]{:S(2)}) collective-permute-start(bf16[64,4096]{1,0:T(8,128)(2,1)S(1)} %collective-permute-done.25), channel_id=1, source_target_pairs={{0,12},{4,0},{8,4},{12,8},{1,13},{5,1},{9,5},{13,9},{2,14},{6,2},{... | collective-permute-start | bytes 1572872 | tf_op jit(solution)/shard_map/ppermute | solution.py:130
  250.0 14.1 %collective-permute-start.23 = (bf16[64,4096]{1,0:T(8,128)(2,1)}, bf16[64,4096]{1,0:T(8,128)(2,1)}, u32[]{:S(2)}, u32[]{:S(2)}) collective-permute-start(bf16[64,4096]{1,0:T(8,128)(2,1)} %collective-permute-done.22), channel_id=1, source_target_pairs={{0,4},{4,8},{8,12},{12,0},{1,5},{5,9},{9,13},{13,1},{2,6},{6,10},{... | collective-permute-start | bytes 1572872 | tf_op jit(solution)/shard_map/ppermute | solution.py:130
  269.8 3.7 %copy-start.15 = (bf16[4096,512]{1,0:T(8,128)(2,1)S(1)}, bf16[4096,512]{1,0:T(8,128)(2,1)}, u32[]{:S(2)}) copy-start(bf16[4096,512]{1,0:T(8,128)(2,1)} %param.35) | copy-start | bytes 12582916
  289.9 11.9 %collective-permute-start.30 = (bf16[4,16,4096]{2,1,0:T(8,128)(2,1)S(1)}, bf16[4,16,4096]{2,1,0:T(8,128)(2,1)S(1)}, u32[]{:S(2)}, u32[]{:S(2)}) collective-permute-start(bf16[4,16,4096]{2,1,0:T(8,128)(2,1)S(1)} %select_bitcast_fusion.2), channel_id=1, source_target_pairs={{0,12},{4,0},{8,4},{12,8},{1,13},{5,1},{9,5},{13,9},{2,14},{6,2},{... | collective-permute-start | bytes 1572872 | tf_op jit(solution)/shard_map/ppermute | solution.py:105
  293.7 12.0 %collective-permute-start.27 = (bf16[4,16,4096]{2,1,0:T(8,128)(2,1)S(1)}, bf16[4,16,4096]{2,1,0:T(8,128)(2,1)S(1)}, u32[]{:S(2)}, u32[]{:S(2)}) collective-permute-start(bf16[4,16,4096]{2,1,0:T(8,128)(2,1)S(1)} %select_bitcast_fusion.3), channel_id=1, source_target_pairs={{0,4},{4,8},{8,12},{12,0},{1,5},{5,9},{9,13},{13,1},{2,6},{6,10},{... | collective-permute-start | bytes 1572872 | tf_op jit(solution)/shard_map/ppermute | solution.py:105
  302.0 11.9 %collective-permute-start.31 = (bf16[4,16,4096]{2,1,0:T(8,128)(2,1)S(1)}, bf16[4,16,4096]{2,1,0:T(8,128)(2,1)S(1)}, u32[]{:S(2)}, u32[]{:S(2)}) collective-permute-start(bf16[4,16,4096]{2,1,0:T(8,128)(2,1)S(1)} %add_convert_fusion.8), channel_id=1, source_target_pairs={{0,12},{4,0},{8,4},{12,8},{1,13},{5,1},{9,5},{13,9},{2,14},{6,2},{... | collective-permute-start | bytes 1572872 | tf_op jit(solution)/shard_map/ppermute | solution.py:105
  305.9 11.9 %collective-permute-start.28 = (bf16[4,16,4096]{2,1,0:T(8,128)(2,1)S(1)}, bf16[4,16,4096]{2,1,0:T(8,128)(2,1)S(1)}, u32[]{:S(2)}, u32[]{:S(2)}) collective-permute-start(bf16[4,16,4096]{2,1,0:T(8,128)(2,1)S(1)} %add_convert_fusion.11), channel_id=1, source_target_pairs={{0,4},{4,8},{8,12},{12,0},{1,5},{5,9},{9,13},{13,1},{2,6},{6,10},{... | collective-permute-start | bytes 1572872 | tf_op jit(solution)/shard_map/ppermute | solution.py:105
  314.1 10.5 %collective-permute-start.32 = (bf16[4,16,4096]{2,1,0:T(8,128)(2,1)S(1)}, bf16[4,16,4096]{2,1,0:T(8,128)(2,1)S(1)}, u32[]{:S(2)}, u32[]{:S(2)}) collective-permute-start(bf16[4,16,4096]{2,1,0:T(8,128)(2,1)S(1)} %add_convert_fusion.7), channel_id=1, source_target_pairs={{0,12},{4,0},{8,4},{12,8},{1,13},{5,1},{9,5},{13,9},{2,14},{6,2},{... | collective-permute-start | bytes 1572872 | tf_op jit(solution)/shard_map/ppermute | solution.py:105
  318.0 10.5 %collective-permute-start.29 = (bf16[4,16,4096]{2,1,0:T(8,128)(2,1)S(1)}, bf16[4,16,4096]{2,1,0:T(8,128)(2,1)S(1)}, u32[]{:S(2)}, u32[]{:S(2)}) collective-permute-start(bf16[4,16,4096]{2,1,0:T(8,128)(2,1)S(1)} %add_convert_fusion.10), channel_id=1, source_target_pairs={{0,4},{4,8},{8,12},{12,0},{1,5},{5,9},{9,13},{13,1},{2,6},{6,10},{... | collective-permute-start | bytes 1572872 | tf_op jit(solution)/shard_map/ppermute | solution.py:105
  (5 other events, 9.7 us)
Sparse Core Ops, SparseCore 0:
  9.9 85.8 all-gather.3
  98.3 78.6 all-gather.5
  185.1 33.2 all-gather.7

commit v10 on v9

--- a/solution.py
+++ b/solution.py
@@ -133,9 +133,15 @@
     return jnp.concatenate(outs, axis=1).reshape(nx * value.shape[0], value.shape[1])
 
 
+def gather_z(value):
+    nz = lax.axis_size("hz")
+    copies = jnp.broadcast_to(value[None], (nz,) + value.shape)
+    got = lax.all_to_all(copies, "hz", 0, 0, tiled=False)
+    return got.reshape(nz * value.shape[0], value.shape[1])
+
+
 def gather_over_head(value):
-    value = lax.all_gather(value, "hz", axis=0, tiled=True)
-    return ring_gather_x(value)
+    return ring_gather_x(gather_z(value))
 
 
 def normalize_rows(layer_sum, mlp_gain):

time: 360 us -> 355 us (0.986)
  waiting for transfers between devices: 181 us -> 148 us
  blocking collectives: 57.2 us -> 86.8 us
    all_gather x1 -> x0, waiting for transfers between devices: 33.4 us -> none  [gather_over_head(): value = lax.all_gather(value, 'hz', axis=0, tiled=True)]
    all_to_all x0 -> x1, blocking collectives: none -> 29.2 us  [gather_z(): got = lax.all_to_all(copies, 'hz', 0, 0, tiled=False)]
  transfers between devices with their start and end apart: 36 -> 35, of which waited for: 14 -> 13; matrix products, arithmetic and copies ran while one was open for 9% -> 9% of each run, Pallas kernels for 0% -> 0%
where the time goes in v10:
time: 355 us; the launch traced here: 354 us
  waiting for transfers between devices  148 us (42%)
  blocking collectives  86.8 us (24%)
  starting transfers between devices  46 us (13%)
  matrix products  24.8 us (7%)
  other arithmetic  20 us (6%)
  local copies, waits for them, and re-layouts  14.6 us (4%)
  between operations  14.5 us (4%)
    ppermute x12, waiting for transfers between devices, ring_sum_x(): got = lax.ppermute(acc.astype(jnp.bfloat16), 'hx', pairs)  62.1 us
    all_to_all x2, blocking collectives, sum_over_head(): pieces = lax.all_to_all(pieces, 'hz', 0, 0, tiled=False)  57.6 us
    ppermute x15, waiting for transfers between devices, send(): return tuple((lax.ppermute(v, axes, pairs) for v in pair))  38.6 us
    all_to_all x1, blocking collectives, gather_z(): got = lax.all_to_all(copies, 'hz', 0, 0, tiled=False)  29.2 us
    ppermute x6, waiting for transfers between devices, ring_gather_x(): got.append(lax.ppermute(got[-1], 'hx', pairs))  28.5 us
    ppermute x12, starting transfers between devices, ring_sum_x(): got = lax.ppermute(acc.astype(jnp.bfloat16), 'hx', pairs)  22.3 us
    all_gather x1, waiting for transfers between devices, shards(): lax.all_gather(out_weight, SEQ, axis=1, tiled=True)  18 us
    ppermute x15, starting transfers between devices, send(): return tuple((lax.ppermute(v, axes, pairs) for v in pair))  12.6 us
  transfers between devices with their start and end apart: 35, of which 13 were waited for; matrix products, arithmetic and copies ran while one was open for 9% of the time, Pallas kernels for 0%

profile of v10, /device:TPU:8, one launch (start us, length us, event | category | flops | bytes accessed | tf_op | source)
XLA Modules:
  0.0 354.5 jit_solution(17849686165738651231)
XLA Ops:
  10.3 1.1 fusion.73
  13.2 1.8 collective-permute-start.6
  15.0 1.1 reduce-window.26
  16.6 1.3 collective-permute-start
  17.9 0.9 fusion.53
  18.9 0.8 collective-permute-start.7
  20.0 1.2 fusion.5
  30.3 1.8 convolution_bitcast_fusion.3
  32.0 0.8 collective-permute-start.13
  32.9 1.3 collective-permute-start.14
  34.9 38.6 %collective-permute-done.14 = f32[8,64,128]{2,1,0:T(8,128)S(1)} collective-permute-done((f32[8,64,128]{2,1,0:T(8,128)S(1)}, f32[8,64,128]{2,1,0:T(8,128)S(1)}, u32[]{:S(2)}, u32[]{:S(2)}) %collective-permute-start.14) | collective-permute-done | bytes 262176 | tf_op jit(solution)/shard_map/ppermute | solution.py:58
  76.0 1.4 fusion.40
  77.8 18.0 %all-gather.3.cloned.1.call-done = bf16[512,4096]{1,0:T(8,128)(2,1)} async-done(((bf16[512,256]{1,0:T(8,128)(2,1)}), bf16[512,4096]{1,0:T(8,128)(2,1)}) %all-gather.3.cloned.1.call-update) | async-done | bytes 4194320 | tf_op jit(solution)/shard_map/all_gather | solution.py:169
  95.8 4.6 %convolution_convert_fusion.1 = bf16[512,4096]{1,0:T(8,128)(2,1)S(1)} fusion(bf16[512,4096]{1,0:T(8,128)(2,1)} %all-gather.3.cloned.1.call-done, f32[512]{0:T(512)S(1)} %copy-done.16, f32[512,512]{1,0:T(8,128)S(1)} %copy.29, bf16[512,512]{1,0:T(8,128)(2,1)S(1)} %copy-done.5), kind=kOutput, calls=%fused_computation.3 | convolution fusion | flops 2151677952 | bytes 9963520 | tf_op jit(solution)/shard_map/dot_general | solution.py:203
  101.2 2.8 collective-permute-start.18
  104.3 11.6 %collective-permute-done.18 = bf16[4,16,4224]{2,1,0:T(8,128)(2,1)S(1)} collective-permute-done((bf16[4,16,4224]{2,1,0:T(8,128)(2,1)S(1)}, bf16[4,16,4224]{2,1,0:T(8,128)(2,1)S(1)}, u32[]{:S(2)}, u32[]{:S(2)}) %collective-permute-start.18) | collective-permute-done | bytes 540704 | tf_op jit(solution)/shard_map/ppermute | solution.py:105
  116.1 3.8 %collective-permute-start.19 = (bf16[4,16,4224]{2,1,0:T(8,128)(2,1)S(1)}, bf16[4,16,4224]{2,1,0:T(8,128)(2,1)S(1)}, u32[]{:S(2)}, u32[]{:S(2)}) collective-permute-start(bf16[4,16,4224]{2,1,0:T(8,128)(2,1)S(1)} %add_convert_fusion.2), channel_id=1, source_target_pairs={{0,12},{4,0},{8,4},{12,8},{1,13},{5,1},{9,5},{13,9},{2,14},{6,2},{... | collective-permute-start | bytes 1622024 | tf_op jit(solution)/shard_map/ppermute | solution.py:105
  120.1 10.8 %collective-permute-done.19 = bf16[4,16,4224]{2,1,0:T(8,128)(2,1)S(1)} collective-permute-done((bf16[4,16,4224]{2,1,0:T(8,128)(2,1)S(1)}, bf16[4,16,4224]{2,1,0:T(8,128)(2,1)S(1)}, u32[]{:S(2)}, u32[]{:S(2)}) %collective-permute-start.19) | collective-permute-done | bytes 540704 | tf_op jit(solution)/shard_map/ppermute | solution.py:105
  131.1 3.8 %collective-permute-start.20 = (bf16[4,16,4224]{2,1,0:T(8,128)(2,1)S(1)}, bf16[4,16,4224]{2,1,0:T(8,128)(2,1)S(1)}, u32[]{:S(2)}, u32[]{:S(2)}) collective-permute-start(bf16[4,16,4224]{2,1,0:T(8,128)(2,1)S(1)} %add_convert_fusion.1), channel_id=1, source_target_pairs={{0,12},{4,0},{8,4},{12,8},{1,13},{5,1},{9,5},{13,9},{2,14},{6,2},{... | collective-permute-start | bytes 1622024 | tf_op jit(solution)/shard_map/ppermute | solution.py:105
  135.2 10.0 %collective-permute-done.20 = bf16[4,16,4224]{2,1,0:T(8,128)(2,1)S(1)} collective-permute-done((bf16[4,16,4224]{2,1,0:T(8,128)(2,1)S(1)}, bf16[4,16,4224]{2,1,0:T(8,128)(2,1)S(1)}, u32[]{:S(2)}, u32[]{:S(2)}) %collective-permute-start.20) | collective-permute-done | bytes 540704 | tf_op jit(solution)/shard_map/ppermute | solution.py:105
  145.3 3.5 collective-permute-done.17
  149.1 34.4 %all_to_all.15 = bf16[4,32,4224]{2,1,0:T(8,128)(2,1)S(1)} all-to-all(bf16[4,32,4224]{2,1,0:T(8,128)(2,1)S(1)} %pad_maximum_fusion.4), channel_id=1, replica_groups=mesh['sy'=4,'sz'=2,'sc'=2,'hx'=4,'hz'=4] {'hz'}, dimensions={0} | all-to-all | bytes 2162688 | tf_op jit(solution)/shard_map/all_to_all | solution.py:116
  184.4 29.2 %all_to_all.16 = bf16[4,32,4096]{2,1,0:T(8,128)(2,1)S(1)} all-to-all(bf16[4,32,4096]{2,1,0:T(8,128)(2,1)S(1)} %broadcast_in_dim.42), channel_id=1, replica_groups=mesh['sy'=4,'sz'=2,'sc'=2,'hx'=4,'hz'=4] {'hz'}, dimensions={0} | all-to-all | bytes 2097152 | tf_op jit(solution)/shard_map/all_to_all | solution.py:139
  213.7 3.3 collective-permute-start.24
  217.0 10.5 %collective-permute-done.24 = bf16[64,4096]{1,0:T(8,128)(2,1)S(1)} collective-permute-done((bf16[64,4096]{1,0:T(8,128)(2,1)S(1)}, bf16[64,4096]{1,0:T(8,128)(2,1)S(1)}, u32[]{:S(2)}, u32[]{:S(2)}) %collective-permute-start.24) | collective-permute-done | bytes 524320 | tf_op jit(solution)/shard_map/ppermute | solution.py:130
  227.5 3.7 %collective-permute-start.25 = (bf16[64,4096]{1,0:T(8,128)(2,1)S(1)}, bf16[64,4096]{1,0:T(8,128)(2,1)S(1)}, u32[]{:S(2)}, u32[]{:S(2)}) collective-permute-start(bf16[64,4096]{1,0:T(8,128)(2,1)S(1)} %collective-permute-done.24), channel_id=1, source_target_pairs={{0,12},{4,0},{8,4},{12,8},{1,13},{5,1},{9,5},{13,9},{2,14},{6,2},{... | collective-permute-start | bytes 1572872 | tf_op jit(solution)/shard_map/ppermute | solution.py:130
  231.2 9.6 %collective-permute-done.25 = bf16[64,4096]{1,0:T(8,128)(2,1)S(1)} collective-permute-done((bf16[64,4096]{1,0:T(8,128)(2,1)S(1)}, bf16[64,4096]{1,0:T(8,128)(2,1)S(1)}, u32[]{:S(2)}, u32[]{:S(2)}) %collective-permute-start.25) | collective-permute-done | bytes 524320 | tf_op jit(solution)/shard_map/ppermute | solution.py:130
  240.8 3.7 %collective-permute-start.26 = (bf16[64,4096]{1,0:T(8,128)(2,1)S(1)}, bf16[64,4096]{1,0:T(8,128)(2,1)S(1)}, u32[]{:S(2)}, u32[]{:S(2)}) collective-permute-start(bf16[64,4096]{1,0:T(8,128)(2,1)S(1)} %collective-permute-done.25), channel_id=1, source_target_pairs={{0,12},{4,0},{8,4},{12,8},{1,13},{5,1},{9,5},{13,9},{2,14},{6,2},{... | collective-permute-start | bytes 1572872 | tf_op jit(solution)/shard_map/ppermute | solution.py:130
  244.9 8.4 %collective-permute-done.26 = bf16[64,4096]{1,0:T(8,128)(2,1)S(1)} collective-permute-done((bf16[64,4096]{1,0:T(8,128)(2,1)S(1)}, bf16[64,4096]{1,0:T(8,128)(2,1)S(1)}, u32[]{:S(2)}, u32[]{:S(2)}) %collective-permute-start.26) | collective-permute-done | bytes 524320 | tf_op jit(solution)/shard_map/ppermute | solution.py:130
  253.5 2.0 gather_fusion.1
  255.5 3.2 broadcast_select_fusion
  258.8 1.5 pad_maximum_fusion.2
  260.2 2.0 gather_fusion
  262.3 2.0 broadcast_select_fusion.1
  265.0 2.1 copy-done.1
  267.1 1.1 copy-done.15
  268.2 2.3 fusion.74
  270.5 11.2 %convolution_convert_fusion = bf16[512,4096]{1,0:T(8,128)(2,1)} fusion(bf16[512,4096]{1,0:T(8,128)(2,1)} %all-gather.5.cloned.1.call-done, bf16[512,4096]{1,0:T(8,128)(2,1)} %bitcast.126, bf16[4096,512]{1,0:T(8,128)(2,1)} %param.36, f32[512,512]{1,0:T(8,128)S(1)} %fusion.74), kind=kOutput, calls=%fused_computation.2 | convolution fusion | flops 4298637312 | bytes 17825792 | tf_op jit(solution)/shard_map/dot_general | solution.py:224
  281.7 2.7 fusion.71
  284.5 3.8 %collective-permute-start.30 = (bf16[4,16,4096]{2,1,0:T(8,128)(2,1)S(1)}, bf16[4,16,4096]{2,1,0:T(8,128)(2,1)S(1)}, u32[]{:S(2)}, u32[]{:S(2)}) collective-permute-start(bf16[4,16,4096]{2,1,0:T(8,128)(2,1)S(1)} %select_bitcast_fusion.2), channel_id=1, source_target_pairs={{0,12},{4,0},{8,4},{12,8},{1,13},{5,1},{9,5},{13,9},{2,14},{6,2},{... | collective-permute-start | bytes 1572872 | tf_op jit(solution)/shard_map/ppermute | solution.py:105
  288.5 8.0 %collective-permute-done.30 = bf16[4,16,4096]{2,1,0:T(8,128)(2,1)S(1)} collective-permute-done((bf16[4,16,4096]{2,1,0:T(8,128)(2,1)S(1)}, bf16[4,16,4096]{2,1,0:T(8,128)(2,1)S(1)}, u32[]{:S(2)}, u32[]{:S(2)}) %collective-permute-start.30) | collective-permute-done | bytes 524320 | tf_op jit(solution)/shard_map/ppermute | solution.py:105
  296.6 3.8 %collective-permute-start.31 = (bf16[4,16,4096]{2,1,0:T(8,128)(2,1)S(1)}, bf16[4,16,4096]{2,1,0:T(8,128)(2,1)S(1)}, u32[]{:S(2)}, u32[]{:S(2)}) collective-permute-start(bf16[4,16,4096]{2,1,0:T(8,128)(2,1)S(1)} %add_convert_fusion.8), channel_id=1, source_target_pairs={{0,12},{4,0},{8,4},{12,8},{1,13},{5,1},{9,5},{13,9},{2,14},{6,2},{... | collective-permute-start | bytes 1572872 | tf_op jit(solution)/shard_map/ppermute | solution.py:105
  300.6 7.9 %collective-permute-done.31 = bf16[4,16,4096]{2,1,0:T(8,128)(2,1)S(1)} collective-permute-done((bf16[4,16,4096]{2,1,0:T(8,128)(2,1)S(1)}, bf16[4,16,4096]{2,1,0:T(8,128)(2,1)S(1)}, u32[]{:S(2)}, u32[]{:S(2)}) %collective-permute-start.31) | collective-permute-done | bytes 524320 | tf_op jit(solution)/shard_map/ppermute | solution.py:105
  308.7 3.8 %collective-permute-start.32 = (bf16[4,16,4096]{2,1,0:T(8,128)(2,1)S(1)}, bf16[4,16,4096]{2,1,0:T(8,128)(2,1)S(1)}, u32[]{:S(2)}, u32[]{:S(2)}) collective-permute-start(bf16[4,16,4096]{2,1,0:T(8,128)(2,1)S(1)} %add_convert_fusion.7), channel_id=1, source_target_pairs={{0,12},{4,0},{8,4},{12,8},{1,13},{5,1},{9,5},{13,9},{2,14},{6,2},{... | collective-permute-start | bytes 1572872 | tf_op jit(solution)/shard_map/ppermute | solution.py:105
  312.7 6.4 %collective-permute-done.32 = bf16[4,16,4096]{2,1,0:T(8,128)(2,1)S(1)} collective-permute-done((bf16[4,16,4096]{2,1,0:T(8,128)(2,1)S(1)}, bf16[4,16,4096]{2,1,0:T(8,128)(2,1)S(1)}, u32[]{:S(2)}, u32[]{:S(2)}) %collective-permute-start.32) | collective-permute-done | bytes 524320 | tf_op jit(solution)/shard_map/ppermute | solution.py:105
  319.3 3.8 %collective-permute-done.29 = bf16[4,16,4096]{2,1,0:T(8,128)(2,1)S(1)} collective-permute-done((bf16[4,16,4096]{2,1,0:T(8,128)(2,1)S(1)}, bf16[4,16,4096]{2,1,0:T(8,128)(2,1)S(1)}, u32[]{:S(2)}, u32[]{:S(2)}) %collective-permute-start.29) | collective-permute-done | bytes 524320 | tf_op jit(solution)/shard_map/ppermute | solution.py:105
  323.4 23.3 %all_to_all.17 = bf16[4,32,4096]{2,1,0:T(8,128)(2,1)S(1)} all-to-all(bf16[4,32,4096]{2,1,0:T(8,128)(2,1)S(1)} %pad_maximum_fusion.5), channel_id=1, replica_groups=mesh['sy'=4,'sz'=2,'sc'=2,'hx'=4,'hz'=4] {'hz'}, dimensions={0} | all-to-all | bytes 2097152 | tf_op jit(solution)/shard_map/all_to_all | solution.py:116
  346.8 0.8 add_convert_fusion.12
  (157 shorter events, 24.7 us)
Async XLA Ops:
  6.5 5.6 %copy-start.4 = (bf16[2,512,128]{2,1,0:T(8,128)(2,1)S(1)}, bf16[2,512,128]{2,1,0:T(8,128)(2,1)}, u32[]{:S(2)}) copy-start(bf16[2,512,128]{2,1,0:T(8,128)(2,1)} %param.26) | copy-start | bytes 786436
  6.5 89.2 %all-gather.3.cloned.1.call-start = ((), (), s32[]{:S(2)}) async-start(), calls=%async_computation.3 | async-start | bytes 4456448 | tf_op jit(solution)/shard_map/all_gather | solution.py:169
  7.3 176.4 %all-gather.5.cloned.1.call-start = ((), (), s32[]{:S(2)}) async-start(), calls=%async_computation.4 | async-start | bytes 4456448 | tf_op jit(solution)/shard_map/all_gather | solution.py:170
  13.2 5.6 %collective-permute-start.6 = (f32[8,64,128]{2,1,0:T(8,128)S(1)}, f32[8,64,128]{2,1,0:T(8,128)S(1)}, u32[]{:S(2)}, u32[]{:S(2)}) collective-permute-start(f32[8,64,128]{2,1,0:T(8,128)S(1)} %fusion.6), channel_id=1, source_target_pairs={{0,16},{32,48},{1,17},{33,49},{2,18},{34,50},{3,19},{35,51},{4,20}... | collective-permute-start | bytes 786440 | tf_op jit(solution)/shard_map/ppermute | solution.py:58
  16.6 4.6 %collective-permute-start = (f32[8]{0:T(128)S(1)}, f32[8]{0:T(128)S(1)}, u32[]{:S(2)}, u32[]{:S(2)}) collective-permute-start(f32[8]{0:T(128)S(1)} %fusion.61), channel_id=1, source_target_pairs={{0,16},{32,48},{1,17},{33,49},{2,18},{34,50},{3,19},{35,51},{4,20}... | collective-permute-start | bytes 104 | tf_op jit(solution)/shard_map/ppermute | solution.py:58
  18.8 9.7 %copy-start.3 = (bf16[512,512]{1,0:T(8,128)(2,1)S(1)}, bf16[512,512]{1,0:T(8,128)(2,1)}, u32[]{:S(2)}) copy-start(bf16[512,512]{1,0:T(8,128)(2,1)} %param.24) | copy-start | bytes 1572868
  18.9 3.6 %collective-permute-start.7 = (f32[8,64,128]{2,1,0:T(8,128)S(1)}, f32[8,64,128]{2,1,0:T(8,128)S(1)}, u32[]{:S(2)}, u32[]{:S(2)}) collective-permute-start(f32[8,64,128]{2,1,0:T(8,128)S(1)} %multiply_add_fusion.2), channel_id=1, source_target_pairs={{16,32},{17,33},{18,34},{19,35},{20,36},{21,37},{22,38},{23,39},{2... | collective-permute-start | bytes 786440 | tf_op jit(solution)/shard_map/ppermute | solution.py:58
  21.2 0.7 collective-permute-start.1
  21.9 1.4 collective-permute-start.2
  22.5 6.0 %copy-start.10 = (f32[8,64,128]{2,1,0:T(8,128)}, f32[8,64,128]{2,1,0:T(8,128)S(1)}, u32[]{:S(2)}) copy-start(f32[8,64,128]{2,1,0:T(8,128)S(1)} %collective-permute-done.7) | copy-start | bytes 786436
  22.6 2.7 collective-permute-start.8
  23.3 2.0 collective-permute-start.5
  23.9 3.5 collective-permute-start.4
  24.6 2.9 collective-permute-start.3
  25.4 2.1 collective-permute-start.11
  26.1 1.4 collective-permute-start.10
  26.8 0.8 collective-permute-start.9
  27.7 5.2 %collective-permute-start.12 = (f32[8,64,128]{2,1,0:T(8,128)S(1)}, f32[8,64,128]{2,1,0:T(8,128)S(1)}, u32[]{:S(2)}, u32[]{:S(2)}) collective-permute-start(f32[8,64,128]{2,1,0:T(8,128)S(1)} %select_add_fusion), channel_id=1, source_target_pairs={{48,16},{49,17},{50,18},{51,19},{52,20},{53,21},{54,22},{55,23},{5... | collective-permute-start | bytes 786440 | tf_op jit(solution)/shard_map/ppermute | solution.py:58
  28.8 5.4 %copy-start.6 = (f32[256,8,64]{0,2,1:T(8,128)S(1)}, f32[256,8,64]{0,2,1:T(8,128)}, u32[]{:S(2)}) copy-start(f32[256,8,64]{0,2,1:T(8,128)} %fusion.5) | copy-start | bytes 1572868
  32.0 41.5 %copy-start.11 = (f32[8,64,128]{2,1,0:T(8,128)S(1)}, f32[8,64,128]{2,1,0:T(8,128)}, u32[]{:S(2)}) copy-start(f32[8,64,128]{2,1,0:T(8,128)} %copy-done.10) | copy-start | bytes 786436
  32.0 41.5 %copy-start.14 = (f32[8]{0:T(128)S(1)}, f32[8]{0:T(128)}, u32[]{:S(2)}) copy-start(f32[8]{0:T(128)} %param.30) | copy-start | bytes 100
  32.0 2.9 collective-permute-start.13
  32.9 40.7 %copy-start.12 = (f32[8,64,128]{2,1,0:T(8,128)}, f32[8,64,128]{2,1,0:T(8,128)S(1)}, u32[]{:S(2)}) copy-start(f32[8,64,128]{2,1,0:T(8,128)S(1)} %collective-permute-done.12) | copy-start | bytes 786436
  32.9 40.7 %collective-permute-start.14 = (f32[8,64,128]{2,1,0:T(8,128)S(1)}, f32[8,64,128]{2,1,0:T(8,128)S(1)}, u32[]{:S(2)}, u32[]{:S(2)}) collective-permute-start(f32[8,64,128]{2,1,0:T(8,128)S(1)} %collective-permute-done.12), channel_id=1, source_target_pairs={{16,0},{17,1},{18,2},{19,3},{20,4},{21,5},{22,6},{23,7},{24,8},{25... | collective-permute-start | bytes 786440 | tf_op jit(solution)/shard_map/ppermute | solution.py:58
  74.3 21.4 %copy-start.16 = (f32[512]{0:T(512)S(1)}, f32[512]{0:T(512)}, u32[]{:S(2)}) copy-start(f32[512]{0:T(512)} %param.31) | copy-start | bytes 6148
  101.2 14.7 %collective-permute-start.18 = (bf16[4,16,4224]{2,1,0:T(8,128)(2,1)S(1)}, bf16[4,16,4224]{2,1,0:T(8,128)(2,1)S(1)}, u32[]{:S(2)}, u32[]{:S(2)}) collective-permute-start(bf16[4,16,4224]{2,1,0:T(8,128)(2,1)S(1)} %select_bitcast_fusion), channel_id=1, source_target_pairs={{0,12},{4,0},{8,4},{12,8},{1,13},{5,1},{9,5},{13,9},{2,14},{6,2},{... | collective-permute-start | bytes 1622024 | tf_op jit(solution)/shard_map/ppermute | solution.py:105
  104.0 15.8 %collective-permute-start.15 = (bf16[4,16,4224]{2,1,0:T(8,128)(2,1)S(1)}, bf16[4,16,4224]{2,1,0:T(8,128)(2,1)S(1)}, u32[]{:S(2)}, u32[]{:S(2)}) collective-permute-start(bf16[4,16,4224]{2,1,0:T(8,128)(2,1)S(1)} %select_bitcast_fusion.1), channel_id=1, source_target_pairs={{0,4},{4,8},{8,12},{12,0},{1,5},{5,9},{9,13},{13,1},{2,6},{6,10},{... | collective-permute-start | bytes 1622024 | tf_op jit(solution)/shard_map/ppermute | solution.py:105
  116.1 14.9 %collective-permute-start.19 = (bf16[4,16,4224]{2,1,0:T(8,128)(2,1)S(1)}, bf16[4,16,4224]{2,1,0:T(8,128)(2,1)S(1)}, u32[]{:S(2)}, u32[]{:S(2)}) collective-permute-start(bf16[4,16,4224]{2,1,0:T(8,128)(2,1)S(1)} %add_convert_fusion.2), channel_id=1, source_target_pairs={{0,12},{4,0},{8,4},{12,8},{1,13},{5,1},{9,5},{13,9},{2,14},{6,2},{... | collective-permute-start | bytes 1622024 | tf_op jit(solution)/shard_map/ppermute | solution.py:105
  120.0 14.9 %collective-permute-start.16 = (bf16[4,16,4224]{2,1,0:T(8,128)(2,1)S(1)}, bf16[4,16,4224]{2,1,0:T(8,128)(2,1)S(1)}, u32[]{:S(2)}, u32[]{:S(2)}) collective-permute-start(bf16[4,16,4224]{2,1,0:T(8,128)(2,1)S(1)} %add_convert_fusion.5), channel_id=1, source_target_pairs={{0,4},{4,8},{8,12},{12,0},{1,5},{5,9},{9,13},{13,1},{2,6},{6,10},{... | collective-permute-start | bytes 1622024 | tf_op jit(solution)/shard_map/ppermute | solution.py:105
  131.1 14.0 %collective-permute-start.20 = (bf16[4,16,4224]{2,1,0:T(8,128)(2,1)S(1)}, bf16[4,16,4224]{2,1,0:T(8,128)(2,1)S(1)}, u32[]{:S(2)}, u32[]{:S(2)}) collective-permute-start(bf16[4,16,4224]{2,1,0:T(8,128)(2,1)S(1)} %add_convert_fusion.1), channel_id=1, source_target_pairs={{0,12},{4,0},{8,4},{12,8},{1,13},{5,1},{9,5},{13,9},{2,14},{6,2},{... | collective-permute-start | bytes 1622024 | tf_op jit(solution)/shard_map/ppermute | solution.py:105
  135.1 13.7 %collective-permute-start.17 = (bf16[4,16,4224]{2,1,0:T(8,128)(2,1)S(1)}, bf16[4,16,4224]{2,1,0:T(8,128)(2,1)S(1)}, u32[]{:S(2)}, u32[]{:S(2)}) collective-permute-start(bf16[4,16,4224]{2,1,0:T(8,128)(2,1)S(1)} %add_convert_fusion.4), channel_id=1, source_target_pairs={{0,4},{4,8},{8,12},{12,0},{1,5},{5,9},{9,13},{13,1},{2,6},{6,10},{... | collective-permute-start | bytes 1622024 | tf_op jit(solution)/shard_map/ppermute | solution.py:105
  149.1 34.8 %copy-start.2 = (bf16[32,4096]{1,0:T(8,128)(2,1)S(1)}, bf16[32,4096]{1,0:T(8,128)(2,1)}, u32[]{:S(2)}) copy-start(bf16[32,4096]{1,0:T(8,128)(2,1)} %param.33) | copy-start | bytes 786436
  149.1 35.0 %copy-start.13 = (f32[4096]{0:T(1024)S(1)}, f32[4096]{0:T(1024)}, u32[]{:S(2)}) copy-start(f32[4096]{0:T(1024)} %param.34) | copy-start | bytes 49156
  213.7 13.8 %collective-permute-start.24 = (bf16[64,4096]{1,0:T(8,128)(2,1)S(1)}, bf16[64,4096]{1,0:T(8,128)(2,1)S(1)}, u32[]{:S(2)}, u32[]{:S(2)}) collective-permute-start(bf16[64,4096]{1,0:T(8,128)(2,1)S(1)} %bitcast.131), channel_id=1, source_target_pairs={{0,12},{4,0},{8,4},{12,8},{1,13},{5,1},{9,5},{13,9},{2,14},{6,2},{... | collective-permute-start | bytes 1572872 | tf_op jit(solution)/shard_map/ppermute | solution.py:130
  217.0 14.2 %collective-permute-start.21 = (bf16[64,4096]{1,0:T(8,128)(2,1)S(1)}, bf16[64,4096]{1,0:T(8,128)(2,1)S(1)}, u32[]{:S(2)}, u32[]{:S(2)}) collective-permute-start(bf16[64,4096]{1,0:T(8,128)(2,1)S(1)} %bitcast.129), channel_id=1, source_target_pairs={{0,4},{4,8},{8,12},{12,0},{1,5},{5,9},{9,13},{13,1},{2,6},{6,10},{... | collective-permute-start | bytes 1572872 | tf_op jit(solution)/shard_map/ppermute | solution.py:130
  227.5 13.3 %collective-permute-start.25 = (bf16[64,4096]{1,0:T(8,128)(2,1)S(1)}, bf16[64,4096]{1,0:T(8,128)(2,1)S(1)}, u32[]{:S(2)}, u32[]{:S(2)}) collective-permute-start(bf16[64,4096]{1,0:T(8,128)(2,1)S(1)} %collective-permute-done.24), channel_id=1, source_target_pairs={{0,12},{4,0},{8,4},{12,8},{1,13},{5,1},{9,5},{13,9},{2,14},{6,2},{... | collective-permute-start | bytes 1572872 | tf_op jit(solution)/shard_map/ppermute | solution.py:130
  231.2 22.1 %copy-start.7 = (bf16[64,4096]{1,0:T(8,128)(2,1)}, bf16[64,4096]{1,0:T(8,128)(2,1)S(1)}, u32[]{:S(2)}) copy-start(bf16[64,4096]{1,0:T(8,128)(2,1)S(1)} %collective-permute-done.21) | copy-start | bytes 1572868
  231.2 13.4 %collective-permute-start.22 = (bf16[64,4096]{1,0:T(8,128)(2,1)S(1)}, bf16[64,4096]{1,0:T(8,128)(2,1)}, u32[]{:S(2)}, u32[]{:S(2)}) collective-permute-start(bf16[64,4096]{1,0:T(8,128)(2,1)S(1)} %collective-permute-done.21), channel_id=1, source_target_pairs={{0,4},{4,8},{8,12},{12,0},{1,5},{5,9},{9,13},{13,1},{2,6},{6,10},{... | collective-permute-start | bytes 1572872 | tf_op jit(solution)/shard_map/ppermute | solution.py:130
  240.8 12.5 %collective-permute-start.26 = (bf16[64,4096]{1,0:T(8,128)(2,1)S(1)}, bf16[64,4096]{1,0:T(8,128)(2,1)S(1)}, u32[]{:S(2)}, u32[]{:S(2)}) collective-permute-start(bf16[64,4096]{1,0:T(8,128)(2,1)S(1)} %collective-permute-done.25), channel_id=1, source_target_pairs={{0,12},{4,0},{8,4},{12,8},{1,13},{5,1},{9,5},{13,9},{2,14},{6,2},{... | collective-permute-start | bytes 1572872 | tf_op jit(solution)/shard_map/ppermute | solution.py:130
  244.6 14.2 %collective-permute-start.23 = (bf16[64,4096]{1,0:T(8,128)(2,1)}, bf16[64,4096]{1,0:T(8,128)(2,1)}, u32[]{:S(2)}, u32[]{:S(2)}) collective-permute-start(bf16[64,4096]{1,0:T(8,128)(2,1)} %collective-permute-done.22), channel_id=1, source_target_pairs={{0,4},{4,8},{8,12},{12,0},{1,5},{5,9},{9,13},{13,1},{2,6},{6,10},{... | collective-permute-start | bytes 1572872 | tf_op jit(solution)/shard_map/ppermute | solution.py:130
  255.5 3.2 copy-start.8
  264.5 3.7 %copy-start.15 = (bf16[4096,512]{1,0:T(8,128)(2,1)S(1)}, bf16[4096,512]{1,0:T(8,128)(2,1)}, u32[]{:S(2)}) copy-start(bf16[4096,512]{1,0:T(8,128)(2,1)} %param.35) | copy-start | bytes 12582916
  284.5 11.9 %collective-permute-start.30 = (bf16[4,16,4096]{2,1,0:T(8,128)(2,1)S(1)}, bf16[4,16,4096]{2,1,0:T(8,128)(2,1)S(1)}, u32[]{:S(2)}, u32[]{:S(2)}) collective-permute-start(bf16[4,16,4096]{2,1,0:T(8,128)(2,1)S(1)} %select_bitcast_fusion.2), channel_id=1, source_target_pairs={{0,12},{4,0},{8,4},{12,8},{1,13},{5,1},{9,5},{13,9},{2,14},{6,2},{... | collective-permute-start | bytes 1572872 | tf_op jit(solution)/shard_map/ppermute | solution.py:105
  288.4 12.0 %collective-permute-start.27 = (bf16[4,16,4096]{2,1,0:T(8,128)(2,1)S(1)}, bf16[4,16,4096]{2,1,0:T(8,128)(2,1)S(1)}, u32[]{:S(2)}, u32[]{:S(2)}) collective-permute-start(bf16[4,16,4096]{2,1,0:T(8,128)(2,1)S(1)} %select_bitcast_fusion.3), channel_id=1, source_target_pairs={{0,4},{4,8},{8,12},{12,0},{1,5},{5,9},{9,13},{13,1},{2,6},{6,10},{... | collective-permute-start | bytes 1572872 | tf_op jit(solution)/shard_map/ppermute | solution.py:105
  296.6 11.9 %collective-permute-start.31 = (bf16[4,16,4096]{2,1,0:T(8,128)(2,1)S(1)}, bf16[4,16,4096]{2,1,0:T(8,128)(2,1)S(1)}, u32[]{:S(2)}, u32[]{:S(2)}) collective-permute-start(bf16[4,16,4096]{2,1,0:T(8,128)(2,1)S(1)} %add_convert_fusion.8), channel_id=1, source_target_pairs={{0,12},{4,0},{8,4},{12,8},{1,13},{5,1},{9,5},{13,9},{2,14},{6,2},{... | collective-permute-start | bytes 1572872 | tf_op jit(solution)/shard_map/ppermute | solution.py:105
  300.6 11.9 %collective-permute-start.28 = (bf16[4,16,4096]{2,1,0:T(8,128)(2,1)S(1)}, bf16[4,16,4096]{2,1,0:T(8,128)(2,1)S(1)}, u32[]{:S(2)}, u32[]{:S(2)}) collective-permute-start(bf16[4,16,4096]{2,1,0:T(8,128)(2,1)S(1)} %add_convert_fusion.11), channel_id=1, source_target_pairs={{0,4},{4,8},{8,12},{12,0},{1,5},{5,9},{9,13},{13,1},{2,6},{6,10},{... | collective-permute-start | bytes 1572872 | tf_op jit(solution)/shard_map/ppermute | solution.py:105
  308.7 10.5 %collective-permute-start.32 = (bf16[4,16,4096]{2,1,0:T(8,128)(2,1)S(1)}, bf16[4,16,4096]{2,1,0:T(8,128)(2,1)S(1)}, u32[]{:S(2)}, u32[]{:S(2)}) collective-permute-start(bf16[4,16,4096]{2,1,0:T(8,128)(2,1)S(1)} %add_convert_fusion.7), channel_id=1, source_target_pairs={{0,12},{4,0},{8,4},{12,8},{1,13},{5,1},{9,5},{13,9},{2,14},{6,2},{... | collective-permute-start | bytes 1572872 | tf_op jit(solution)/shard_map/ppermute | solution.py:105
  312.6 10.5 %collective-permute-start.29 = (bf16[4,16,4096]{2,1,0:T(8,128)(2,1)S(1)}, bf16[4,16,4096]{2,1,0:T(8,128)(2,1)S(1)}, u32[]{:S(2)}, u32[]{:S(2)}) collective-permute-start(bf16[4,16,4096]{2,1,0:T(8,128)(2,1)S(1)} %add_convert_fusion.10), channel_id=1, source_target_pairs={{0,4},{4,8},{8,12},{12,0},{1,5},{5,9},{9,13},{13,1},{2,6},{6,10},{... | collective-permute-start | bytes 1572872 | tf_op jit(solution)/shard_map/ppermute | solution.py:105
  (4 other events, 6.4 us)
Sparse Core Ops, SparseCore 0:
  9.9 85.8 all-gather.2
  98.3 78.7 all-gather.4
